TPU v7x, 512 devices: a whole 4x4x16 slice. The times are simulated.
512 devices in a mesh: dp: 32 (over z, core), expert: 16 (over y, x).
Axes of the slice: x: 4, y: 4, z: 16, core: 2. Of those that a mesh axis runs over, the one named last changes fastest.
Arguments:
- stream: bfloat16 [8192, 2304], P(('dp', 'expert')), may hold values from -6 to 6
- queries: bfloat16 [8192, 2048], P('dp', 'expert'), may hold values from -200 to 200
- key_pages: bfloat16 [1024, 128, 2048], P('dp', None, 'expert'), may hold values from -10.5 to 10.5
- value_pages: bfloat16 [1024, 128, 2048], P('dp', None, 'expert'), may hold values from -6 to 6
- query_counts: int32 [32, 16], P('dp'), may hold values from 1 to 32, 256 in all within a row
- cached_lengths: int32 [32, 16], P('dp'), may hold values from 0 to 224, as said below
- page_tables: int32 [32, 32], P('dp'), may hold values from 0 to 31, each once within a row
- out_proj: bfloat16 [2048, 2304], P('expert'), may hold values from -0.29882812 to 0.29882812
- moe_gain: float32 [2304], replicated, may hold values from 0.1 to 1.9
- router: bfloat16 [2304, 8], replicated, may hold values from -0.125 to 0.125
- gate_proj: bfloat16 [16, 2048, 2304], P('expert', 'dp'), may hold values from -0.125 to 0.125
- up_proj: bfloat16 [16, 2048, 2304], P('expert', 'dp'), may hold values from -0.125 to 0.125
- down_proj: bfloat16 [16, 2048, 2304], P('expert', 'dp'), may hold values from -0.09375 to 0.09375
- routes: int32 [8192, 2], P(('dp', 'expert')), may hold values from 0 to 7, all different within a row; in each aligned block of 16 rows (0 to 15, 16 to 31, ...) at most 6 rows name the same one
- next_gain: float32 [2304], replicated, may hold values from 0.1 to 1.9
Outputs:
- resid_out: bfloat16 [8192, 2304], P(('dp', 'expert'))
- normed_out: bfloat16 [8192, 2304], P(('dp', 'expert'))
Inputs may be any that keep to these rules, and one draw needn't show every extreme that they name: `query_counts`: each group's counts sum to 256, and one of them is 32. `cached_lengths`: in each group one sequence has no cached tokens and another has 224. `page_tables`: each group's row is a permutation of its 32 pages; sequence s uses entries s * 2 to s * 2 + 1. `routes`: each row names two different experts; in each device's aligned block of 16 rows no expert is named by more than 6 rows.
All inputs are finite; a program needn't handle non-finite values.
Results may differ from a plain program's by a relative error of at most 0.014.
Values may be sent and summed in bfloat16 or wider, within the bound.
No kernel may reach another device: no remote copies, remote signals or barrier semaphores. Data moves between devices by JAX's collectives and lax.ppermute only.
A program may use at most 64 MiB of HBM per device.

v0:
```python
import jax
import jax.numpy as jnp
from jax import lax
from jax.sharding import PartitionSpec as P

HD = 64
QMAX = 32


eps = 1e-06


def rms_scale(values, gain):
    mean_square = jnp.mean(values * values, axis=-1, keepdims=True)
    return values * lax.rsqrt(mean_square + eps) * gain


def paged_attention(
    group_queries, group_keys, group_values, counts, cached, page_table, head_count
):
    row_count, lane_count = group_queries.shape
    head_size = lane_count // head_count
    seq_count = counts.shape[0]
    page_count = page_table.shape[0] // seq_count
    page_len = group_keys.shape[1]
    starts = jnp.cumsum(counts) - counts
    slot_ids = jnp.arange(QMAX, dtype=jnp.int32)
    row_index = jnp.clip(starts[:, None] + slot_ids[None, :], 0, row_count - 1)
    picked = group_queries[row_index].reshape(seq_count, QMAX, head_count, head_size)
    page_ids = page_table.reshape(seq_count, page_count)
    seq_keys = group_keys[page_ids].reshape(seq_count, page_count * page_len, head_count, head_size)
    seq_values = group_values[page_ids].reshape(
        seq_count, page_count * page_len, head_count, head_size
    )
    scores = jnp.einsum(
        "sqhd,skhd->shqk", picked, seq_keys, preferred_element_type=jnp.float32
    ) * head_size ** (-0.5)
    key_position = jnp.arange(page_count * page_len, dtype=jnp.int32)
    last_key = cached[:, None] + slot_ids[None, :]
    allowed = key_position[None, None, :] <= last_key[:, :, None]
    scores = jnp.where(allowed[:, None, :, :], scores, -1e30)
    row_max = jnp.max(scores, axis=-1, keepdims=True)
    weights = jnp.exp(scores - row_max)
    row_total = jnp.sum(weights, axis=-1, keepdims=True)
    probabilities = weights.astype(jnp.bfloat16)
    attended = (
        jnp.einsum("shqk,skhd->shqd", probabilities, seq_values, preferred_element_type=jnp.float32)
        / row_total
    )
    attended = (
        attended.astype(jnp.bfloat16).transpose(0, 2, 1, 3).reshape(seq_count, QMAX, lane_count)
    )
    row_ids = jnp.arange(row_count, dtype=jnp.int32)
    owning = jnp.sum((starts[None, :] <= row_ids[:, None]).astype(jnp.int32), axis=1) - 1
    offset = row_ids - starts[owning]
    return attended[owning, offset]


def on_device(
    stream,
    queries,
    key_pages,
    value_pages,
    query_counts,
    cached_lengths,
    page_tables,
    out_proj,
    moe_gain,
    router,
    gate_proj,
    up_proj,
    down_proj,
    routes,
    next_gain,
):
    held = lax.all_gather(
        jnp.stack([gate_proj[0], up_proj[0], down_proj[0]]), "zz", axis=1, tiled=True
    )
    gate_held = held[0]
    up_held = held[1]
    down_held = held[2]
    heads_here = queries.shape[1] // HD
    attended = paged_attention(
        queries,
        key_pages,
        value_pages,
        query_counts[0],
        cached_lengths[0],
        page_tables[0],
        heads_here,
    )
    own_rows = stream.shape[0]
    partial_proj = jnp.dot(attended, out_proj, preferred_element_type=jnp.float32).astype(
        jnp.bfloat16
    )
    expert_count = lax.axis_size("expert")
    gathered_proj = lax.all_to_all(
        partial_proj.reshape(expert_count, own_rows, partial_proj.shape[1]),
        "expert",
        split_axis=0,
        concat_axis=0,
        tiled=True,
    )
    projected = jnp.sum(gathered_proj.astype(jnp.float32), axis=0)
    hidden = stream.astype(jnp.float32) + projected
    normed = rms_scale(hidden, moe_gain).astype(jnp.bfloat16)
    logits = jnp.dot(normed, router, preferred_element_type=jnp.float32)
    chosen = jnp.take_along_axis(logits, routes, axis=1)
    first_share = jax.nn.sigmoid(chosen[:, 0] - chosen[:, 1])
    shares = jnp.stack([first_share, 1.0 - first_share], axis=1)
    expert_devs = lax.axis_size("expert")
    experts_all = expert_devs // 2
    model_width = stream.shape[1]
    capacity = max(2, min(own_rows, 3 * own_rows // experts_all))
    flat_routes = routes.reshape(-1)
    onehot = (flat_routes[:, None] == jnp.arange(experts_all, dtype=jnp.int32)[None, :]).astype(
        jnp.int32
    )
    earlier = jnp.cumsum(onehot, axis=0) - onehot
    position = jnp.sum(earlier * onehot, axis=1)
    target = flat_routes * capacity + position
    placing = (
        jnp.arange(experts_all * capacity, dtype=jnp.int32)[:, None] == target[None, :]
    ).astype(jnp.bfloat16)
    repeated = jnp.repeat(normed, 2, axis=0)
    packed = jnp.dot(placing, repeated, preferred_element_type=jnp.float32).astype(jnp.bfloat16)
    packed = packed.reshape(experts_all, 1, capacity, model_width)
    outgoing = jnp.broadcast_to(packed, (experts_all, 2, capacity, model_width))
    arrived = lax.all_to_all(
        outgoing.reshape(expert_devs * capacity, model_width),
        "expert",
        split_axis=0,
        concat_axis=0,
        tiled=True,
    )
    n_zz = lax.axis_size("zz")
    n_h = lax.axis_size("h")
    n_c = lax.axis_size("c")
    slot_total = arrived.shape[0]
    piece = slot_total // n_zz
    sent = lax.all_to_all(
        arrived.reshape(n_zz, piece, model_width), "zz", split_axis=0, concat_axis=0, tiled=True
    )
    over_h = lax.all_gather(sent, "h")
    rows_here = lax.all_gather(over_h, "c")
    flat_rows = rows_here.reshape(n_c * n_h * n_zz * piece, model_width)
    gate_val = lax.dot_general(
        flat_rows, gate_held, (((1,), (1,)), ((), ())), preferred_element_type=jnp.float32
    )
    up_val = lax.dot_general(
        flat_rows, up_held, (((1,), (1,)), ((), ())), preferred_element_type=jnp.float32
    )
    activated = (jax.nn.silu(gate_val) * up_val).astype(jnp.bfloat16)
    partial = jnp.dot(activated, down_held, preferred_element_type=jnp.float32).astype(jnp.bfloat16)
    partial = partial.reshape(n_c, n_h, n_zz, piece, model_width)
    back_c = lax.all_to_all(partial, "c", split_axis=0, concat_axis=0, tiled=True)
    back_h = lax.all_to_all(back_c, "h", split_axis=1, concat_axis=1, tiled=True)
    summed = jnp.sum(back_h.astype(jnp.float32), axis=(0, 1)).astype(jnp.bfloat16)
    own_slots = lax.all_to_all(summed, "zz", split_axis=0, concat_axis=0, tiled=True)
    returned = lax.all_to_all(
        own_slots.reshape(slot_total, model_width), "expert", split_axis=0, concat_axis=0, tiled=True
    ).astype(jnp.float32)
    arranged = returned.reshape(experts_all, 2, capacity, model_width)
    expert_result = jnp.sum(arranged, axis=1)
    per_slot = expert_result.reshape(experts_all * capacity, model_width)[target]
    expert_mix = jnp.sum(per_slot.reshape(own_rows, 2, model_width) * shares[:, :, None], axis=1)
    combined = hidden + expert_mix
    return (combined.astype(jnp.bfloat16), rms_scale(combined, next_gain).astype(jnp.bfloat16))


def solution(mesh):
    n_dp = mesh.shape["dp"]
    n_chips = n_dp // 2
    split = jax.sharding.Mesh(
        mesh.devices.reshape(n_chips // 4, 4, 2, mesh.shape["expert"]), ("zz", "h", "c", "expert")
    )
    dp = ("zz", "h", "c")
    placed = (
        P((*dp, "expert"), None),
        P(dp, "expert"),
        P(dp, None, "expert"),
        P(dp, None, "expert"),
        P(dp, None),
        P(dp, None),
        P(dp, None),
        P("expert", None),
        P(),
        P(),
        P("expert", dp, None),
        P("expert", dp, None),
        P("expert", dp, None),
        P((*dp, "expert"), None),
        P(),
    )

    return jax.shard_map(
        on_device,
        mesh=split,
        in_specs=placed,
        out_specs=(P((*dp, "expert"), None), P((*dp, "expert"), None)),
        check_vma=False,
    )
```

profile of v0, /device:TPU:1, one launch (start us, length us, event | category | flops | bytes accessed | tf_op | source)
XLA Modules:
  0.0 500.5 jit_solution(1844362708287082595)
XLA Ops:
  7.2 0.8 copy.103
  8.2 0.7 bitcast_subtract_fusion.1
  8.8 0.7 fusion.39
  9.5 0.7 fusion.42
  10.3 0.5 broadcast.418
  10.8 1.3 reduce.24
  12.3 0.7 iota_add_fusion
  13.2 4.4 compare_select_fusion.4
  17.6 5.6 %select_select_fusion = s32[256]{0:T(256)S(1)} fusion(pred[256]{0:T(512)(128)(4,1)S(1)} %get-tuple-element.10, pred[256]{0:T(512)(128)(4,1)S(1)} %get-tuple-element.9, pred[256]{0:T(512)(128)(4,1)S(1)} %get-tuple-element.8, pred[256]{0:T(512)(128)(4,1)S(1)} %get-tuple-element.7, pred[256]{0:T(512)(128)(4,1)S(1)} %get-tuple-element.6, ...), kind=kLoop, calls=%fused_computation.85 | loop fusion | flops 2304 | bytes 4388 | tf_op jit(solution)/shard_map/gather | solution.py:55
  23.2 0.8 iota_compare_fusion
  24.0 1.9 gather_fusion
  26.1 0.7 gather_fusion.2
  26.9 2.0 gather_fusion.1
  28.8 1.8 reshape.422
  30.7 1.9 reshape.423
  32.6 2.6 fusion.43
  35.2 0.4 fusion.21
  35.6 0.6 fusion.17
  36.2 0.2 copy.109
  36.6 1.7 gather_fusion.3
  38.3 1.5 convolution_convert_fusion.1
  39.8 7.7 %all-to-all-start = ((bf16[16,16,2304]{2,1,0:T(8,128)(2,1)}), bf16[16,16,2304]{2,1,0:T(8,128)(2,1)S(1)}, u32[]{:S(2)}, u32[]{:S(2)}) async-start(bf16[16,16,2304]{2,1,0:T(8,128)(2,1)} %bitcast.27), calls=%async_computation | async-start | bytes 2359296 | tf_op jit(solution)/shard_map/all_to_all | solution.py:97
  47.8 0.2 select_reduce_fusion
  48.0 15.5 %all-to-all-done = bf16[16,16,2304]{2,1,0:T(8,128)(2,1)S(1)} async-done(((bf16[16,16,2304]{2,1,0:T(8,128)(2,1)}), bf16[16,16,2304]{2,1,0:T(8,128)(2,1)S(1)}, u32[]{:S(2)}, u32[]{:S(2)}) %all-to-all-start) | async-done | bytes 1179680 | tf_op jit(solution)/shard_map/all_to_all | solution.py:97
  63.6 0.2 convert_reduce_fusion
  64.1 0.2 convolution_convert_fusion.2
  64.5 13.9 %all_to_all.43 = bf16[16,6,2304]{2,1,0:T(8,128)(2,1)S(1)} all-to-all(bf16[16,6,2304]{2,1,0:T(8,128)(2,1)S(1)} %bitcast.80), channel_id=1, replica_groups=mesh['zz'=4,'h'=4,'c'=2,'expert'=16] {'expert'}, dimensions={0} | all-to-all | bytes 884736 | tf_op jit(solution)/shard_map/all_to_all | solution.py:129
  78.5 40.3 %all_to_all.44 = bf16[4,24,2304]{2,1,0:T(8,128)(2,1)} all-to-all(bf16[4,24,2304]{2,1,0:T(8,128)(2,1)S(1)} %reshape.289), channel_id=1, replica_groups=mesh['zz'=4,'h'=4,'c'=2,'expert'=16] {'zz'}, dimensions={0} | all-to-all | bytes 884736 | tf_op jit(solution)/shard_map/all_to_all | solution.py:141
  118.9 1.1 pad_maximum_fusion
  120.1 45.0 %all-gather.8.cloned.1.call-done = bf16[16,24,2304]{2,1,0:T(8,128)(2,1)} async-done(((bf16[4,24,2304]{2,1,0:T(8,128)(2,1)}), bf16[16,24,2304]{2,1,0:T(8,128)(2,1)}) %all-gather.8.cloned.1.call-update) | async-done | bytes 1769488 | tf_op jit(solution)/shard_map/all_gather | solution.py:144
  165.1 144.1 %all-gather.6.cloned.1.call-done = bf16[3,256,2304]{2,1,0:T(8,128)(2,1)} async-done(((bf16[3,64,2304]{2,1,0:T(8,128)(2,1)}), bf16[3,256,2304]{2,1,0:T(8,128)(2,1)}) %all-gather.6.cloned.1.call-update) | async-done | bytes 3538960 | tf_op jit(solution)/shard_map/all_gather | solution.py:76
  309.2 23.0 %all-gather.10.cloned.1.call-done = bf16[8,4,24,2304]{3,2,1,0:T(8,128)(2,1)} async-done(((bf16[4,4,24,2304]{3,2,1,0:T(8,128)(2,1)}), bf16[8,4,24,2304]{3,2,1,0:T(8,128)(2,1)}) %all-gather.10.cloned.1.call-update) | async-done | bytes 3538960 | tf_op jit(solution)/shard_map/all_gather | solution.py:145
  332.2 3.4 fusion.20
  335.7 8.3 %convolution_convert_fusion = bf16[768,2304]{1,0:T(8,128)(2,1)} fusion(bf16[3,256,2304]{2,1,0:T(8,128)(2,1)} %all-gather.6.cloned.1.call-done, bf16[768,2304]{1,0:T(8,128)(2,1)} %bitcast.90, f32[768,256]{1,0:T(8,128)S(1)} %fusion.20), kind=kOutput, calls=%fused_computation.6 | convolution fusion | flops 1814888448 | bytes 10223616 | tf_op jit(solution)/shard_map/dot_general | solution.py:154
  343.9 7.7 %all_to_all.45 = bf16[2,4,4,24,2304]{4,3,2,1,0:T(8,128)(2,1)S(1)} all-to-all(bf16[2,4,4,24,2304]{4,3,2,1,0:T(8,128)(2,1)} %bitcast.79), channel_id=1, replica_groups=mesh['zz'=4,'h'=4,'c'=2,'expert'=16] {'c'}, dimensions={0} | all-to-all | bytes 7077888 | tf_op jit(solution)/shard_map/all_to_all | solution.py:156
  351.7 0.2 copy.111
  351.9 82.1 %all_to_all.46 = bf16[2,4,4,24,2304]{4,3,2,0,1:T(8,128)(2,1)} all-to-all(bf16[2,4,4,24,2304]{4,3,2,0,1:T(8,128)(2,1)S(1)} %copy.111), channel_id=1, replica_groups=mesh['zz'=4,'h'=4,'c'=2,'expert'=16] {'h'}, dimensions={1} | all-to-all | bytes 7077888 | tf_op jit(solution)/shard_map/all_to_all | solution.py:157
  434.0 3.4 reduce_sum.91
  437.4 11.0 %all-to-all-start.5 = ((bf16[4,24,2304]{2,1,0:T(8,128)(2,1)}), bf16[4,24,2304]{2,1,0:T(8,128)(2,1)S(1)}, u32[]{:S(2)}, u32[]{:S(2)}) async-start(bf16[4,24,2304]{2,1,0:T(8,128)(2,1)} %reduce_sum.91), calls=%async_computation.5 | async-start | bytes 884736 | tf_op jit(solution)/shard_map/all_to_all | solution.py:159
  448.9 0.7 gather_fusion.5
  449.8 23.0 %all-to-all-done.5 = bf16[4,24,2304]{2,1,0:T(8,128)(2,1)S(1)} async-done(((bf16[4,24,2304]{2,1,0:T(8,128)(2,1)}), bf16[4,24,2304]{2,1,0:T(8,128)(2,1)S(1)}, u32[]{:S(2)}, u32[]{:S(2)}) %all-to-all-start.5) | async-done | bytes 442400 | tf_op jit(solution)/shard_map/all_to_all | solution.py:159
  472.8 1.0 all_to_all.34
  473.8 6.5 %all-to-all-start.6 = ((bf16[16,6,2304]{2,1,0:T(8,128)(2,1)}), bf16[16,6,2304]{2,1,0:T(8,128)(2,1)S(1)}, u32[]{:S(2)}, u32[]{:S(2)}) async-start(bf16[16,6,2304]{2,1,0:T(8,128)(2,1)} %all_to_all.34), calls=%async_computation.6 | async-start | bytes 1179648 | tf_op jit(solution)/shard_map/all_to_all | solution.py:160
  480.4 11.1 %all-to-all-done.6 = bf16[16,6,2304]{2,1,0:T(8,128)(2,1)S(1)} async-done(((bf16[16,6,2304]{2,1,0:T(8,128)(2,1)}), bf16[16,6,2304]{2,1,0:T(8,128)(2,1)S(1)}, u32[]{:S(2)}, u32[]{:S(2)}) %all-to-all-start.6) | async-done | bytes 442400 | tf_op jit(solution)/shard_map/all_to_all | solution.py:160
  491.8 0.7 gather_fusion.4
  492.4 0.2 reshape.293
  492.6 0.4 multiply_reduce_fusion
  493.2 0.7 multiply_convert_fusion
  (77 shorter events, 3.2 us)
Async XLA Ops:
  7.2 18.9 %copy-start = (bf16[32,128,128]{2,1,0:T(8,128)(2,1)S(1)}, bf16[32,128,128]{2,1,0:T(8,128)(2,1)}, u32[]{:S(2)}) copy-start(bf16[32,128,128]{2,1,0:T(8,128)(2,1)} %param.18) | copy-start | bytes 3145732
  28.8 3.7 copy-start.7
  32.6 3.1 copy-start.1
  35.6 2.6 copy-start.3
  36.6 10.9 %copy-start.11 = (s32[16,2]{0,1:T(2,128)S(1)}, s32[16,2]{0,1:T(2,128)}, u32[]{:S(2)}) copy-start(s32[16,2]{0,1:T(2,128)} %param.28) | copy-start | bytes 388
  38.3 25.5 %copy-start.2 = (bf16[16,2304]{1,0:T(8,128)(2,1)S(1)}, bf16[16,2304]{1,0:T(8,128)(2,1)}, u32[]{:S(2)}) copy-start(bf16[16,2304]{1,0:T(8,128)(2,1)} %param.15) | copy-start | bytes 221188
  39.8 24.1 %copy-start.9 = (f32[2304]{0:T(1024)S(1)}, f32[2304]{0:T(1024)}, u32[]{:S(2)}) copy-start(f32[2304]{0:T(1024)} %param.23) | copy-start | bytes 27652
  39.8 23.8 %all-to-all-start = ((bf16[16,16,2304]{2,1,0:T(8,128)(2,1)}), bf16[16,16,2304]{2,1,0:T(8,128)(2,1)S(1)}, u32[]{:S(2)}, u32[]{:S(2)}) async-start(bf16[16,16,2304]{2,1,0:T(8,128)(2,1)} %bitcast.27), calls=%async_computation | async-start | bytes 2359296 | tf_op jit(solution)/shard_map/all_to_all | solution.py:97
  47.5 117.6 %all-gather.8.cloned.1.call-start = ((), (), s32[]{:S(2)}) async-start(), calls=%async_computation.8 | async-start | bytes 2211840 | tf_op jit(solution)/shard_map/all_gather | solution.py:144
  64.3 54.6 %copy-start.4 = (bf16[1,64,2304]{2,1,0:T(8,128)(2,1)S(1)}, bf16[1,64,2304]{2,1,0:T(8,128)(2,1)}, u32[]{:S(2)}) copy-start(bf16[1,64,2304]{2,1,0:T(8,128)(2,1)} %param.27) | copy-start | bytes 884740
  64.3 54.6 %copy-start.5 = (bf16[1,64,2304]{2,1,0:T(8,128)(2,1)S(1)}, bf16[1,64,2304]{2,1,0:T(8,128)(2,1)}, u32[]{:S(2)}) copy-start(bf16[1,64,2304]{2,1,0:T(8,128)(2,1)} %param.26) | copy-start | bytes 884740
  64.4 54.6 %copy-start.6 = (bf16[1,64,2304]{2,1,0:T(8,128)(2,1)S(1)}, bf16[1,64,2304]{2,1,0:T(8,128)(2,1)}, u32[]{:S(2)}) copy-start(bf16[1,64,2304]{2,1,0:T(8,128)(2,1)} %param.25) | copy-start | bytes 884740
  118.9 190.3 %all-gather.6.cloned.1.call-start = ((), (), s32[]{:S(2)}) async-start(), calls=%async_computation.7 | async-start | bytes 4423680 | tf_op jit(solution)/shard_map/all_gather | solution.py:76
  120.1 212.1 %all-gather.10.cloned.1.call-start = ((), (), s32[]{:S(2)}) async-start(), calls=%async_computation.9 | async-start | bytes 5308416 | tf_op jit(solution)/shard_map/all_gather | solution.py:145
  434.0 14.8 %copy-start.8 = (bf16[2304,8]{0,1:T(8,128)(2,1)S(1)}, bf16[2304,8]{0,1:T(8,128)(2,1)}, u32[]{:S(2)}) copy-start(bf16[2304,8]{0,1:T(8,128)(2,1)} %param.24) | copy-start | bytes 110596
  437.4 35.4 %all-to-all-start.5 = ((bf16[4,24,2304]{2,1,0:T(8,128)(2,1)}), bf16[4,24,2304]{2,1,0:T(8,128)(2,1)S(1)}, u32[]{:S(2)}, u32[]{:S(2)}) async-start(bf16[4,24,2304]{2,1,0:T(8,128)(2,1)} %reduce_sum.91), calls=%async_computation.5 | async-start | bytes 884736 | tf_op jit(solution)/shard_map/all_to_all | solution.py:159
  473.8 17.8 %all-to-all-start.6 = ((bf16[16,6,2304]{2,1,0:T(8,128)(2,1)}), bf16[16,6,2304]{2,1,0:T(8,128)(2,1)S(1)}, u32[]{:S(2)}, u32[]{:S(2)}) async-start(bf16[16,6,2304]{2,1,0:T(8,128)(2,1)} %all_to_all.34), calls=%async_computation.6 | async-start | bytes 1179648 | tf_op jit(solution)/shard_map/all_to_all | solution.py:160
  491.7 1.5 copy-start.10
Sparse Core Ops, SparseCore 0:
  119.0 46.0 all-gather.7
  167.2 141.9 all-gather.5
  311.3 20.8 all-gather.9
where the time goes:
time: 501 us; the launch traced here: 500 us
  waiting for transfers between devices  262 us (52%)
  blocking collectives  144 us (29%)
  starting transfers between devices  25.4 us (5%)
  other arithmetic  21.6 us (4%)
  local copies, waits for them, and re-layouts  16.8 us (3%)
  matrix products  16.7 us (3%)
  between operations  14.2 us (3%)
    all_gather x1, waiting for transfers between devices, on_device(): lax.all_gather(jnp.stack([gate_proj[0], up_proj[0], down_proj[0]]), 'zz',...  144 us
    all_to_all x1, blocking collectives, on_device(): lax.all_to_all(back_c, 'h', split_axis=1, concat_axis=1, tiled=True)  82.1 us
    all_gather x1, waiting for transfers between devices, on_device(): over_h = lax.all_gather(sent, 'h')  45 us
    all_to_all x1, blocking collectives, on_device(): lax.all_to_all(arrived.reshape(n_zz, piece, model_width), 'zz', split_axi...  40.3 us
    all_gather x1, waiting for transfers between devices, on_device(): rows_here = lax.all_gather(over_h, 'c')  23 us
    all_to_all x1, waiting for transfers between devices, on_device(): lax.all_to_all(summed, 'zz', split_axis=0, concat_axis=0, tiled=True)  23 us
    all_to_all x1, waiting for transfers between devices, on_device(): lax.all_to_all(partial_proj.reshape(expert_count, own_rows, partial_proj....  15.5 us
    all_to_all x1, blocking collectives, on_device(): lax.all_to_all(outgoing.reshape(expert_devs * capacity, model_width), 'ex...  13.9 us
  transfers between devices with their start and end apart: 6, of which 6 were waited for; matrix products, arithmetic and copies ran while one was open for 1% of the time, Pallas kernels for 0%

commit v1 on v0

--- a/solution.py
+++ b/solution.py
@@ -141,8 +141,11 @@
     sent = lax.all_to_all(
         arrived.reshape(n_zz, piece, model_width), "zz", split_axis=0, concat_axis=0, tiled=True
     )
-    over_h = lax.all_gather(sent, "h")
-    rows_here = lax.all_gather(over_h, "c")
+    swap = [(0, 1), (1, 0)]
+    from_h = lax.ppermute(sent, "h", swap)
+    both_h = jnp.stack([sent, from_h])
+    from_c = lax.ppermute(both_h, "c", swap)
+    rows_here = jnp.stack([both_h, from_c])
     flat_rows = rows_here.reshape(n_c * n_h * n_zz * piece, model_width)
     gate_val = lax.dot_general(
         flat_rows, gate_held, (((1,), (1,)), ((), ())), preferred_element_type=jnp.float32
@@ -153,9 +156,10 @@
     activated = (jax.nn.silu(gate_val) * up_val).astype(jnp.bfloat16)
     partial = jnp.dot(activated, down_held, preferred_element_type=jnp.float32).astype(jnp.bfloat16)
     partial = partial.reshape(n_c, n_h, n_zz, piece, model_width)
-    back_c = lax.all_to_all(partial, "c", split_axis=0, concat_axis=0, tiled=True)
-    back_h = lax.all_to_all(back_c, "h", split_axis=1, concat_axis=1, tiled=True)
-    summed = jnp.sum(back_h.astype(jnp.float32), axis=(0, 1)).astype(jnp.bfloat16)
+    back_c = lax.ppermute(partial[1], "c", swap)
+    sum_c = (partial[0].astype(jnp.float32) + back_c.astype(jnp.float32)).astype(jnp.bfloat16)
+    back_h = lax.ppermute(sum_c[1], "h", swap)
+    summed = (sum_c[0].astype(jnp.float32) + back_h.astype(jnp.float32)).astype(jnp.bfloat16)
     own_slots = lax.all_to_all(summed, "zz", split_axis=0, concat_axis=0, tiled=True)
     returned = lax.all_to_all(
         own_slots.reshape(slot_total, model_width), "expert", split_axis=0, concat_axis=0, tiled=True
@@ -172,7 +176,7 @@
     n_dp = mesh.shape["dp"]
     n_chips = n_dp // 2
     split = jax.sharding.Mesh(
-        mesh.devices.reshape(n_chips // 4, 4, 2, mesh.shape["expert"]), ("zz", "h", "c", "expert")
+        mesh.devices.reshape(n_chips // 2, 2, 2, mesh.shape["expert"]), ("zz", "h", "c", "expert")
     )
     dp = ("zz", "h", "c")
     placed = (

time: 501 us -> 312 us (0.62)
  the two profiles are of different devices: /device:TPU:1 before, /device:TPU:64 now
where the time goes in v1:
time: 312 us; the launch traced here: 311 us
  waiting for transfers between devices  116 us (37%)
  blocking collectives  84.8 us (27%)
  starting transfers between devices  37.1 us (12%)
  other arithmetic  22 us (7%)
  local copies, waits for them, and re-layouts  21.1 us (7%)
  matrix products  15.3 us (5%)
  between operations  14.7 us (5%)
    all_to_all x1, blocking collectives, on_device(): lax.all_to_all(arrived.reshape(n_zz, piece, model_width), 'zz', split_axi...  69.4 us
    ppermute x1, waiting for transfers between devices, on_device(): from_h = lax.ppermute(sent, 'h', swap)  37.3 us
    all_to_all x1, waiting for transfers between devices, on_device(): lax.all_to_all(summed, 'zz', split_axis=0, concat_axis=0, tiled=True)  32 us
    all_to_all x1, waiting for transfers between devices, on_device(): lax.all_to_all(partial_proj.reshape(expert_count, own_rows, partial_proj....  18.2 us
    all_to_all x1, blocking collectives, on_device(): lax.all_to_all(outgoing.reshape(expert_devs * capacity, model_width), 'ex...  15.4 us
    all_to_all x1, waiting for transfers between devices, on_device(): lax.all_to_all(own_slots.reshape(slot_total, model_width), 'expert', spli...  12.3 us
    ppermute x1, waiting for transfers between devices, on_device(): back_h = lax.ppermute(sum_c[1], 'h', swap)  10.5 us
    gather x3, other arithmetic, paged_attention(): offset = row_ids - starts[owning]  10.3 us
  transfers between devices with their start and end apart: 8, of which 8 were waited for; matrix products, arithmetic and copies ran while one was open for 11% of the time, Pallas kernels for 0%

profile of v1, /device:TPU:64, one launch (start us, length us, event | category | flops | bytes accessed | tf_op | source)
XLA Modules:
  0.0 310.9 jit_solution(15228036104417608593)
XLA Ops:
  7.3 2.2 pad_maximum_fusion.2
  9.7 0.6 copy-done.20
  10.5 1.3 gather_fusion
  12.0 0.5 broadcast.418
  12.5 0.7 reduce.23
  13.4 0.7 gather_fusion.1
  14.2 1.8 reshape.426
  16.0 0.7 gather_fusion.2
  16.8 1.9 reshape.427
  18.9 2.6 fusion.48
  22.0 0.5 fusion.20
  22.9 0.7 fusion.47
  23.8 4.4 %compare_select_fusion.4 = (s32[256,1]{0,1:T(1,128)S(1)}, s32[256,1]{0,1:T(1,128)S(1)}) fusion(s32[]{:T(128)} %bitcast.17, s32[]{:T(128)} %bitcast.18, s32[]{:T(128)} %bitcast.19, s32[]{:T(128)} %bitcast.20, s32[]{:T(128)} %bitcast.21, s32[]{:T(128)} %bitcast.23, s32[]{:T(128)} %bitcast.22, s32[256,1]{0,1:T(1,128)S(1)} %bitcast.102, s32[256,1]{0,1:T(1,128)S(1)} %bitcast.101), kind=kLoop, calls=%fused_computation.82 | loop fusion | flops 3584 | bytes 4124 | tf_op jit(solution)/shard_map/gather | solution.py:55
  28.3 5.8 %select_select_fusion = s32[256]{0:T(256)S(1)} fusion(pred[256]{0:T(512)(128)(4,1)S(1)} %get-tuple-element.10, pred[256]{0:T(512)(128)(4,1)S(1)} %get-tuple-element.9, pred[256]{0:T(512)(128)(4,1)S(1)} %get-tuple-element.8, pred[256]{0:T(512)(128)(4,1)S(1)} %get-tuple-element.7, pred[256]{0:T(512)(128)(4,1)S(1)} %get-tuple-element.6, ...), kind=kLoop, calls=%fused_computation.96 | loop fusion | flops 2304 | bytes 4388 | tf_op jit(solution)/shard_map/gather | solution.py:55
  34.1 1.7 gather_fusion.3
  35.8 1.5 convolution_convert_fusion.1
  37.2 7.2 %all-to-all-start = ((bf16[16,16,2304]{2,1,0:T(8,128)(2,1)}), bf16[16,16,2304]{2,1,0:T(8,128)(2,1)S(1)}, u32[]{:S(2)}, u32[]{:S(2)}) async-start(bf16[16,16,2304]{2,1,0:T(8,128)(2,1)} %bitcast.27), calls=%async_computation | async-start | bytes 2359296 | tf_op jit(solution)/shard_map/all_to_all | solution.py:97
  44.9 0.5 copy-done.18
  45.4 18.2 %all-to-all-done = bf16[16,16,2304]{2,1,0:T(8,128)(2,1)S(1)} async-done(((bf16[16,16,2304]{2,1,0:T(8,128)(2,1)}), bf16[16,16,2304]{2,1,0:T(8,128)(2,1)S(1)}, u32[]{:S(2)}, u32[]{:S(2)}) %all-to-all-start) | async-done | bytes 1179680 | tf_op jit(solution)/shard_map/all_to_all | solution.py:97
  64.1 0.6 copy-done.7
  65.2 15.4 %all_to_all.33 = bf16[16,6,2304]{2,1,0:T(8,128)(2,1)S(1)} all-to-all(bf16[16,6,2304]{2,1,0:T(8,128)(2,1)S(1)} %bitcast.99), channel_id=1, replica_groups=mesh['zz'=8,'h'=2,'c'=2,'expert'=16] {'expert'}, dimensions={0} | all-to-all | bytes 884736 | tf_op jit(solution)/shard_map/all_to_all | solution.py:129
  80.7 69.4 %all_to_all.34 = bf16[8,12,2304]{2,1,0:T(8,128)(2,1)S(1)} all-to-all(bf16[8,12,2304]{2,1,0:T(8,128)(2,1)S(1)} %reshape.295), channel_id=1, replica_groups=mesh['zz'=8,'h'=2,'c'=2,'expert'=16] {'zz'}, dimensions={0} | all-to-all | bytes 884736 | tf_op jit(solution)/shard_map/all_to_all | solution.py:141
  150.3 1.9 collective-permute-start
  152.2 37.3 %collective-permute-done = bf16[8,12,2304]{2,0,1:T(8,128)(2,1)S(1)} collective-permute-done((bf16[8,12,2304]{2,0,1:T(8,128)(2,1)S(1)}, bf16[8,12,2304]{2,0,1:T(8,128)(2,1)S(1)}, u32[]{:S(2)}, u32[]{:S(2)}) %collective-permute-start) | collective-permute-done | bytes 442400 | tf_op jit(solution)/shard_map/ppermute | solution.py:145
  190.0 2.1 collective-permute-start.1
  192.1 2.2 collective-permute-done.1
  194.8 1.5 reshape.296
  196.3 2.2 all-gather.2.cloned.1.call-done
  198.5 4.3 %fusion.1 = f32[384,512]{1,0:T(8,128)} fusion(bf16[384,2304]{1,0:T(8,128)(2,1)} %reshape.296, bf16[3,512,2304]{2,1,0:T(8,128)(2,1)} %all-gather.2.cloned.1.call-done), kind=kOutput, calls=%fused_computation.13 | convolution fusion | flops 905969664 | bytes 4915200 | tf_op jit(solution)/shard_map/dot_general | solution.py:150
  202.8 6.1 %convolution_convert_fusion = bf16[384,2304]{1,0:T(8,128)(2,1)} fusion(bf16[3,512,2304]{2,1,0:T(8,128)(2,1)} %all-gather.2.cloned.1.call-done, bf16[384,2304]{1,0:T(8,128)(2,1)S(1)} %copy-done.3, f32[384,512]{1,0:T(8,128)} %fusion.1), kind=kOutput, calls=%fused_computation.6 | convolution fusion | flops 1814003712 | bytes 9043968 | tf_op jit(solution)/shard_map/dot_general | solution.py:157
  208.9 2.8 fusion.46
  211.9 1.2 copy.109
  213.1 1.9 collective-permute-start.2
  215.0 1.5 reshape.300
  216.5 1.2 collective-permute-done.2
  217.7 1.4 add_convert_fusion
  219.4 7.7 %collective-permute-start.3 = (bf16[8,12,2304]{2,0,1:T(8,128)(2,1)S(1)}, bf16[8,12,2304]{2,0,1:T(8,128)(2,1)S(1)}, u32[]{:S(2)}, u32[]{:S(2)}) collective-permute-start(bf16[8,12,2304]{2,0,1:T(8,128)(2,1)S(1)} %copy.111), channel_id=1, source_target_pairs={{0,32},{32,0},{1,33},{33,1},{2,34},{34,2},{3,35},{35,3},{4,36},{36... | collective-permute-start | bytes 1327112 | tf_op jit(solution)/shard_map/ppermute | solution.py:161
  227.1 10.5 %collective-permute-done.3 = bf16[8,12,2304]{2,0,1:T(8,128)(2,1)S(1)} collective-permute-done((bf16[8,12,2304]{2,0,1:T(8,128)(2,1)S(1)}, bf16[8,12,2304]{2,0,1:T(8,128)(2,1)S(1)}, u32[]{:S(2)}, u32[]{:S(2)}) %collective-permute-start.3) | collective-permute-done | bytes 442400 | tf_op jit(solution)/shard_map/ppermute | solution.py:161
  237.6 0.9 fusion.23
  238.5 9.6 %all-to-all-start.3 = ((bf16[8,12,2304]{2,1,0:T(8,128)(2,1)}), bf16[8,12,2304]{2,1,0:T(8,128)(2,1)S(1)}, u32[]{:S(2)}, u32[]{:S(2)}) async-start(bf16[8,12,2304]{2,1,0:T(8,128)(2,1)} %fusion.23), calls=%async_computation.3 | async-start | bytes 1179648 | tf_op jit(solution)/shard_map/all_to_all | solution.py:163
  248.7 0.7 gather_fusion.5
  249.5 32.0 %all-to-all-done.3 = bf16[8,12,2304]{2,1,0:T(8,128)(2,1)S(1)} async-done(((bf16[8,12,2304]{2,1,0:T(8,128)(2,1)}), bf16[8,12,2304]{2,1,0:T(8,128)(2,1)S(1)}, u32[]{:S(2)}, u32[]{:S(2)}) %all-to-all-start.3) | async-done | bytes 442400 | tf_op jit(solution)/shard_map/all_to_all | solution.py:163
  281.5 1.0 all_to_all.26
  282.5 6.7 %all-to-all-start.4 = ((bf16[16,6,2304]{2,1,0:T(8,128)(2,1)}), bf16[16,6,2304]{2,1,0:T(8,128)(2,1)S(1)}, u32[]{:S(2)}, u32[]{:S(2)}) async-start(bf16[16,6,2304]{2,1,0:T(8,128)(2,1)} %all_to_all.26), calls=%async_computation.4 | async-start | bytes 1179648 | tf_op jit(solution)/shard_map/all_to_all | solution.py:164
  289.4 12.3 %all-to-all-done.4 = bf16[16,6,2304]{2,1,0:T(8,128)(2,1)S(1)} async-done(((bf16[16,6,2304]{2,1,0:T(8,128)(2,1)}), bf16[16,6,2304]{2,1,0:T(8,128)(2,1)S(1)}, u32[]{:S(2)}, u32[]{:S(2)}) %all-to-all-start.4) | async-done | bytes 442400 | tf_op jit(solution)/shard_map/all_to_all | solution.py:164
  301.8 0.7 gather_fusion.4
  302.7 0.4 multiply_reduce_fusion
  303.3 0.7 multiply_convert_fusion
  (112 shorter events, 6.3 us)
Async XLA Ops:
  7.2 6.2 %copy-start = (bf16[32,128,128]{2,1,0:T(8,128)(2,1)S(1)}, bf16[32,128,128]{2,1,0:T(8,128)(2,1)}, u32[]{:S(2)}) copy-start(bf16[32,128,128]{2,1,0:T(8,128)(2,1)} %param.17) | copy-start | bytes 3145732
  7.2 2.3 copy-start.16
  7.2 3.3 %copy-start.1 = (bf16[256,128]{1,0:T(8,128)(2,1)S(1)}, bf16[256,128]{1,0:T(8,128)(2,1)}, u32[]{:S(2)}) copy-start(bf16[256,128]{1,0:T(8,128)(2,1)} %param.16) | copy-start | bytes 196612
  7.2 5.3 %copy-start.22 = (s32[1,32]{1,0:T(1,128)S(1)}, s32[1,32]{1,0:T(1,128)}, u32[]{:S(2)}) copy-start(s32[1,32]{1,0:T(1,128)} %param.21) | copy-start | bytes 388
  7.2 191.3 %all-gather.2.cloned.1.call-start = ((), (), s32[]{:S(2)}) async-start(), calls=%async_computation.5 | async-start | bytes 7962624 | tf_op jit(solution)/shard_map/all_gather | solution.py:76
  9.7 0.6 copy-start.20
  14.2 1.8 copy-start.4
  16.7 1.9 copy-start.15
  18.9 3.1 copy-start.2
  22.0 1.7 copy-start.17
  22.0 1.7 copy-start.21
  22.5 13.2 %copy-start.9 = (bf16[128,2304]{1,0:T(8,128)(2,1)S(1)}, bf16[128,2304]{1,0:T(8,128)(2,1)}, u32[]{:S(2)}) copy-start(bf16[128,2304]{1,0:T(8,128)(2,1)} %param.22) | copy-start | bytes 1769476
  35.8 8.7 %copy-start.13 = (s32[16,2]{0,1:T(2,128)S(1)}, s32[16,2]{0,1:T(2,128)}, u32[]{:S(2)}) copy-start(s32[16,2]{0,1:T(2,128)} %param.28) | copy-start | bytes 388
  37.2 26.6 %copy-start.5 = (bf16[16,2304]{1,0:T(8,128)(2,1)S(1)}, bf16[16,2304]{1,0:T(8,128)(2,1)}, u32[]{:S(2)}) copy-start(bf16[16,2304]{1,0:T(8,128)(2,1)} %param.15) | copy-start | bytes 221188
  37.2 26.7 %copy-start.11 = (f32[2304]{0:T(1024)S(1)}, f32[2304]{0:T(1024)}, u32[]{:S(2)}) copy-start(f32[2304]{0:T(1024)} %param.23) | copy-start | bytes 27652
  37.2 26.4 %all-to-all-start = ((bf16[16,16,2304]{2,1,0:T(8,128)(2,1)}), bf16[16,16,2304]{2,1,0:T(8,128)(2,1)S(1)}, u32[]{:S(2)}, u32[]{:S(2)}) async-start(bf16[16,16,2304]{2,1,0:T(8,128)(2,1)} %bitcast.27), calls=%async_computation | async-start | bytes 2359296 | tf_op jit(solution)/shard_map/all_to_all | solution.py:97
  44.9 0.5 copy-start.18
  64.1 0.6 copy-start.7
  150.3 39.2 %collective-permute-start = (bf16[8,12,2304]{2,0,1:T(8,128)(2,1)S(1)}, bf16[8,12,2304]{2,0,1:T(8,128)(2,1)S(1)}, u32[]{:S(2)}, u32[]{:S(2)}) collective-permute-start(bf16[8,12,2304]{2,0,1:T(8,128)(2,1)S(1)} %copy.105), channel_id=1, source_target_pairs={{0,32},{32,0},{1,33},{33,1},{2,34},{34,2},{3,35},{35,3},{4,36},{36... | collective-permute-start | bytes 1327112 | tf_op jit(solution)/shard_map/ppermute | solution.py:145
  190.0 4.3 %collective-permute-start.1 = (bf16[2,8,12,2304]{3,1,2,0:T(8,128)(2,1)S(1)}, bf16[2,8,12,2304]{3,1,2,0:T(8,128)(2,1)S(1)}, u32[]{:S(2)}, u32[]{:S(2)}) collective-permute-start(bf16[2,8,12,2304]{3,1,2,0:T(8,128)(2,1)S(1)} %copy.107), channel_id=1, source_target_pairs={{0,16},{16,0},{1,17},{17,1},{2,18},{18,2},{3,19},{19,3},{4,20},{20... | collective-permute-start | bytes 2654216 | tf_op jit(solution)/shard_map/ppermute | solution.py:147
  196.3 6.5 %copy-start.3 = (bf16[384,2304]{1,0:T(8,128)(2,1)S(1)}, bf16[384,2304]{1,0:T(8,128)(2,1)}, u32[]{:S(2)}) copy-start(bf16[384,2304]{1,0:T(8,128)(2,1)} %reshape.296) | copy-start | bytes 5308420
  213.1 4.7 %collective-permute-start.2 = (bf16[2,8,12,2304]{3,1,2,0:T(8,128)(2,1)}, bf16[2,8,12,2304]{3,1,2,0:T(8,128)(2,1)}, u32[]{:S(2)}, u32[]{:S(2)}) collective-permute-start(bf16[2,8,12,2304]{3,1,2,0:T(8,128)(2,1)} %copy.109), channel_id=1, source_target_pairs={{0,16},{16,0},{1,17},{17,1},{2,18},{18,2},{3,19},{19,3},{4,20},{20... | collective-permute-start | bytes 2654216 | tf_op jit(solution)/shard_map/ppermute | solution.py:159
  219.2 28.9 %copy-start.14 = (s32[16,2]{0,1:T(2,128)S(1)}, s32[16,2]{0,1:T(2,128)}, u32[]{:S(2)}) copy-start(s32[16,2]{0,1:T(2,128)} %param.28) | copy-start | bytes 388
  219.3 29.2 %copy-start.19 = (s32[32]{0:T(128)S(1)}, s32[32]{0:T(128)}, u32[]{:S(2)}) copy-start(s32[32]{0:T(128)} %copy-done.18) | copy-start | bytes 388
  219.3 29.2 %copy-start.8 = (bf16[16,2304]{1,0:T(8,128)(2,1)S(1)}, bf16[16,2304]{1,0:T(8,128)(2,1)}, u32[]{:S(2)}) copy-start(bf16[16,2304]{1,0:T(8,128)(2,1)} %copy-done.7) | copy-start | bytes 221188
  219.3 29.2 %copy-start.10 = (bf16[2304,8]{0,1:T(8,128)(2,1)S(1)}, bf16[2304,8]{0,1:T(8,128)(2,1)}, u32[]{:S(2)}) copy-start(bf16[2304,8]{0,1:T(8,128)(2,1)} %param.24) | copy-start | bytes 110596
  219.4 18.1 %collective-permute-start.3 = (bf16[8,12,2304]{2,0,1:T(8,128)(2,1)S(1)}, bf16[8,12,2304]{2,0,1:T(8,128)(2,1)S(1)}, u32[]{:S(2)}, u32[]{:S(2)}) collective-permute-start(bf16[8,12,2304]{2,0,1:T(8,128)(2,1)S(1)} %copy.111), channel_id=1, source_target_pairs={{0,32},{32,0},{1,33},{33,1},{2,34},{34,2},{3,35},{35,3},{4,36},{36... | collective-permute-start | bytes 1327112 | tf_op jit(solution)/shard_map/ppermute | solution.py:161
  238.5 43.1 %all-to-all-start.3 = ((bf16[8,12,2304]{2,1,0:T(8,128)(2,1)}), bf16[8,12,2304]{2,1,0:T(8,128)(2,1)S(1)}, u32[]{:S(2)}, u32[]{:S(2)}) async-start(bf16[8,12,2304]{2,1,0:T(8,128)(2,1)} %fusion.23), calls=%async_computation.3 | async-start | bytes 1179648 | tf_op jit(solution)/shard_map/all_to_all | solution.py:163
  282.5 19.1 %all-to-all-start.4 = ((bf16[16,6,2304]{2,1,0:T(8,128)(2,1)}), bf16[16,6,2304]{2,1,0:T(8,128)(2,1)S(1)}, u32[]{:S(2)}, u32[]{:S(2)}) async-start(bf16[16,6,2304]{2,1,0:T(8,128)(2,1)} %all_to_all.26), calls=%async_computation.4 | async-start | bytes 1179648 | tf_op jit(solution)/shard_map/all_to_all | solution.py:164
  301.8 1.3 copy-start.6
  301.8 1.5 copy-start.12
Sparse Core Ops, SparseCore 0:
  10.1 188.3 all-gather.1

commit v2 on v1

--- a/solution.py
+++ b/solution.py
@@ -138,8 +138,15 @@
     n_c = lax.axis_size("c")
     slot_total = arrived.shape[0]
     piece = slot_total // n_zz
-    sent = lax.all_to_all(
-        arrived.reshape(n_zz, piece, model_width), "zz", split_axis=0, concat_axis=0, tiled=True
+    zz_index = lax.axis_index("zz")
+    by_piece = arrived.reshape(n_zz, piece, model_width)
+    rolled = lax.dynamic_slice_in_dim(jnp.concatenate([by_piece, by_piece]), zz_index, n_zz, axis=0)
+    sent = jnp.stack(
+        [rolled[0]]
+        + [
+            lax.ppermute(rolled[k], "zz", [(i, (i + k) % n_zz) for i in range(n_zz)])
+            for k in range(1, n_zz)
+        ]
     )
     swap = [(0, 1), (1, 0)]
     from_h = lax.ppermute(sent, "h", swap)
@@ -160,7 +167,16 @@
     sum_c = (partial[0].astype(jnp.float32) + back_c.astype(jnp.float32)).astype(jnp.bfloat16)
     back_h = lax.ppermute(sum_c[1], "h", swap)
     summed = (sum_c[0].astype(jnp.float32) + back_h.astype(jnp.float32)).astype(jnp.bfloat16)
-    own_slots = lax.all_to_all(summed, "zz", split_axis=0, concat_axis=0, tiled=True)
+    back_rel = jnp.stack(
+        [summed[0]]
+        + [
+            lax.ppermute(summed[k], "zz", [(i, (i - k) % n_zz) for i in range(n_zz)])
+            for k in range(1, n_zz)
+        ]
+    )
+    own_slots = lax.dynamic_slice_in_dim(
+        jnp.concatenate([back_rel, back_rel]), (n_zz - zz_index) % n_zz, n_zz, axis=0
+    )
     returned = lax.all_to_all(
         own_slots.reshape(slot_total, model_width), "expert", split_axis=0, concat_axis=0, tiled=True
     ).astype(jnp.float32)

time: 312 us -> 326 us (1.045)
  the two profiles are of different devices: /device:TPU:64 before, /device:TPU:32 now
where the time goes in v2:
time: 326 us; the launch traced here: 325 us
  starting transfers between devices  139 us (43%)
  waiting for transfers between devices  109 us (33%)
  local copies, waits for them, and re-layouts  23.8 us (7%)
  other arithmetic  23.6 us (7%)
  matrix products  15.5 us (5%)
  between operations  15 us (5%)
    ppermute x7, starting transfers between devices, on_device(): lax.ppermute(rolled[k], 'zz', [(i, (i + k) % n_zz) for i in range(n_zz)])  44.1 us
    ppermute x7, starting transfers between devices, on_device(): lax.ppermute(summed[k], 'zz', [(i, (i - k) % n_zz) for i in range(n_zz)])  38.6 us
    ppermute x1, starting transfers between devices, on_device(): from_h = lax.ppermute(sent, 'h', swap)  32.6 us
    ppermute x1, waiting for transfers between devices, on_device(): from_h = lax.ppermute(sent, 'h', swap)  31.4 us
    all_to_all x1, waiting for transfers between devices, on_device(): lax.all_to_all(partial_proj.reshape(expert_count, own_rows, partial_proj....  18.2 us
    ppermute x7, waiting for transfers between devices, on_device(): lax.ppermute(summed[k], 'zz', [(i, (i - k) % n_zz) for i in range(n_zz)])  13 us
    all_to_all x1, waiting for transfers between devices, on_device(): lax.all_to_all(own_slots.reshape(slot_total, model_width), 'expert', spli...  12.3 us
    all_to_all x1, waiting for transfers between devices, on_device(): lax.all_to_all(outgoing.reshape(expert_devs * capacity, model_width), 'ex...  12 us
  transfers between devices with their start and end apart: 22, of which 12 were waited for; matrix products, arithmetic and copies ran while one was open for 11% of the time, Pallas kernels for 0%

profile of v2, /device:TPU:32, one launch (start us, length us, event | category | flops | bytes accessed | tf_op | source)
XLA Modules:
  0.0 325.2 jit_solution(10123222100625176872)
XLA Ops:
  7.2 2.2 pad_maximum_fusion.2
  12.6 1.8 reshape.426
  14.5 1.3 gather_fusion
  17.0 1.9 reshape.427
  18.9 2.6 fusion.49
  23.7 4.4 %compare_select_fusion.4 = (s32[256,1]{0,1:T(1,128)S(1)}, s32[256,1]{0,1:T(1,128)S(1)}) fusion(s32[]{:T(128)} %bitcast.17, s32[]{:T(128)} %bitcast.18, s32[]{:T(128)} %bitcast.19, s32[]{:T(128)} %bitcast.20, s32[]{:T(128)} %bitcast.21, s32[]{:T(128)} %bitcast.23, s32[]{:T(128)} %bitcast.22, s32[256,1]{0,1:T(1,128)S(1)} %bitcast.164, s32[256,1]{0,1:T(1,128)S(1)} %bitcast.163), kind=kLoop, calls=%fused_computation.123 | loop fusion | flops 3584 | bytes 4124 | tf_op jit(solution)/shard_map/gather | solution.py:55
  28.1 5.8 %select_select_fusion = s32[256]{0:T(256)S(1)} fusion(pred[256]{0:T(512)(128)(4,1)S(1)} %get-tuple-element.10, pred[256]{0:T(512)(128)(4,1)S(1)} %get-tuple-element.9, pred[256]{0:T(512)(128)(4,1)S(1)} %get-tuple-element.8, pred[256]{0:T(512)(128)(4,1)S(1)} %get-tuple-element.7, pred[256]{0:T(512)(128)(4,1)S(1)} %get-tuple-element.6, ...), kind=kLoop, calls=%fused_computation.137 | loop fusion | flops 2304 | bytes 4388 | tf_op jit(solution)/shard_map/gather | solution.py:55
  34.0 1.7 gather_fusion.3
  35.7 1.5 convolution_convert_fusion.1
  37.1 7.2 %all-to-all-start = ((bf16[16,16,2304]{2,1,0:T(8,128)(2,1)}), bf16[16,16,2304]{2,1,0:T(8,128)(2,1)S(1)}, u32[]{:S(2)}, u32[]{:S(2)}) async-start(bf16[16,16,2304]{2,1,0:T(8,128)(2,1)} %bitcast.27), calls=%async_computation | async-start | bytes 2359296 | tf_op jit(solution)/shard_map/all_to_all | solution.py:97
  45.4 18.2 %all-to-all-done = bf16[16,16,2304]{2,1,0:T(8,128)(2,1)S(1)} async-done(((bf16[16,16,2304]{2,1,0:T(8,128)(2,1)}), bf16[16,16,2304]{2,1,0:T(8,128)(2,1)S(1)}, u32[]{:S(2)}, u32[]{:S(2)}) %all-to-all-start) | async-done | bytes 1179680 | tf_op jit(solution)/shard_map/all_to_all | solution.py:97
  65.9 3.6 %all-to-all-start.1 = ((bf16[16,6,2304]{2,1,0:T(8,128)(2,1)}), bf16[16,6,2304]{2,1,0:T(8,128)(2,1)S(1)}, u32[]{:S(2)}, u32[]{:S(2)}) async-start(bf16[16,6,2304]{2,1,0:T(8,128)(2,1)} %bitcast.28), calls=%async_computation.1 | async-start | bytes 1179648 | tf_op jit(solution)/shard_map/all_to_all | solution.py:129
  69.5 12.0 %all-to-all-done.1 = bf16[16,6,2304]{2,1,0:T(8,128)(2,1)S(1)} async-done(((bf16[16,6,2304]{2,1,0:T(8,128)(2,1)}), bf16[16,6,2304]{2,1,0:T(8,128)(2,1)S(1)}, u32[]{:S(2)}, u32[]{:S(2)}) %all-to-all-start.1) | async-done | bytes 442400 | tf_op jit(solution)/shard_map/all_to_all | solution.py:129
  81.9 5.2 %collective-permute-start = (bf16[12,2304]{1,0:T(8,128)(2,1)S(1)}, bf16[12,2304]{1,0:T(8,128)(2,1)S(1)}, u32[]{:S(2)}, u32[]{:S(2)}) collective-permute-start(bf16[12,2304]{1,0:T(8,128)(2,1)S(1)} %get-tuple-element.35), channel_id=1, source_target_pairs={{0,64},{64,128},{128,192},{192,256},{256,320},{320,384},{384,448},... | collective-permute-start | bytes 165896 | tf_op jit(solution)/shard_map/ppermute | solution.py:147
  87.1 9.1 %collective-permute-start.1 = (bf16[12,2304]{1,0:T(8,128)(2,1)S(1)}, bf16[12,2304]{1,0:T(8,128)(2,1)S(1)}, u32[]{:S(2)}, u32[]{:S(2)}) collective-permute-start(bf16[12,2304]{1,0:T(8,128)(2,1)S(1)} %get-tuple-element.34), channel_id=1, source_target_pairs={{0,128},{64,192},{128,256},{192,320},{256,384},{320,448},{384,0},{... | collective-permute-start | bytes 165896 | tf_op jit(solution)/shard_map/ppermute | solution.py:147
  96.2 7.3 %collective-permute-start.2 = (bf16[12,2304]{1,0:T(8,128)(2,1)S(1)}, bf16[12,2304]{1,0:T(8,128)(2,1)S(1)}, u32[]{:S(2)}, u32[]{:S(2)}) collective-permute-start(bf16[12,2304]{1,0:T(8,128)(2,1)S(1)} %get-tuple-element.33), channel_id=1, source_target_pairs={{0,192},{64,256},{128,320},{192,384},{256,448},{320,0},{384,64},{4... | collective-permute-start | bytes 165896 | tf_op jit(solution)/shard_map/ppermute | solution.py:147
  103.5 4.6 %collective-permute-start.3 = (bf16[12,2304]{1,0:T(8,128)(2,1)S(1)}, bf16[12,2304]{1,0:T(8,128)(2,1)S(1)}, u32[]{:S(2)}, u32[]{:S(2)}) collective-permute-start(bf16[12,2304]{1,0:T(8,128)(2,1)S(1)} %get-tuple-element.32), channel_id=1, source_target_pairs={{0,256},{64,320},{128,384},{192,448},{256,0},{320,64},{384,128},{4... | collective-permute-start | bytes 165896 | tf_op jit(solution)/shard_map/ppermute | solution.py:147
  108.1 9.1 %collective-permute-start.4 = (bf16[12,2304]{1,0:T(8,128)(2,1)S(1)}, bf16[12,2304]{1,0:T(8,128)(2,1)S(1)}, u32[]{:S(2)}, u32[]{:S(2)}) collective-permute-start(bf16[12,2304]{1,0:T(8,128)(2,1)S(1)} %get-tuple-element.31), channel_id=1, source_target_pairs={{0,320},{64,384},{128,448},{192,0},{256,64},{320,128},{384,192},{4... | collective-permute-start | bytes 165896 | tf_op jit(solution)/shard_map/ppermute | solution.py:147
  117.2 5.5 %collective-permute-start.5 = (bf16[12,2304]{1,0:T(8,128)(2,1)S(1)}, bf16[12,2304]{1,0:T(8,128)(2,1)S(1)}, u32[]{:S(2)}, u32[]{:S(2)}) collective-permute-start(bf16[12,2304]{1,0:T(8,128)(2,1)S(1)} %get-tuple-element.30), channel_id=1, source_target_pairs={{0,384},{64,448},{128,0},{192,64},{256,128},{320,192},{384,256},{4... | collective-permute-start | bytes 165896 | tf_op jit(solution)/shard_map/ppermute | solution.py:147
  122.7 3.4 %collective-permute-start.6 = (bf16[12,2304]{1,0:T(8,128)(2,1)S(1)}, bf16[12,2304]{1,0:T(8,128)(2,1)S(1)}, u32[]{:S(2)}, u32[]{:S(2)}) collective-permute-start(bf16[12,2304]{1,0:T(8,128)(2,1)S(1)} %get-tuple-element.29), channel_id=1, source_target_pairs={{0,448},{64,0},{128,64},{192,128},{256,192},{320,256},{384,320},{4... | collective-permute-start | bytes 165896 | tf_op jit(solution)/shard_map/ppermute | solution.py:147
  127.0 4.0 %collective-permute-done.4 = bf16[12,2304]{1,0:T(8,128)(2,1)S(1)} collective-permute-done((bf16[12,2304]{1,0:T(8,128)(2,1)S(1)}, bf16[12,2304]{1,0:T(8,128)(2,1)S(1)}, u32[]{:S(2)}, u32[]{:S(2)}) %collective-permute-start.4) | collective-permute-done | bytes 55328 | tf_op jit(solution)/shard_map/ppermute | solution.py:147
  131.0 3.4 %collective-permute-done.5 = bf16[12,2304]{1,0:T(8,128)(2,1)S(1)} collective-permute-done((bf16[12,2304]{1,0:T(8,128)(2,1)S(1)}, bf16[12,2304]{1,0:T(8,128)(2,1)S(1)}, u32[]{:S(2)}, u32[]{:S(2)}) %collective-permute-start.5) | collective-permute-done | bytes 55328 | tf_op jit(solution)/shard_map/ppermute | solution.py:147
  135.4 32.6 %collective-permute-start.7 = (bf16[8,12,2304]{2,0,1:T(8,128)(2,1)S(1)}, bf16[8,12,2304]{2,0,1:T(8,128)(2,1)S(1)}, u32[]{:S(2)}, u32[]{:S(2)}) collective-permute-start(bf16[8,12,2304]{2,0,1:T(8,128)(2,1)S(1)} %copy.105), channel_id=1, source_target_pairs={{0,32},{32,0},{1,33},{33,1},{2,34},{34,2},{3,35},{35,3},{4,36},{36... | collective-permute-start | bytes 1327112 | tf_op jit(solution)/shard_map/ppermute | solution.py:152
  167.9 31.4 %collective-permute-done.7 = bf16[8,12,2304]{2,0,1:T(8,128)(2,1)S(1)} collective-permute-done((bf16[8,12,2304]{2,0,1:T(8,128)(2,1)S(1)}, bf16[8,12,2304]{2,0,1:T(8,128)(2,1)S(1)}, u32[]{:S(2)}, u32[]{:S(2)}) %collective-permute-start.7) | collective-permute-done | bytes 442400 | tf_op jit(solution)/shard_map/ppermute | solution.py:152
  199.8 2.2 collective-permute-start.8
  202.1 2.1 collective-permute-done.8
  204.6 1.5 reshape.296
  206.2 4.4 %fusion.1 = f32[384,512]{1,0:T(8,128)} fusion(bf16[384,2304]{1,0:T(8,128)(2,1)} %reshape.296, bf16[3,512,2304]{2,1,0:T(8,128)(2,1)} %all-gather.2.cloned.1.call-done), kind=kOutput, calls=%fused_computation.13 | convolution fusion | flops 905969664 | bytes 4915200 | tf_op jit(solution)/shard_map/dot_general | solution.py:157
  210.6 6.1 %convolution_convert_fusion = bf16[384,2304]{1,0:T(8,128)(2,1)} fusion(bf16[3,512,2304]{2,1,0:T(8,128)(2,1)} %all-gather.2.cloned.1.call-done, bf16[384,2304]{1,0:T(8,128)(2,1)S(1)} %copy-done.4, f32[384,512]{1,0:T(8,128)} %fusion.1), kind=kOutput, calls=%fused_computation.6 | convolution fusion | flops 1814003712 | bytes 9043968 | tf_op jit(solution)/shard_map/dot_general | solution.py:164
  216.7 2.8 fusion.47
  219.7 1.2 copy.109
  220.9 2.0 collective-permute-start.9
  224.1 1.5 reshape.300
  225.7 1.4 add_convert_fusion
  228.3 3.3 %collective-permute-start.10 = (bf16[8,12,2304]{2,0,1:T(8,128)(2,1)S(1)}, bf16[8,12,2304]{2,0,1:T(8,128)(2,1)S(1)}, u32[]{:S(2)}, u32[]{:S(2)}) collective-permute-start(bf16[8,12,2304]{2,0,1:T(8,128)(2,1)S(1)} %copy.111), channel_id=1, source_target_pairs={{0,32},{32,0},{1,33},{33,1},{2,34},{34,2},{3,35},{35,3},{4,36},{36... | collective-permute-start | bytes 1327112 | tf_op jit(solution)/shard_map/ppermute | solution.py:168
  232.0 10.6 %collective-permute-done.10 = bf16[8,12,2304]{2,0,1:T(8,128)(2,1)S(1)} collective-permute-done((bf16[8,12,2304]{2,0,1:T(8,128)(2,1)S(1)}, bf16[8,12,2304]{2,0,1:T(8,128)(2,1)S(1)}, u32[]{:S(2)}, u32[]{:S(2)}) %collective-permute-start.10) | collective-permute-done | bytes 442400 | tf_op jit(solution)/shard_map/ppermute | solution.py:168
  242.7 1.2 fusion.23
  244.5 6.6 %collective-permute-start.11 = (bf16[12,2304]{1,0:T(8,128)(2,1)}, bf16[12,2304]{1,0:T(8,128)(2,1)S(1)}, u32[]{:S(2)}, u32[]{:S(2)}) collective-permute-start(bf16[12,2304]{1,0:T(8,128)(2,1)} %get-tuple-element.28), channel_id=1, source_target_pairs={{0,448},{64,0},{128,64},{192,128},{256,192},{320,256},{384,320},{4... | collective-permute-start | bytes 165896 | tf_op jit(solution)/shard_map/ppermute | solution.py:173
  252.1 4.2 %collective-permute-start.12 = (bf16[12,2304]{1,0:T(8,128)(2,1)S(1)}, bf16[12,2304]{1,0:T(8,128)(2,1)S(1)}, u32[]{:S(2)}, u32[]{:S(2)}) collective-permute-start(bf16[12,2304]{1,0:T(8,128)(2,1)S(1)} %get-tuple-element.27), channel_id=1, source_target_pairs={{0,384},{64,448},{128,0},{192,64},{256,128},{320,192},{384,256},{4... | collective-permute-start | bytes 165896 | tf_op jit(solution)/shard_map/ppermute | solution.py:173
  256.3 6.2 %collective-permute-start.13 = (bf16[12,2304]{1,0:T(8,128)(2,1)S(1)}, bf16[12,2304]{1,0:T(8,128)(2,1)S(1)}, u32[]{:S(2)}, u32[]{:S(2)}) collective-permute-start(bf16[12,2304]{1,0:T(8,128)(2,1)S(1)} %get-tuple-element.26), channel_id=1, source_target_pairs={{0,320},{64,384},{128,448},{192,0},{256,64},{320,128},{384,192},{4... | collective-permute-start | bytes 165896 | tf_op jit(solution)/shard_map/ppermute | solution.py:173
  262.5 6.3 %collective-permute-start.14 = (bf16[12,2304]{1,0:T(8,128)(2,1)S(1)}, bf16[12,2304]{1,0:T(8,128)(2,1)S(1)}, u32[]{:S(2)}, u32[]{:S(2)}) collective-permute-start(bf16[12,2304]{1,0:T(8,128)(2,1)S(1)} %get-tuple-element.25), channel_id=1, source_target_pairs={{0,256},{64,320},{128,384},{192,448},{256,0},{320,64},{384,128},{4... | collective-permute-start | bytes 165896 | tf_op jit(solution)/shard_map/ppermute | solution.py:173
  268.8 6.0 %collective-permute-start.15 = (bf16[12,2304]{1,0:T(8,128)(2,1)S(1)}, bf16[12,2304]{1,0:T(8,128)(2,1)S(1)}, u32[]{:S(2)}, u32[]{:S(2)}) collective-permute-start(bf16[12,2304]{1,0:T(8,128)(2,1)S(1)} %get-tuple-element.24), channel_id=1, source_target_pairs={{0,192},{64,256},{128,320},{192,384},{256,448},{320,0},{384,64},{4... | collective-permute-start | bytes 165896 | tf_op jit(solution)/shard_map/ppermute | solution.py:173
  274.9 5.1 %collective-permute-start.16 = (bf16[12,2304]{1,0:T(8,128)(2,1)S(1)}, bf16[12,2304]{1,0:T(8,128)(2,1)S(1)}, u32[]{:S(2)}, u32[]{:S(2)}) collective-permute-start(bf16[12,2304]{1,0:T(8,128)(2,1)S(1)} %get-tuple-element.23), channel_id=1, source_target_pairs={{0,128},{64,192},{128,256},{192,320},{256,384},{320,448},{384,0},{... | collective-permute-start | bytes 165896 | tf_op jit(solution)/shard_map/ppermute | solution.py:173
  280.0 4.2 %collective-permute-start.17 = (bf16[12,2304]{1,0:T(8,128)(2,1)S(1)}, bf16[12,2304]{1,0:T(8,128)(2,1)S(1)}, u32[]{:S(2)}, u32[]{:S(2)}) collective-permute-start(bf16[12,2304]{1,0:T(8,128)(2,1)S(1)} %get-tuple-element.21), channel_id=1, source_target_pairs={{0,64},{64,128},{128,192},{192,256},{256,320},{320,384},{384,448},... | collective-permute-start | bytes 165896 | tf_op jit(solution)/shard_map/ppermute | solution.py:173
  284.3 8.7 %collective-permute-done.15 = bf16[12,2304]{1,0:T(8,128)(2,1)S(1)} collective-permute-done((bf16[12,2304]{1,0:T(8,128)(2,1)S(1)}, bf16[12,2304]{1,0:T(8,128)(2,1)S(1)}, u32[]{:S(2)}, u32[]{:S(2)}) %collective-permute-start.15) | collective-permute-done | bytes 55328 | tf_op jit(solution)/shard_map/ppermute | solution.py:173
  293.0 4.3 %collective-permute-done.16 = bf16[12,2304]{1,0:T(8,128)(2,1)S(1)} collective-permute-done((bf16[12,2304]{1,0:T(8,128)(2,1)S(1)}, bf16[12,2304]{1,0:T(8,128)(2,1)S(1)}, u32[]{:S(2)}, u32[]{:S(2)}) %collective-permute-start.16) | collective-permute-done | bytes 55328 | tf_op jit(solution)/shard_map/ppermute | solution.py:173
  298.5 5.0 %all-to-all-start.2 = ((bf16[16,6,2304]{2,1,0:T(8,128)(2,1)}), bf16[16,6,2304]{2,1,0:T(8,128)(2,1)S(1)}, u32[]{:S(2)}, u32[]{:S(2)}) async-start(bf16[16,6,2304]{2,1,0:T(8,128)(2,1)} %all_to_all.18), calls=%async_computation.2 | async-start | bytes 1179648 | tf_op jit(solution)/shard_map/all_to_all | solution.py:180
  303.6 12.3 %all-to-all-done.2 = bf16[16,6,2304]{2,1,0:T(8,128)(2,1)S(1)} async-done(((bf16[16,6,2304]{2,1,0:T(8,128)(2,1)}), bf16[16,6,2304]{2,1,0:T(8,128)(2,1)S(1)}, u32[]{:S(2)}, u32[]{:S(2)}) %all-to-all-start.2) | async-done | bytes 442400 | tf_op jit(solution)/shard_map/all_to_all | solution.py:180
  (167 shorter events, 21.2 us)
Async XLA Ops:
  7.2 4.7 %copy-start = (bf16[32,128,128]{2,1,0:T(8,128)(2,1)S(1)}, bf16[32,128,128]{2,1,0:T(8,128)(2,1)}, u32[]{:S(2)}) copy-start(bf16[32,128,128]{2,1,0:T(8,128)(2,1)} %param.17) | copy-start | bytes 3145732
  7.2 2.3 copy-start.19
  7.2 3.8 %copy-start.23 = (s32[1,32]{1,0:T(1,128)S(1)}, s32[1,32]{1,0:T(1,128)}, u32[]{:S(2)}) copy-start(s32[1,32]{1,0:T(1,128)} %param.21) | copy-start | bytes 388
  7.2 199.0 %all-gather.2.cloned.1.call-start = ((), (), s32[]{:S(2)}) async-start(), calls=%async_computation.3 | async-start | bytes 7962624 | tf_op jit(solution)/shard_map/all_gather | solution.py:76
  12.6 1.8 copy-start.1
  14.5 1.5 copy-start.20
  14.5 1.7 copy-start.5
  18.9 3.1 copy-start.3
  21.9 1.7 copy-start.24
  22.5 13.2 %copy-start.10 = (bf16[128,2304]{1,0:T(8,128)(2,1)S(1)}, bf16[128,2304]{1,0:T(8,128)(2,1)}, u32[]{:S(2)}) copy-start(bf16[128,2304]{1,0:T(8,128)(2,1)} %param.22) | copy-start | bytes 1769476
  37.1 7.2 %copy-start.15 = (s32[16,2]{0,1:T(2,128)S(1)}, s32[16,2]{0,1:T(2,128)}, u32[]{:S(2)}) copy-start(s32[16,2]{0,1:T(2,128)} %param.28) | copy-start | bytes 388
  37.1 26.4 %all-to-all-start = ((bf16[16,16,2304]{2,1,0:T(8,128)(2,1)}), bf16[16,16,2304]{2,1,0:T(8,128)(2,1)S(1)}, u32[]{:S(2)}, u32[]{:S(2)}) async-start(bf16[16,16,2304]{2,1,0:T(8,128)(2,1)} %bitcast.27), calls=%async_computation | async-start | bytes 2359296 | tf_op jit(solution)/shard_map/all_to_all | solution.py:97
  44.3 19.4 %copy-start.6 = (bf16[16,2304]{1,0:T(8,128)(2,1)S(1)}, bf16[16,2304]{1,0:T(8,128)(2,1)}, u32[]{:S(2)}) copy-start(bf16[16,2304]{1,0:T(8,128)(2,1)} %param.15) | copy-start | bytes 221188
  44.3 19.6 %copy-start.13 = (f32[2304]{0:T(1024)S(1)}, f32[2304]{0:T(1024)}, u32[]{:S(2)}) copy-start(f32[2304]{0:T(1024)} %param.23) | copy-start | bytes 27652
  44.8 0.5 copy-start.21
  64.0 0.6 copy-start.8
  65.9 15.6 %all-to-all-start.1 = ((bf16[16,6,2304]{2,1,0:T(8,128)(2,1)}), bf16[16,6,2304]{2,1,0:T(8,128)(2,1)S(1)}, u32[]{:S(2)}, u32[]{:S(2)}) async-start(bf16[16,6,2304]{2,1,0:T(8,128)(2,1)} %bitcast.28), calls=%async_computation.1 | async-start | bytes 1179648 | tf_op jit(solution)/shard_map/all_to_all | solution.py:129
  81.9 35.3 %collective-permute-start = (bf16[12,2304]{1,0:T(8,128)(2,1)S(1)}, bf16[12,2304]{1,0:T(8,128)(2,1)S(1)}, u32[]{:S(2)}, u32[]{:S(2)}) collective-permute-start(bf16[12,2304]{1,0:T(8,128)(2,1)S(1)} %get-tuple-element.35), channel_id=1, source_target_pairs={{0,64},{64,128},{128,192},{192,256},{256,320},{320,384},{384,448},... | collective-permute-start | bytes 165896 | tf_op jit(solution)/shard_map/ppermute | solution.py:147
  87.1 35.6 %collective-permute-start.1 = (bf16[12,2304]{1,0:T(8,128)(2,1)S(1)}, bf16[12,2304]{1,0:T(8,128)(2,1)S(1)}, u32[]{:S(2)}, u32[]{:S(2)}) collective-permute-start(bf16[12,2304]{1,0:T(8,128)(2,1)S(1)} %get-tuple-element.34), channel_id=1, source_target_pairs={{0,128},{64,192},{128,256},{192,320},{256,384},{320,448},{384,0},{... | collective-permute-start | bytes 165896 | tf_op jit(solution)/shard_map/ppermute | solution.py:147
  96.2 30.8 %collective-permute-start.2 = (bf16[12,2304]{1,0:T(8,128)(2,1)S(1)}, bf16[12,2304]{1,0:T(8,128)(2,1)S(1)}, u32[]{:S(2)}, u32[]{:S(2)}) collective-permute-start(bf16[12,2304]{1,0:T(8,128)(2,1)S(1)} %get-tuple-element.33), channel_id=1, source_target_pairs={{0,192},{64,256},{128,320},{192,384},{256,448},{320,0},{384,64},{4... | collective-permute-start | bytes 165896 | tf_op jit(solution)/shard_map/ppermute | solution.py:147
  103.5 23.5 %collective-permute-start.3 = (bf16[12,2304]{1,0:T(8,128)(2,1)S(1)}, bf16[12,2304]{1,0:T(8,128)(2,1)S(1)}, u32[]{:S(2)}, u32[]{:S(2)}) collective-permute-start(bf16[12,2304]{1,0:T(8,128)(2,1)S(1)} %get-tuple-element.32), channel_id=1, source_target_pairs={{0,256},{64,320},{128,384},{192,448},{256,0},{320,64},{384,128},{4... | collective-permute-start | bytes 165896 | tf_op jit(solution)/shard_map/ppermute | solution.py:147
  108.1 22.9 %collective-permute-start.4 = (bf16[12,2304]{1,0:T(8,128)(2,1)S(1)}, bf16[12,2304]{1,0:T(8,128)(2,1)S(1)}, u32[]{:S(2)}, u32[]{:S(2)}) collective-permute-start(bf16[12,2304]{1,0:T(8,128)(2,1)S(1)} %get-tuple-element.31), channel_id=1, source_target_pairs={{0,320},{64,384},{128,448},{192,0},{256,64},{320,128},{384,192},{4... | collective-permute-start | bytes 165896 | tf_op jit(solution)/shard_map/ppermute | solution.py:147
  117.2 17.2 %collective-permute-start.5 = (bf16[12,2304]{1,0:T(8,128)(2,1)S(1)}, bf16[12,2304]{1,0:T(8,128)(2,1)S(1)}, u32[]{:S(2)}, u32[]{:S(2)}) collective-permute-start(bf16[12,2304]{1,0:T(8,128)(2,1)S(1)} %get-tuple-element.30), channel_id=1, source_target_pairs={{0,384},{64,448},{128,0},{192,64},{256,128},{320,192},{384,256},{4... | collective-permute-start | bytes 165896 | tf_op jit(solution)/shard_map/ppermute | solution.py:147
  122.7 12.5 %collective-permute-start.6 = (bf16[12,2304]{1,0:T(8,128)(2,1)S(1)}, bf16[12,2304]{1,0:T(8,128)(2,1)S(1)}, u32[]{:S(2)}, u32[]{:S(2)}) collective-permute-start(bf16[12,2304]{1,0:T(8,128)(2,1)S(1)} %get-tuple-element.29), channel_id=1, source_target_pairs={{0,448},{64,0},{128,64},{192,128},{256,192},{320,256},{384,320},{4... | collective-permute-start | bytes 165896 | tf_op jit(solution)/shard_map/ppermute | solution.py:147
  135.4 63.9 %collective-permute-start.7 = (bf16[8,12,2304]{2,0,1:T(8,128)(2,1)S(1)}, bf16[8,12,2304]{2,0,1:T(8,128)(2,1)S(1)}, u32[]{:S(2)}, u32[]{:S(2)}) collective-permute-start(bf16[8,12,2304]{2,0,1:T(8,128)(2,1)S(1)} %copy.105), channel_id=1, source_target_pairs={{0,32},{32,0},{1,33},{33,1},{2,34},{34,2},{3,35},{35,3},{4,36},{36... | collective-permute-start | bytes 1327112 | tf_op jit(solution)/shard_map/ppermute | solution.py:152
  199.8 4.3 %collective-permute-start.8 = (bf16[2,8,12,2304]{3,1,2,0:T(8,128)(2,1)S(1)}, bf16[2,8,12,2304]{3,1,2,0:T(8,128)(2,1)S(1)}, u32[]{:S(2)}, u32[]{:S(2)}) collective-permute-start(bf16[2,8,12,2304]{3,1,2,0:T(8,128)(2,1)S(1)} %copy.107), channel_id=1, source_target_pairs={{0,16},{16,0},{1,17},{17,1},{2,18},{18,2},{3,19},{19,3},{4,20},{20... | collective-permute-start | bytes 2654216 | tf_op jit(solution)/shard_map/ppermute | solution.py:154
  206.1 4.4 %copy-start.4 = (bf16[384,2304]{1,0:T(8,128)(2,1)S(1)}, bf16[384,2304]{1,0:T(8,128)(2,1)}, u32[]{:S(2)}) copy-start(bf16[384,2304]{1,0:T(8,128)(2,1)} %reshape.296) | copy-start | bytes 5308420
  219.7 3.2 copy-start.16
  220.9 4.8 %collective-permute-start.9 = (bf16[2,8,12,2304]{3,1,2,0:T(8,128)(2,1)}, bf16[2,8,12,2304]{3,1,2,0:T(8,128)(2,1)}, u32[]{:S(2)}, u32[]{:S(2)}) collective-permute-start(bf16[2,8,12,2304]{3,1,2,0:T(8,128)(2,1)} %copy.109), channel_id=1, source_target_pairs={{0,16},{16,0},{1,17},{17,1},{2,18},{18,2},{3,19},{19,3},{4,20},{20... | collective-permute-start | bytes 2654216 | tf_op jit(solution)/shard_map/ppermute | solution.py:166
  227.1 1.0 copy-start.2
  228.1 3.5 %copy-start.12 = (s32[16,2,1]{1,0,2:T(8,128)S(1)}, s32[16,2,1]{1,0,2:T(8,128)}, u32[]{:S(2)}) copy-start(s32[16,2,1]{1,0,2:T(8,128)} %copy.114) | copy-start | bytes 388
  228.1 3.5 %copy-start.18 = (s32[16,2]{0,1:T(2,128)S(1)}, s32[16,2]{0,1:T(2,128)}, u32[]{:S(2)}) copy-start(s32[16,2]{0,1:T(2,128)} %get-tuple-element.40) | copy-start | bytes 388
  228.1 3.8 %copy-start.22 = (s32[32]{0:T(128)S(1)}, s32[32]{0:T(128)}, u32[]{:S(2)}) copy-start(s32[32]{0:T(128)} %copy-done.21) | copy-start | bytes 388
  228.3 14.3 %collective-permute-start.10 = (bf16[8,12,2304]{2,0,1:T(8,128)(2,1)S(1)}, bf16[8,12,2304]{2,0,1:T(8,128)(2,1)S(1)}, u32[]{:S(2)}, u32[]{:S(2)}) collective-permute-start(bf16[8,12,2304]{2,0,1:T(8,128)(2,1)S(1)} %copy.111), channel_id=1, source_target_pairs={{0,32},{32,0},{1,33},{33,1},{2,34},{34,2},{3,35},{35,3},{4,36},{36... | collective-permute-start | bytes 1327112 | tf_op jit(solution)/shard_map/ppermute | solution.py:168
  232.0 19.1 %copy-start.9 = (bf16[16,2304]{1,0:T(8,128)(2,1)S(1)}, bf16[16,2304]{1,0:T(8,128)(2,1)}, u32[]{:S(2)}) copy-start(bf16[16,2304]{1,0:T(8,128)(2,1)} %copy-done.8) | copy-start | bytes 221188
  232.0 19.1 %copy-start.11 = (bf16[2304,8]{0,1:T(8,128)(2,1)S(1)}, bf16[2304,8]{0,1:T(8,128)(2,1)}, u32[]{:S(2)}) copy-start(bf16[2304,8]{0,1:T(8,128)(2,1)} %param.24) | copy-start | bytes 110596
  244.5 30.3 %collective-permute-start.11 = (bf16[12,2304]{1,0:T(8,128)(2,1)}, bf16[12,2304]{1,0:T(8,128)(2,1)S(1)}, u32[]{:S(2)}, u32[]{:S(2)}) collective-permute-start(bf16[12,2304]{1,0:T(8,128)(2,1)} %get-tuple-element.28), channel_id=1, source_target_pairs={{0,448},{64,0},{128,64},{192,128},{256,192},{320,256},{384,320},{4... | collective-permute-start | bytes 165896 | tf_op jit(solution)/shard_map/ppermute | solution.py:173
  252.1 27.9 %collective-permute-start.12 = (bf16[12,2304]{1,0:T(8,128)(2,1)S(1)}, bf16[12,2304]{1,0:T(8,128)(2,1)S(1)}, u32[]{:S(2)}, u32[]{:S(2)}) collective-permute-start(bf16[12,2304]{1,0:T(8,128)(2,1)S(1)} %get-tuple-element.27), channel_id=1, source_target_pairs={{0,384},{64,448},{128,0},{192,64},{256,128},{320,192},{384,256},{4... | collective-permute-start | bytes 165896 | tf_op jit(solution)/shard_map/ppermute | solution.py:173
  256.3 28.0 %collective-permute-start.13 = (bf16[12,2304]{1,0:T(8,128)(2,1)S(1)}, bf16[12,2304]{1,0:T(8,128)(2,1)S(1)}, u32[]{:S(2)}, u32[]{:S(2)}) collective-permute-start(bf16[12,2304]{1,0:T(8,128)(2,1)S(1)} %get-tuple-element.26), channel_id=1, source_target_pairs={{0,320},{64,384},{128,448},{192,0},{256,64},{320,128},{384,192},{4... | collective-permute-start | bytes 165896 | tf_op jit(solution)/shard_map/ppermute | solution.py:173
  262.5 21.8 %collective-permute-start.14 = (bf16[12,2304]{1,0:T(8,128)(2,1)S(1)}, bf16[12,2304]{1,0:T(8,128)(2,1)S(1)}, u32[]{:S(2)}, u32[]{:S(2)}) collective-permute-start(bf16[12,2304]{1,0:T(8,128)(2,1)S(1)} %get-tuple-element.25), channel_id=1, source_target_pairs={{0,256},{64,320},{128,384},{192,448},{256,0},{320,64},{384,128},{4... | collective-permute-start | bytes 165896 | tf_op jit(solution)/shard_map/ppermute | solution.py:173
  268.8 24.2 %collective-permute-start.15 = (bf16[12,2304]{1,0:T(8,128)(2,1)S(1)}, bf16[12,2304]{1,0:T(8,128)(2,1)S(1)}, u32[]{:S(2)}, u32[]{:S(2)}) collective-permute-start(bf16[12,2304]{1,0:T(8,128)(2,1)S(1)} %get-tuple-element.24), channel_id=1, source_target_pairs={{0,192},{64,256},{128,320},{192,384},{256,448},{320,0},{384,64},{4... | collective-permute-start | bytes 165896 | tf_op jit(solution)/shard_map/ppermute | solution.py:173
  274.9 22.4 %collective-permute-start.16 = (bf16[12,2304]{1,0:T(8,128)(2,1)S(1)}, bf16[12,2304]{1,0:T(8,128)(2,1)S(1)}, u32[]{:S(2)}, u32[]{:S(2)}) collective-permute-start(bf16[12,2304]{1,0:T(8,128)(2,1)S(1)} %get-tuple-element.23), channel_id=1, source_target_pairs={{0,128},{64,192},{128,256},{192,320},{256,384},{320,448},{384,0},{... | collective-permute-start | bytes 165896 | tf_op jit(solution)/shard_map/ppermute | solution.py:173
  280.0 17.3 %collective-permute-start.17 = (bf16[12,2304]{1,0:T(8,128)(2,1)S(1)}, bf16[12,2304]{1,0:T(8,128)(2,1)S(1)}, u32[]{:S(2)}, u32[]{:S(2)}) collective-permute-start(bf16[12,2304]{1,0:T(8,128)(2,1)S(1)} %get-tuple-element.21), channel_id=1, source_target_pairs={{0,64},{64,128},{128,192},{192,256},{256,320},{320,384},{384,448},... | collective-permute-start | bytes 165896 | tf_op jit(solution)/shard_map/ppermute | solution.py:173
  297.5 6.0 %copy-start.17 = (s32[16,2]{0,1:T(2,128)S(1)}, s32[16,2]{0,1:T(2,128)}, u32[]{:S(2)}) copy-start(s32[16,2]{0,1:T(2,128)} %param.28) | copy-start | bytes 388
  298.5 17.4 %all-to-all-start.2 = ((bf16[16,6,2304]{2,1,0:T(8,128)(2,1)}), bf16[16,6,2304]{2,1,0:T(8,128)(2,1)S(1)}, u32[]{:S(2)}, u32[]{:S(2)}) async-start(bf16[16,6,2304]{2,1,0:T(8,128)(2,1)} %all_to_all.18), calls=%async_computation.2 | async-start | bytes 1179648 | tf_op jit(solution)/shard_map/all_to_all | solution.py:180
  316.1 1.3 copy-start.7
  316.8 0.8 copy-start.14
Sparse Core Ops, SparseCore 0:
  10.1 194.0 all-gather.1

commit v3 on v1

--- a/solution.py
+++ b/solution.py
@@ -73,12 +73,10 @@
     routes,
     next_gain,
 ):
-    held = lax.all_gather(
-        jnp.stack([gate_proj[0], up_proj[0], down_proj[0]]), "zz", axis=1, tiled=True
-    )
+    held = lax.all_gather(jnp.stack([gate_proj[0], up_proj[0]]), "zz", axis=1, tiled=True)
+    down_held = lax.all_gather(down_proj[0], "zz", axis=0, tiled=True)
     gate_held = held[0]
     up_held = held[1]
-    down_held = held[2]
     heads_here = queries.shape[1] // HD
     attended = paged_attention(
         queries,

time: 312 us -> 323 us (1.035)
  the two profiles are of different devices: /device:TPU:64 before, /device:TPU:32 now
where the time goes in v3:
time: 323 us; the launch traced here: 322 us
  waiting for transfers between devices  146 us (45%)
  blocking collectives  62.1 us (19%)
  starting transfers between devices  39.3 us (12%)
  other arithmetic  22.3 us (7%)
  local copies, waits for them, and re-layouts  21.8 us (7%)
  matrix products  15.5 us (5%)
  between operations  14.6 us (5%)
    all_to_all x1, blocking collectives, on_device(): lax.all_to_all(arrived.reshape(n_zz, piece, model_width), 'zz', split_axi...  62.1 us
    all_gather x1, waiting for transfers between devices, on_device(): down_held = lax.all_gather(down_proj[0], 'zz', axis=0, tiled=True)  50.6 us
    all_to_all x1, waiting for transfers between devices, on_device(): lax.all_to_all(summed, 'zz', split_axis=0, concat_axis=0, tiled=True)  31.7 us
    all_to_all x1, waiting for transfers between devices, on_device(): lax.all_to_all(partial_proj.reshape(expert_count, own_rows, partial_proj....  18.2 us
    ppermute x1, waiting for transfers between devices, on_device(): back_h = lax.ppermute(sum_c[1], 'h', swap)  12.2 us
    all_to_all x1, waiting for transfers between devices, on_device(): lax.all_to_all(outgoing.reshape(expert_devs * capacity, model_width), 'ex...  11.2 us
    all_to_all x1, waiting for transfers between devices, on_device(): lax.all_to_all(own_slots.reshape(slot_total, model_width), 'expert', spli...  10.4 us
    gather x3, other arithmetic, paged_attention(): offset = row_ids - starts[owning]  10.1 us
  transfers between devices with their start and end apart: 10, of which 9 were waited for; matrix products, arithmetic and copies ran while one was open for 13% of the time, Pallas kernels for 0%

profile of v3, /device:TPU:32, one launch (start us, length us, event | category | flops | bytes accessed | tf_op | source)
XLA Modules:
  0.0 322.1 jit_solution(10618253538408629677)
XLA Ops:
  7.2 2.1 pad_maximum_fusion.2
  9.3 0.7 copy.97
  10.2 0.7 bitcast_subtract_fusion.1
  11.1 1.3 gather_fusion
  13.1 0.7 reduce.23
  14.0 0.7 gather_fusion.1
  14.7 1.9 reshape.427
  16.7 0.7 gather_fusion.2
  17.4 1.9 reshape.428
  19.5 2.6 fusion.47
  22.6 0.6 fusion.21
  23.5 0.7 fusion.46
  24.4 4.5 %compare_select_fusion.4 = (s32[256,1]{0,1:T(1,128)S(1)}, s32[256,1]{0,1:T(1,128)S(1)}) fusion(s32[]{:T(128)} %bitcast.17, s32[]{:T(128)} %bitcast.18, s32[]{:T(128)} %bitcast.19, s32[]{:T(128)} %bitcast.20, s32[]{:T(128)} %bitcast.21, s32[]{:T(128)} %bitcast.23, s32[]{:T(128)} %bitcast.22, s32[256,1]{0,1:T(1,128)S(1)} %bitcast.101, s32[256,1]{0,1:T(1,128)S(1)} %bitcast.100), kind=kLoop, calls=%fused_computation.80 | loop fusion | flops 3584 | bytes 4124 | tf_op jit(solution)/shard_map/gather | solution.py:55
  28.9 5.6 %select_select_fusion = s32[256]{0:T(256)S(1)} fusion(pred[256]{0:T(512)(128)(4,1)S(1)} %get-tuple-element.10, pred[256]{0:T(512)(128)(4,1)S(1)} %get-tuple-element.9, pred[256]{0:T(512)(128)(4,1)S(1)} %get-tuple-element.8, pred[256]{0:T(512)(128)(4,1)S(1)} %get-tuple-element.7, pred[256]{0:T(512)(128)(4,1)S(1)} %get-tuple-element.6, ...), kind=kLoop, calls=%fused_computation.94 | loop fusion | flops 2304 | bytes 4388 | tf_op jit(solution)/shard_map/gather | solution.py:55
  34.5 1.7 gather_fusion.3
  36.2 1.5 convolution_convert_fusion.1
  37.7 7.2 %all-to-all-start = ((bf16[16,16,2304]{2,1,0:T(8,128)(2,1)}), bf16[16,16,2304]{2,1,0:T(8,128)(2,1)S(1)}, u32[]{:S(2)}, u32[]{:S(2)}) async-start(bf16[16,16,2304]{2,1,0:T(8,128)(2,1)} %bitcast.27), calls=%async_computation | async-start | bytes 2359296 | tf_op jit(solution)/shard_map/all_to_all | solution.py:95
  45.9 18.2 %all-to-all-done = bf16[16,16,2304]{2,1,0:T(8,128)(2,1)S(1)} async-done(((bf16[16,16,2304]{2,1,0:T(8,128)(2,1)}), bf16[16,16,2304]{2,1,0:T(8,128)(2,1)S(1)}, u32[]{:S(2)}, u32[]{:S(2)}) %all-to-all-start) | async-done | bytes 1179680 | tf_op jit(solution)/shard_map/all_to_all | solution.py:95
  65.5 0.8 broadcast_in_dim.25
  66.3 3.6 %all-to-all-start.1 = ((bf16[16,6,2304]{2,1,0:T(8,128)(2,1)}), bf16[16,6,2304]{2,1,0:T(8,128)(2,1)S(1)}, u32[]{:S(2)}, u32[]{:S(2)}) async-start(bf16[16,6,2304]{2,1,0:T(8,128)(2,1)} %bitcast.28), calls=%async_computation.1 | async-start | bytes 1179648 | tf_op jit(solution)/shard_map/all_to_all | solution.py:127
  70.0 0.7 all-gather.6.cloned.1.call-update
  70.7 11.2 %all-to-all-done.1 = bf16[16,6,2304]{2,1,0:T(8,128)(2,1)S(1)} async-done(((bf16[16,6,2304]{2,1,0:T(8,128)(2,1)}), bf16[16,6,2304]{2,1,0:T(8,128)(2,1)S(1)}, u32[]{:S(2)}, u32[]{:S(2)}) %all-to-all-start.1) | async-done | bytes 442400 | tf_op jit(solution)/shard_map/all_to_all | solution.py:127
  82.0 62.1 %all_to_all.33 = bf16[8,12,2304]{2,1,0:T(8,128)(2,1)S(1)} all-to-all(bf16[8,12,2304]{2,1,0:T(8,128)(2,1)S(1)} %reshape.295), channel_id=1, replica_groups=mesh['zz'=8,'h'=2,'c'=2,'expert'=16] {'zz'}, dimensions={0} | all-to-all | bytes 884736 | tf_op jit(solution)/shard_map/all_to_all | solution.py:139
  144.2 8.7 %collective-permute-start = (bf16[8,12,2304]{2,0,1:T(8,128)(2,1)S(1)}, bf16[8,12,2304]{2,0,1:T(8,128)(2,1)S(1)}, u32[]{:S(2)}, u32[]{:S(2)}) collective-permute-start(bf16[8,12,2304]{2,0,1:T(8,128)(2,1)S(1)} %copy.105), channel_id=1, source_target_pairs={{0,32},{32,0},{1,33},{33,1},{2,34},{34,2},{3,35},{35,3},{4,36},{36... | collective-permute-start | bytes 1327112 | tf_op jit(solution)/shard_map/ppermute | solution.py:143
  152.9 8.0 %collective-permute-done = bf16[8,12,2304]{2,0,1:T(8,128)(2,1)S(1)} collective-permute-done((bf16[8,12,2304]{2,0,1:T(8,128)(2,1)S(1)}, bf16[8,12,2304]{2,0,1:T(8,128)(2,1)S(1)}, u32[]{:S(2)}, u32[]{:S(2)}) %collective-permute-start) | collective-permute-done | bytes 442400 | tf_op jit(solution)/shard_map/ppermute | solution.py:143
  161.5 2.1 collective-permute-start.1
  163.6 2.2 collective-permute-done.1
  166.3 1.5 reshape.296
  167.8 4.4 %fusion.1 = f32[384,512]{1,0:T(8,128)} fusion(bf16[384,2304]{1,0:T(8,128)(2,1)} %reshape.296, bf16[2,512,2304]{2,1,0:T(8,128)(2,1)} %all-gather.4.cloned.1.call-done), kind=kOutput, calls=%fused_computation.12 | convolution fusion | flops 905969664 | bytes 4915200 | tf_op jit(solution)/shard_map/dot_general | solution.py:148
  172.2 50.6 %all-gather.6.cloned.1.call-done = bf16[1,512,2304]{2,1,0:T(8,128)(2,1)} async-done(((bf16[1,64,2304]{2,1,0:T(8,128)(2,1)}), bf16[1,512,2304]{2,1,0:T(8,128)(2,1)}) %all-gather.6.cloned.1.call-update) | async-done | bytes 2359312 | tf_op jit(solution)/shard_map/all_gather | solution.py:77
  222.8 6.1 %convolution_convert_fusion = bf16[384,2304]{1,0:T(8,128)(2,1)} fusion(bf16[1,512,2304]{2,1,0:T(8,128)(2,1)} %all-gather.6.cloned.1.call-done, bf16[384,2304]{1,0:T(8,128)(2,1)S(1)} %copy-done.3, bf16[2,512,2304]{2,1,0:T(8,128)(2,1)} %all-gather.4.cloned.1.call-done, f32[384,512]{1,0:T(8,128)} %fusion.1), kind=kOutput, calls=%fused_computation.6 | convolution fusion | flops 1814003712 | bytes 9043968 | tf_op jit(solution)/shard_map/dot_general | solution.py:155
  228.9 2.8 fusion.45
  231.9 1.2 copy.109
  233.1 1.9 collective-permute-start.2
  235.0 1.5 reshape.300
  236.5 1.2 collective-permute-done.2
  237.7 1.4 add_convert_fusion
  239.4 1.9 collective-permute-start.3
  241.4 12.2 %collective-permute-done.3 = bf16[8,12,2304]{2,0,1:T(8,128)(2,1)S(1)} collective-permute-done((bf16[8,12,2304]{2,0,1:T(8,128)(2,1)S(1)}, bf16[8,12,2304]{2,0,1:T(8,128)(2,1)S(1)}, u32[]{:S(2)}, u32[]{:S(2)}) %collective-permute-start.3) | collective-permute-done | bytes 442400 | tf_op jit(solution)/shard_map/ppermute | solution.py:159
  253.5 0.9 fusion.24
  254.5 7.2 %all-to-all-start.3 = ((bf16[8,12,2304]{2,1,0:T(8,128)(2,1)}), bf16[8,12,2304]{2,1,0:T(8,128)(2,1)S(1)}, u32[]{:S(2)}, u32[]{:S(2)}) async-start(bf16[8,12,2304]{2,1,0:T(8,128)(2,1)} %fusion.24), calls=%async_computation.3 | async-start | bytes 1179648 | tf_op jit(solution)/shard_map/all_to_all | solution.py:161
  262.3 0.7 gather_fusion.5
  263.1 31.7 %all-to-all-done.3 = bf16[8,12,2304]{2,1,0:T(8,128)(2,1)S(1)} async-done(((bf16[8,12,2304]{2,1,0:T(8,128)(2,1)}), bf16[8,12,2304]{2,1,0:T(8,128)(2,1)S(1)}, u32[]{:S(2)}, u32[]{:S(2)}) %all-to-all-start.3) | async-done | bytes 442400 | tf_op jit(solution)/shard_map/all_to_all | solution.py:161
  294.9 1.0 all_to_all.26
  295.8 6.6 %all-to-all-start.4 = ((bf16[16,6,2304]{2,1,0:T(8,128)(2,1)}), bf16[16,6,2304]{2,1,0:T(8,128)(2,1)S(1)}, u32[]{:S(2)}, u32[]{:S(2)}) async-start(bf16[16,6,2304]{2,1,0:T(8,128)(2,1)} %all_to_all.26), calls=%async_computation.4 | async-start | bytes 1179648 | tf_op jit(solution)/shard_map/all_to_all | solution.py:162
  302.5 10.4 %all-to-all-done.4 = bf16[16,6,2304]{2,1,0:T(8,128)(2,1)S(1)} async-done(((bf16[16,6,2304]{2,1,0:T(8,128)(2,1)}), bf16[16,6,2304]{2,1,0:T(8,128)(2,1)S(1)}, u32[]{:S(2)}, u32[]{:S(2)}) %all-to-all-start.4) | async-done | bytes 442400 | tf_op jit(solution)/shard_map/all_to_all | solution.py:162
  313.1 0.7 gather_fusion.4
  314.6 0.7 multiply_convert_fusion
  (110 shorter events, 8.1 us)
Async XLA Ops:
  7.2 6.8 %copy-start = (bf16[32,128,128]{2,1,0:T(8,128)(2,1)S(1)}, bf16[32,128,128]{2,1,0:T(8,128)(2,1)}, u32[]{:S(2)}) copy-start(bf16[32,128,128]{2,1,0:T(8,128)(2,1)} %param.17) | copy-start | bytes 3145732
  7.2 3.9 %copy-start.1 = (bf16[256,128]{1,0:T(8,128)(2,1)S(1)}, bf16[256,128]{1,0:T(8,128)(2,1)}, u32[]{:S(2)}) copy-start(bf16[256,128]{1,0:T(8,128)(2,1)} %param.16) | copy-start | bytes 196612
  7.2 5.9 %copy-start.19 = (s32[1,32]{1,0:T(1,128)S(1)}, s32[1,32]{1,0:T(1,128)}, u32[]{:S(2)}) copy-start(s32[1,32]{1,0:T(1,128)} %param.21) | copy-start | bytes 388
  7.2 160.6 %all-gather.4.cloned.1.call-start = ((), (), s32[]{:S(2)}) async-start(), calls=%async_computation.5 | async-start | bytes 5308416 | tf_op jit(solution)/shard_map/all_gather | solution.py:76
  14.7 1.9 copy-start.4
  17.4 1.9 copy-start.15
  19.5 3.1 copy-start.2
  22.6 1.7 copy-start.16
  23.1 13.0 %copy-start.9 = (bf16[128,2304]{1,0:T(8,128)(2,1)S(1)}, bf16[128,2304]{1,0:T(8,128)(2,1)}, u32[]{:S(2)}) copy-start(bf16[128,2304]{1,0:T(8,128)(2,1)} %param.22) | copy-start | bytes 1769476
  36.2 8.7 %copy-start.13 = (s32[16,2]{0,1:T(2,128)S(1)}, s32[16,2]{0,1:T(2,128)}, u32[]{:S(2)}) copy-start(s32[16,2]{0,1:T(2,128)} %param.28) | copy-start | bytes 388
  37.7 26.6 %copy-start.5 = (bf16[16,2304]{1,0:T(8,128)(2,1)S(1)}, bf16[16,2304]{1,0:T(8,128)(2,1)}, u32[]{:S(2)}) copy-start(bf16[16,2304]{1,0:T(8,128)(2,1)} %param.15) | copy-start | bytes 221188
  37.7 26.8 %copy-start.11 = (f32[2304]{0:T(1024)S(1)}, f32[2304]{0:T(1024)}, u32[]{:S(2)}) copy-start(f32[2304]{0:T(1024)} %param.23) | copy-start | bytes 27652
  37.7 26.4 %all-to-all-start = ((bf16[16,16,2304]{2,1,0:T(8,128)(2,1)}), bf16[16,16,2304]{2,1,0:T(8,128)(2,1)S(1)}, u32[]{:S(2)}, u32[]{:S(2)}) async-start(bf16[16,16,2304]{2,1,0:T(8,128)(2,1)} %bitcast.27), calls=%async_computation | async-start | bytes 2359296 | tf_op jit(solution)/shard_map/all_to_all | solution.py:95
  45.4 0.5 copy-start.17
  64.6 0.6 copy-start.7
  66.3 15.6 %all-to-all-start.1 = ((bf16[16,6,2304]{2,1,0:T(8,128)(2,1)}), bf16[16,6,2304]{2,1,0:T(8,128)(2,1)S(1)}, u32[]{:S(2)}, u32[]{:S(2)}) async-start(bf16[16,6,2304]{2,1,0:T(8,128)(2,1)} %bitcast.28), calls=%async_computation.1 | async-start | bytes 1179648 | tf_op jit(solution)/shard_map/all_to_all | solution.py:127
  69.9 152.9 %all-gather.6.cloned.1.call-start = ((), (), s32[]{:S(2)}) async-start(), calls=%async_computation.6 | async-start | bytes 2654208 | tf_op jit(solution)/shard_map/all_gather | solution.py:77
  144.2 16.7 %collective-permute-start = (bf16[8,12,2304]{2,0,1:T(8,128)(2,1)S(1)}, bf16[8,12,2304]{2,0,1:T(8,128)(2,1)S(1)}, u32[]{:S(2)}, u32[]{:S(2)}) collective-permute-start(bf16[8,12,2304]{2,0,1:T(8,128)(2,1)S(1)} %copy.105), channel_id=1, source_target_pairs={{0,32},{32,0},{1,33},{33,1},{2,34},{34,2},{3,35},{35,3},{4,36},{36... | collective-permute-start | bytes 1327112 | tf_op jit(solution)/shard_map/ppermute | solution.py:143
  161.5 4.3 %collective-permute-start.1 = (bf16[2,8,12,2304]{3,1,2,0:T(8,128)(2,1)S(1)}, bf16[2,8,12,2304]{3,1,2,0:T(8,128)(2,1)S(1)}, u32[]{:S(2)}, u32[]{:S(2)}) collective-permute-start(bf16[2,8,12,2304]{3,1,2,0:T(8,128)(2,1)S(1)} %copy.107), channel_id=1, source_target_pairs={{0,16},{16,0},{1,17},{17,1},{2,18},{18,2},{3,19},{19,3},{4,20},{20... | collective-permute-start | bytes 2654216 | tf_op jit(solution)/shard_map/ppermute | solution.py:145
  167.8 55.0 %copy-start.3 = (bf16[384,2304]{1,0:T(8,128)(2,1)S(1)}, bf16[384,2304]{1,0:T(8,128)(2,1)}, u32[]{:S(2)}) copy-start(bf16[384,2304]{1,0:T(8,128)(2,1)} %reshape.296) | copy-start | bytes 5308420
  233.1 4.7 %collective-permute-start.2 = (bf16[2,8,12,2304]{3,1,2,0:T(8,128)(2,1)}, bf16[2,8,12,2304]{3,1,2,0:T(8,128)(2,1)}, u32[]{:S(2)}, u32[]{:S(2)}) collective-permute-start(bf16[2,8,12,2304]{3,1,2,0:T(8,128)(2,1)} %copy.109), channel_id=1, source_target_pairs={{0,16},{16,0},{1,17},{17,1},{2,18},{18,2},{3,19},{19,3},{4,20},{20... | collective-permute-start | bytes 2654216 | tf_op jit(solution)/shard_map/ppermute | solution.py:157
  239.2 22.5 %copy-start.14 = (s32[16,2]{0,1:T(2,128)S(1)}, s32[16,2]{0,1:T(2,128)}, u32[]{:S(2)}) copy-start(s32[16,2]{0,1:T(2,128)} %param.28) | copy-start | bytes 388
  239.3 22.8 %copy-start.18 = (s32[32]{0:T(128)S(1)}, s32[32]{0:T(128)}, u32[]{:S(2)}) copy-start(s32[32]{0:T(128)} %copy-done.17) | copy-start | bytes 388
  239.3 22.9 %copy-start.8 = (bf16[16,2304]{1,0:T(8,128)(2,1)S(1)}, bf16[16,2304]{1,0:T(8,128)(2,1)}, u32[]{:S(2)}) copy-start(bf16[16,2304]{1,0:T(8,128)(2,1)} %copy-done.7) | copy-start | bytes 221188
  239.3 22.9 %copy-start.10 = (bf16[2304,8]{0,1:T(8,128)(2,1)S(1)}, bf16[2304,8]{0,1:T(8,128)(2,1)}, u32[]{:S(2)}) copy-start(bf16[2304,8]{0,1:T(8,128)(2,1)} %param.24) | copy-start | bytes 110596
  239.4 14.1 %collective-permute-start.3 = (bf16[8,12,2304]{2,0,1:T(8,128)(2,1)S(1)}, bf16[8,12,2304]{2,0,1:T(8,128)(2,1)S(1)}, u32[]{:S(2)}, u32[]{:S(2)}) collective-permute-start(bf16[8,12,2304]{2,0,1:T(8,128)(2,1)S(1)} %copy.111), channel_id=1, source_target_pairs={{0,32},{32,0},{1,33},{33,1},{2,34},{34,2},{3,35},{35,3},{4,36},{36... | collective-permute-start | bytes 1327112 | tf_op jit(solution)/shard_map/ppermute | solution.py:159
  254.5 40.4 %all-to-all-start.3 = ((bf16[8,12,2304]{2,1,0:T(8,128)(2,1)}), bf16[8,12,2304]{2,1,0:T(8,128)(2,1)S(1)}, u32[]{:S(2)}, u32[]{:S(2)}) async-start(bf16[8,12,2304]{2,1,0:T(8,128)(2,1)} %fusion.24), calls=%async_computation.3 | async-start | bytes 1179648 | tf_op jit(solution)/shard_map/all_to_all | solution.py:161
  295.8 17.1 %all-to-all-start.4 = ((bf16[16,6,2304]{2,1,0:T(8,128)(2,1)}), bf16[16,6,2304]{2,1,0:T(8,128)(2,1)S(1)}, u32[]{:S(2)}, u32[]{:S(2)}) async-start(bf16[16,6,2304]{2,1,0:T(8,128)(2,1)} %all_to_all.26), calls=%async_computation.4 | async-start | bytes 1179648 | tf_op jit(solution)/shard_map/all_to_all | solution.py:162
  313.1 1.3 copy-start.6
  313.1 1.5 copy-start.12
Sparse Core Ops, SparseCore 0:
  10.1 138.9 all-gather.3
  151.2 71.5 all-gather.5

commit v4 on v1

--- a/solution.py
+++ b/solution.py
@@ -158,9 +158,17 @@
     partial = partial.reshape(n_c, n_h, n_zz, piece, model_width)
     back_c = lax.ppermute(partial[1], "c", swap)
     sum_c = (partial[0].astype(jnp.float32) + back_c.astype(jnp.float32)).astype(jnp.bfloat16)
-    back_h = lax.ppermute(sum_c[1], "h", swap)
-    summed = (sum_c[0].astype(jnp.float32) + back_h.astype(jnp.float32)).astype(jnp.bfloat16)
-    own_slots = lax.all_to_all(summed, "zz", split_axis=0, concat_axis=0, tiled=True)
+    by_dest = jnp.where(lax.axis_index("h") == 0, sum_c, sum_c[::-1]).transpose(1, 0, 2, 3)
+    both_back = lax.all_to_all(
+        by_dest.reshape(n_zz * n_h, piece, model_width),
+        ("zz", "h"),
+        split_axis=0,
+        concat_axis=0,
+        tiled=True,
+    )
+    own_slots = jnp.sum(
+        both_back.reshape(n_zz, n_h, piece, model_width).astype(jnp.float32), axis=1
+    ).astype(jnp.bfloat16)
     returned = lax.all_to_all(
         own_slots.reshape(slot_total, model_width), "expert", split_axis=0, concat_axis=0, tiled=True
     ).astype(jnp.float32)

time: 312 us -> 319 us (1.022)
  the two profiles are of different devices: /device:TPU:64 before, /device:TPU:32 now
where the time goes in v4:
time: 319 us; the launch traced here: 318 us
  waiting for transfers between devices  135 us (42%)
  blocking collectives  79.1 us (25%)
  starting transfers between devices  30.8 us (10%)
  other arithmetic  21.5 us (7%)
  local copies, waits for them, and re-layouts  21.2 us (7%)
  matrix products  15.3 us (5%)
  between operations  14.6 us (5%)
    all_to_all x1, blocking collectives, on_device(): lax.all_to_all(arrived.reshape(n_zz, piece, model_width), 'zz', split_axi...  63.8 us
    all_to_all x1, waiting for transfers between devices, on_device(): lax.all_to_all(by_dest.reshape(n_zz * n_h, piece, model_width), ('zz', 'h...  54 us
    ppermute x1, waiting for transfers between devices, on_device(): from_h = lax.ppermute(sent, 'h', swap)  32.4 us
    all_to_all x1, waiting for transfers between devices, on_device(): lax.all_to_all(partial_proj.reshape(expert_count, own_rows, partial_proj....  18.2 us
    all_gather x1, waiting for transfers between devices, on_device(): lax.all_gather(jnp.stack([gate_proj[0], up_proj[0], down_proj[0]]), 'zz',...  16.8 us
    all_to_all x1, blocking collectives, on_device(): lax.all_to_all(outgoing.reshape(expert_devs * capacity, model_width), 'ex...  15.4 us
    all_to_all x1, waiting for transfers between devices, on_device(): lax.all_to_all(own_slots.reshape(slot_total, model_width), 'expert', spli...  10.4 us
    gather x3, other arithmetic, paged_attention(): offset = row_ids - starts[owning]  10.3 us
  transfers between devices with their start and end apart: 7, of which 7 were waited for; matrix products, arithmetic and copies ran while one was open for 11% of the time, Pallas kernels for 0%

profile of v4, /device:TPU:32, one launch (start us, length us, event | category | flops | bytes accessed | tf_op | source)
XLA Modules:
  0.0 317.8 jit_solution(15344442360777546170)
XLA Ops:
  7.3 2.2 pad_maximum_fusion.2
  9.9 1.3 gather_fusion
  11.4 0.5 broadcast.418
  11.9 0.7 reduce.24
  12.8 0.7 gather_fusion.1
  13.6 1.8 reshape.431
  15.4 0.7 gather_fusion.2
  16.2 1.9 reshape.432
  18.3 2.6 fusion.48
  20.9 0.4 fusion.24
  21.4 0.5 fusion.20
  22.3 0.7 fusion.47
  23.2 4.4 %compare_select_fusion.4 = (s32[256,1]{0,1:T(1,128)S(1)}, s32[256,1]{0,1:T(1,128)S(1)}) fusion(s32[]{:T(128)} %bitcast.17, s32[]{:T(128)} %bitcast.18, s32[]{:T(128)} %bitcast.19, s32[]{:T(128)} %bitcast.20, s32[]{:T(128)} %bitcast.21, s32[]{:T(128)} %bitcast.23, s32[]{:T(128)} %bitcast.22, s32[256,1]{0,1:T(1,128)S(1)} %bitcast.100, s32[256,1]{0,1:T(1,128)S(1)} %bitcast.99), kind=kLoop, calls=%fused_computation.81 | loop fusion | flops 3584 | bytes 4124 | tf_op jit(solution)/shard_map/gather | solution.py:55
  27.6 5.8 %select_select_fusion = s32[256]{0:T(256)S(1)} fusion(pred[256]{0:T(512)(128)(4,1)S(1)} %get-tuple-element.10, pred[256]{0:T(512)(128)(4,1)S(1)} %get-tuple-element.9, pred[256]{0:T(512)(128)(4,1)S(1)} %get-tuple-element.8, pred[256]{0:T(512)(128)(4,1)S(1)} %get-tuple-element.7, pred[256]{0:T(512)(128)(4,1)S(1)} %get-tuple-element.6, ...), kind=kLoop, calls=%fused_computation.95 | loop fusion | flops 2304 | bytes 4388 | tf_op jit(solution)/shard_map/gather | solution.py:55
  33.4 1.7 gather_fusion.3
  35.1 1.5 convolution_convert_fusion.1
  36.6 7.2 %all-to-all-start = ((bf16[16,16,2304]{2,1,0:T(8,128)(2,1)}), bf16[16,16,2304]{2,1,0:T(8,128)(2,1)S(1)}, u32[]{:S(2)}, u32[]{:S(2)}) async-start(bf16[16,16,2304]{2,1,0:T(8,128)(2,1)} %bitcast.27), calls=%async_computation | async-start | bytes 2359296 | tf_op jit(solution)/shard_map/all_to_all | solution.py:97
  44.3 0.5 copy-done.17
  44.8 18.2 %all-to-all-done = bf16[16,16,2304]{2,1,0:T(8,128)(2,1)S(1)} async-done(((bf16[16,16,2304]{2,1,0:T(8,128)(2,1)}), bf16[16,16,2304]{2,1,0:T(8,128)(2,1)S(1)}, u32[]{:S(2)}, u32[]{:S(2)}) %all-to-all-start) | async-done | bytes 1179680 | tf_op jit(solution)/shard_map/all_to_all | solution.py:97
  63.6 0.5 copy-done.7
  64.4 15.4 %all_to_all.33 = bf16[16,6,2304]{2,1,0:T(8,128)(2,1)S(1)} all-to-all(bf16[16,6,2304]{2,1,0:T(8,128)(2,1)S(1)} %bitcast.97), channel_id=1, replica_groups=mesh['zz'=8,'h'=2,'c'=2,'expert'=16] {'expert'}, dimensions={0} | all-to-all | bytes 884736 | tf_op jit(solution)/shard_map/all_to_all | solution.py:129
  79.9 63.8 %all_to_all.34 = bf16[8,12,2304]{2,1,0:T(8,128)(2,1)S(1)} all-to-all(bf16[8,12,2304]{2,1,0:T(8,128)(2,1)S(1)} %reshape.299), channel_id=1, replica_groups=mesh['zz'=8,'h'=2,'c'=2,'expert'=16] {'zz'}, dimensions={0} | all-to-all | bytes 884736 | tf_op jit(solution)/shard_map/all_to_all | solution.py:141
  143.8 6.1 %collective-permute-start = (bf16[8,12,2304]{2,0,1:T(8,128)(2,1)S(1)}, bf16[8,12,2304]{2,0,1:T(8,128)(2,1)S(1)}, u32[]{:S(2)}, u32[]{:S(2)}) collective-permute-start(bf16[8,12,2304]{2,0,1:T(8,128)(2,1)S(1)} %copy.110), channel_id=1, source_target_pairs={{0,32},{32,0},{1,33},{33,1},{2,34},{34,2},{3,35},{35,3},{4,36},{36... | collective-permute-start | bytes 1327112 | tf_op jit(solution)/shard_map/ppermute | solution.py:145
  149.9 32.4 %collective-permute-done = bf16[8,12,2304]{2,0,1:T(8,128)(2,1)S(1)} collective-permute-done((bf16[8,12,2304]{2,0,1:T(8,128)(2,1)S(1)}, bf16[8,12,2304]{2,0,1:T(8,128)(2,1)S(1)}, u32[]{:S(2)}, u32[]{:S(2)}) %collective-permute-start) | collective-permute-done | bytes 442400 | tf_op jit(solution)/shard_map/ppermute | solution.py:145
  182.6 0.3 copy.112
  182.9 2.1 collective-permute-start.1
  185.0 2.2 collective-permute-done.1
  187.4 0.3 pad_maximum_fusion
  187.7 1.5 reshape.300
  189.2 16.8 %all-gather.2.cloned.1.call-done = bf16[3,512,2304]{2,1,0:T(8,128)(2,1)} async-done(((bf16[3,64,2304]{2,1,0:T(8,128)(2,1)}), bf16[3,512,2304]{2,1,0:T(8,128)(2,1)}) %all-gather.2.cloned.1.call-update) | async-done | bytes 7077904 | tf_op jit(solution)/shard_map/all_gather | solution.py:76
  206.0 4.3 %fusion.1 = f32[384,512]{1,0:T(8,128)} fusion(bf16[384,2304]{1,0:T(8,128)(2,1)} %reshape.300, bf16[3,512,2304]{2,1,0:T(8,128)(2,1)} %all-gather.2.cloned.1.call-done), kind=kOutput, calls=%fused_computation.13 | convolution fusion | flops 905969664 | bytes 4915200 | tf_op jit(solution)/shard_map/dot_general | solution.py:150
  210.3 6.1 %convolution_convert_fusion = bf16[384,2304]{1,0:T(8,128)(2,1)} fusion(bf16[3,512,2304]{2,1,0:T(8,128)(2,1)} %all-gather.2.cloned.1.call-done, bf16[384,2304]{1,0:T(8,128)(2,1)S(1)} %copy-done.3, f32[384,512]{1,0:T(8,128)} %fusion.1), kind=kOutput, calls=%fused_computation.6 | convolution fusion | flops 1814003712 | bytes 9043968 | tf_op jit(solution)/shard_map/dot_general | solution.py:157
  216.4 2.8 fusion.46
  219.4 1.2 copy.114
  220.6 1.9 collective-permute-start.2
  222.5 1.5 reshape.306
  224.1 1.2 collective-permute-done.2
  225.3 1.4 add_convert_fusion
  226.9 1.1 copy.128
  228.0 6.5 %all-to-all-start.3 = ((bf16[16,12,2304]{2,1,0:T(8,128)(2,1)}), bf16[16,12,2304]{2,1,0:T(8,128)(2,1)S(1)}, u32[]{:S(2)}, u32[]{:S(2)}) async-start(bf16[16,12,2304]{2,1,0:T(8,128)(2,1)} %bitcast.37), calls=%async_computation.3 | async-start | bytes 2359296 | tf_op jit(solution)/shard_map/all_to_all | solution.py:162
  235.1 0.7 gather_fusion.5
  236.0 54.0 %all-to-all-done.3 = bf16[16,12,2304]{2,1,0:T(8,128)(2,1)S(1)} async-done(((bf16[16,12,2304]{2,1,0:T(8,128)(2,1)}), bf16[16,12,2304]{2,1,0:T(8,128)(2,1)S(1)}, u32[]{:S(2)}, u32[]{:S(2)}) %all-to-all-start.3) | async-done | bytes 884768 | tf_op jit(solution)/shard_map/all_to_all | solution.py:162
  290.2 1.0 all_to_all.26
  291.2 6.9 %all-to-all-start.4 = ((bf16[16,6,2304]{2,1,0:T(8,128)(2,1)}), bf16[16,6,2304]{2,1,0:T(8,128)(2,1)S(1)}, u32[]{:S(2)}, u32[]{:S(2)}) async-start(bf16[16,6,2304]{2,1,0:T(8,128)(2,1)} %all_to_all.26), calls=%async_computation.4 | async-start | bytes 1179648 | tf_op jit(solution)/shard_map/all_to_all | solution.py:172
  298.2 10.4 %all-to-all-done.4 = bf16[16,6,2304]{2,1,0:T(8,128)(2,1)S(1)} async-done(((bf16[16,6,2304]{2,1,0:T(8,128)(2,1)}), bf16[16,6,2304]{2,1,0:T(8,128)(2,1)S(1)}, u32[]{:S(2)}, u32[]{:S(2)}) %all-to-all-start.4) | async-done | bytes 442400 | tf_op jit(solution)/shard_map/all_to_all | solution.py:172
  308.8 0.7 gather_fusion.4
  309.7 0.4 multiply_reduce_fusion
  310.3 0.7 multiply_convert_fusion
  (104 shorter events, 5.5 us)
Async XLA Ops:
  7.2 5.6 %copy-start = (bf16[32,128,128]{2,1,0:T(8,128)(2,1)S(1)}, bf16[32,128,128]{2,1,0:T(8,128)(2,1)}, u32[]{:S(2)}) copy-start(bf16[32,128,128]{2,1,0:T(8,128)(2,1)} %param.17) | copy-start | bytes 3145732
  7.2 2.3 copy-start.16
  7.2 2.7 copy-start.1
  7.2 4.7 %copy-start.19 = (s32[1,32]{1,0:T(1,128)S(1)}, s32[1,32]{1,0:T(1,128)}, u32[]{:S(2)}) copy-start(s32[1,32]{1,0:T(1,128)} %param.21) | copy-start | bytes 388
  7.2 198.8 %all-gather.2.cloned.1.call-start = ((), (), s32[]{:S(2)}) async-start(), calls=%async_computation.5 | async-start | bytes 7962624 | tf_op jit(solution)/shard_map/all_gather | solution.py:76
  13.6 1.8 copy-start.4
  16.2 1.9 copy-start.15
  18.3 3.1 copy-start.2
  21.9 13.2 %copy-start.9 = (bf16[128,2304]{1,0:T(8,128)(2,1)S(1)}, bf16[128,2304]{1,0:T(8,128)(2,1)}, u32[]{:S(2)}) copy-start(bf16[128,2304]{1,0:T(8,128)(2,1)} %param.22) | copy-start | bytes 1769476
  35.1 8.7 %copy-start.13 = (s32[16,2]{0,1:T(2,128)S(1)}, s32[16,2]{0,1:T(2,128)}, u32[]{:S(2)}) copy-start(s32[16,2]{0,1:T(2,128)} %param.28) | copy-start | bytes 388
  36.6 26.6 %copy-start.5 = (bf16[16,2304]{1,0:T(8,128)(2,1)S(1)}, bf16[16,2304]{1,0:T(8,128)(2,1)}, u32[]{:S(2)}) copy-start(bf16[16,2304]{1,0:T(8,128)(2,1)} %param.15) | copy-start | bytes 221188
  36.6 26.8 %copy-start.11 = (f32[2304]{0:T(1024)S(1)}, f32[2304]{0:T(1024)}, u32[]{:S(2)}) copy-start(f32[2304]{0:T(1024)} %param.23) | copy-start | bytes 27652
  36.6 26.4 %all-to-all-start = ((bf16[16,16,2304]{2,1,0:T(8,128)(2,1)}), bf16[16,16,2304]{2,1,0:T(8,128)(2,1)S(1)}, u32[]{:S(2)}, u32[]{:S(2)}) async-start(bf16[16,16,2304]{2,1,0:T(8,128)(2,1)} %bitcast.27), calls=%async_computation | async-start | bytes 2359296 | tf_op jit(solution)/shard_map/all_to_all | solution.py:97
  44.3 0.5 copy-start.17
  63.5 0.6 copy-start.7
  143.8 38.5 %collective-permute-start = (bf16[8,12,2304]{2,0,1:T(8,128)(2,1)S(1)}, bf16[8,12,2304]{2,0,1:T(8,128)(2,1)S(1)}, u32[]{:S(2)}, u32[]{:S(2)}) collective-permute-start(bf16[8,12,2304]{2,0,1:T(8,128)(2,1)S(1)} %copy.110), channel_id=1, source_target_pairs={{0,32},{32,0},{1,33},{33,1},{2,34},{34,2},{3,35},{35,3},{4,36},{36... | collective-permute-start | bytes 1327112 | tf_op jit(solution)/shard_map/ppermute | solution.py:145
  182.9 4.3 %collective-permute-start.1 = (bf16[2,8,12,2304]{3,1,2,0:T(8,128)(2,1)S(1)}, bf16[2,8,12,2304]{3,1,2,0:T(8,128)(2,1)S(1)}, u32[]{:S(2)}, u32[]{:S(2)}) collective-permute-start(bf16[2,8,12,2304]{3,1,2,0:T(8,128)(2,1)S(1)} %copy.112), channel_id=1, source_target_pairs={{0,16},{16,0},{1,17},{17,1},{2,18},{18,2},{3,19},{19,3},{4,20},{20... | collective-permute-start | bytes 2654216 | tf_op jit(solution)/shard_map/ppermute | solution.py:147
  189.2 21.1 %copy-start.3 = (bf16[384,2304]{1,0:T(8,128)(2,1)S(1)}, bf16[384,2304]{1,0:T(8,128)(2,1)}, u32[]{:S(2)}) copy-start(bf16[384,2304]{1,0:T(8,128)(2,1)} %reshape.300) | copy-start | bytes 5308420
  220.6 4.7 %collective-permute-start.2 = (bf16[2,8,12,2304]{3,1,2,0:T(8,128)(2,1)}, bf16[2,8,12,2304]{3,1,2,0:T(8,128)(2,1)}, u32[]{:S(2)}, u32[]{:S(2)}) collective-permute-start(bf16[2,8,12,2304]{3,1,2,0:T(8,128)(2,1)} %copy.114), channel_id=1, source_target_pairs={{0,16},{16,0},{1,17},{17,1},{2,18},{18,2},{3,19},{19,3},{4,20},{20... | collective-permute-start | bytes 2654216 | tf_op jit(solution)/shard_map/ppermute | solution.py:159
  228.0 6.6 %copy-start.14 = (s32[16,2]{0,1:T(2,128)S(1)}, s32[16,2]{0,1:T(2,128)}, u32[]{:S(2)}) copy-start(s32[16,2]{0,1:T(2,128)} %param.28) | copy-start | bytes 388
  228.0 6.9 %copy-start.18 = (s32[32]{0:T(128)S(1)}, s32[32]{0:T(128)}, u32[]{:S(2)}) copy-start(s32[32]{0:T(128)} %copy-done.17) | copy-start | bytes 388
  228.0 7.0 %copy-start.8 = (bf16[16,2304]{1,0:T(8,128)(2,1)S(1)}, bf16[16,2304]{1,0:T(8,128)(2,1)}, u32[]{:S(2)}) copy-start(bf16[16,2304]{1,0:T(8,128)(2,1)} %copy-done.7) | copy-start | bytes 221188
  228.0 7.0 %copy-start.10 = (bf16[2304,8]{0,1:T(8,128)(2,1)S(1)}, bf16[2304,8]{0,1:T(8,128)(2,1)}, u32[]{:S(2)}) copy-start(bf16[2304,8]{0,1:T(8,128)(2,1)} %param.24) | copy-start | bytes 110596
  228.0 62.0 %all-to-all-start.3 = ((bf16[16,12,2304]{2,1,0:T(8,128)(2,1)}), bf16[16,12,2304]{2,1,0:T(8,128)(2,1)S(1)}, u32[]{:S(2)}, u32[]{:S(2)}) async-start(bf16[16,12,2304]{2,1,0:T(8,128)(2,1)} %bitcast.37), calls=%async_computation.3 | async-start | bytes 2359296 | tf_op jit(solution)/shard_map/all_to_all | solution.py:162
  291.2 17.4 %all-to-all-start.4 = ((bf16[16,6,2304]{2,1,0:T(8,128)(2,1)}), bf16[16,6,2304]{2,1,0:T(8,128)(2,1)S(1)}, u32[]{:S(2)}, u32[]{:S(2)}) async-start(bf16[16,6,2304]{2,1,0:T(8,128)(2,1)} %all_to_all.26), calls=%async_computation.4 | async-start | bytes 1179648 | tf_op jit(solution)/shard_map/all_to_all | solution.py:172
  308.8 1.3 copy-start.6
  308.8 1.5 copy-start.12
Sparse Core Ops, SparseCore 0:
  10.1 195.8 all-gather.1

commit v5 on v1

--- a/solution.py
+++ b/solution.py
@@ -77,7 +77,6 @@
         jnp.stack([gate_proj[0], up_proj[0], down_proj[0]]), "zz", axis=1, tiled=True
     )
     gate_held = held[0]
-    up_held = held[1]
     down_held = held[2]
     heads_here = queries.shape[1] // HD
     attended = paged_attention(
@@ -134,8 +133,6 @@
         tiled=True,
     )
     n_zz = lax.axis_size("zz")
-    n_h = lax.axis_size("h")
-    n_c = lax.axis_size("c")
     slot_total = arrived.shape[0]
     piece = slot_total // n_zz
     sent = lax.all_to_all(
@@ -146,20 +143,28 @@
     both_h = jnp.stack([sent, from_h])
     from_c = lax.ppermute(both_h, "c", swap)
     rows_here = jnp.stack([both_h, from_c])
-    flat_rows = rows_here.reshape(n_c * n_h * n_zz * piece, model_width)
-    gate_val = lax.dot_general(
-        flat_rows, gate_held, (((1,), (1,)), ((), ())), preferred_element_type=jnp.float32
-    )
-    up_val = lax.dot_general(
-        flat_rows, up_held, (((1,), (1,)), ((), ())), preferred_element_type=jnp.float32
-    )
-    activated = (jax.nn.silu(gate_val) * up_val).astype(jnp.bfloat16)
-    partial = jnp.dot(activated, down_held, preferred_element_type=jnp.float32).astype(jnp.bfloat16)
-    partial = partial.reshape(n_c, n_h, n_zz, piece, model_width)
-    back_c = lax.ppermute(partial[1], "c", swap)
-    sum_c = (partial[0].astype(jnp.float32) + back_c.astype(jnp.float32)).astype(jnp.bfloat16)
-    back_h = lax.ppermute(sum_c[1], "h", swap)
-    summed = (sum_c[0].astype(jnp.float32) + back_h.astype(jnp.float32)).astype(jnp.bfloat16)
+    gate_up = held[:2].reshape(-1, model_width)
+    units = gate_held.shape[0]
+
+    def expert_part(rows):
+        flat_rows = rows.reshape(-1, model_width)
+        both = lax.dot_general(
+            flat_rows, gate_up, (((1,), (1,)), ((), ())), preferred_element_type=jnp.float32
+        )
+        activated = (jax.nn.silu(both[:, :units]) * both[:, units:]).astype(jnp.bfloat16)
+        part = jnp.dot(activated, down_held, preferred_element_type=jnp.float32)
+        return part.astype(jnp.bfloat16).reshape(rows.shape)
+
+    other_core = expert_part(rows_here[1])
+    back_c = lax.ppermute(other_core, "c", swap)
+    other_block = expert_part(rows_here[0, 1])
+    sum_other = (other_block.astype(jnp.float32) + back_c[1].astype(jnp.float32)).astype(
+        jnp.bfloat16
+    )
+    back_h = lax.ppermute(sum_other, "h", swap)
+    own = expert_part(rows_here[0, 0])
+    sum_own = (own.astype(jnp.float32) + back_c[0].astype(jnp.float32)).astype(jnp.bfloat16)
+    summed = (sum_own.astype(jnp.float32) + back_h.astype(jnp.float32)).astype(jnp.bfloat16)
     own_slots = lax.all_to_all(summed, "zz", split_axis=0, concat_axis=0, tiled=True)
     returned = lax.all_to_all(
         own_slots.reshape(slot_total, model_width), "expert", split_axis=0, concat_axis=0, tiled=True

time: 312 us -> 316 us (1.013)
  matrix products: 15.3 us -> 23.9 us
  local copies, waits for them, and re-layouts: 21.1 us -> 27.9 us
  blocking collectives: 84.8 us -> 80.7 us
  waiting for transfers between devices: 116 us -> 112 us
  other arithmetic: 22 us -> 18.7 us
    ppermute x2, waiting for transfers between devices: 11.7 us -> 2.65 us  [the longest x1 2.65 us: on_device(): back_h = lax.ppermute(sum_other, 'h', swap)]
    dot_general x2 -> x6, matrix products: 10.4 us -> 18.9 us  [the longest x3 9.48 us: expert_part(): part = jnp.dot(activated, down_held, preferred_element_type=jnp.float32)]
    all_gather x1, waiting for transfers between devices: 2.2 us -> 10.2 us  [on_device(): lax.all_gather(jnp.stack([gate_proj[0], up_proj[0], down_proj[0]]), 'zz',...]
    all_to_all x1, blocking collectives: 69.4 us -> 65.4 us  [on_device(): lax.all_to_all(arrived.reshape(n_zz, piece, model_width), 'zz', split_axi...]
    slice x0 -> x3, local copies, waits for them, and re-layouts: none -> 3.92 us  [the longest x1 2.64 us: on_device(): gate_up = held[:2].reshape(-1, model_width)]
    ppermute x1, waiting for transfers between devices: 37.3 us -> 33.6 us  [on_device(): from_h = lax.ppermute(sent, 'h', swap)]
  transfers between devices with their start and end apart: 8 -> 8, of which waited for: 8 -> 7; matrix products, arithmetic and copies ran while one was open for 11% -> 16% of each run, Pallas kernels for 0% -> 0%
where the time goes in v5:
time: 316 us; the launch traced here: 315 us
  waiting for transfers between devices  112 us (35%)
  blocking collectives  80.7 us (26%)
  starting transfers between devices  37.3 us (12%)
  local copies, waits for them, and re-layouts  27.9 us (9%)
  matrix products  23.9 us (8%)
  other arithmetic  18.7 us (6%)
  between operations  14.7 us (5%)
    all_to_all x1, blocking collectives, on_device(): lax.all_to_all(arrived.reshape(n_zz, piece, model_width), 'zz', split_axi...  65.4 us
    ppermute x1, waiting for transfers between devices, on_device(): from_h = lax.ppermute(sent, 'h', swap)  33.6 us
    all_to_all x1, waiting for transfers between devices, on_device(): lax.all_to_all(summed, 'zz', split_axis=0, concat_axis=0, tiled=True)  32.4 us
    all_to_all x1, waiting for transfers between devices, on_device(): lax.all_to_all(partial_proj.reshape(expert_count, own_rows, partial_proj....  18.2 us
    all_to_all x1, blocking collectives, on_device(): lax.all_to_all(outgoing.reshape(expert_devs * capacity, model_width), 'ex...  15.4 us
    all_to_all x1, waiting for transfers between devices, on_device(): lax.all_to_all(own_slots.reshape(slot_total, model_width), 'expert', spli...  12.3 us
    gather x3, other arithmetic, paged_attention(): offset = row_ids - starts[owning]  10.3 us
    all_gather x1, waiting for transfers between devices, on_device(): lax.all_gather(jnp.stack([gate_proj[0], up_proj[0], down_proj[0]]), 'zz',...  10.2 us
  transfers between devices with their start and end apart: 8, of which 7 were waited for; matrix products, arithmetic and copies ran while one was open for 16% of the time, Pallas kernels for 0%

profile of v5, /device:TPU:64, one launch (start us, length us, event | category | flops | bytes accessed | tf_op | source)
XLA Modules:
  0.0 314.8 jit_solution(10458365868849174473)
XLA Ops:
  7.3 2.2 pad_maximum_fusion.1
  10.0 0.7 reduce.23
  11.3 1.3 gather_fusion
  12.8 0.7 gather_fusion.2
  13.6 2.0 gather_fusion.1
  15.5 1.8 reshape.433
  17.4 1.9 reshape.434
  19.5 2.6 fusion.53
  22.5 0.5 fusion.18
  23.5 0.7 fusion.52
  24.3 4.4 %compare_select_fusion.4 = (s32[256,1]{0,1:T(1,128)S(1)}, s32[256,1]{0,1:T(1,128)S(1)}) fusion(s32[]{:T(128)} %bitcast.17, s32[]{:T(128)} %bitcast.18, s32[]{:T(128)} %bitcast.19, s32[]{:T(128)} %bitcast.20, s32[]{:T(128)} %bitcast.21, s32[]{:T(128)} %bitcast.23, s32[]{:T(128)} %bitcast.22, s32[256,1]{0,1:T(1,128)S(1)} %bitcast.99, s32[256,1]{0,1:T(1,128)S(1)} %bitcast.98), kind=kLoop, calls=%fused_computation.82 | loop fusion | flops 3584 | bytes 4124 | tf_op jit(solution)/shard_map/gather | solution.py:55
  28.8 5.8 %select_select_fusion = s32[256]{0:T(256)S(1)} fusion(pred[256]{0:T(512)(128)(4,1)S(1)} %get-tuple-element.10, pred[256]{0:T(512)(128)(4,1)S(1)} %get-tuple-element.9, pred[256]{0:T(512)(128)(4,1)S(1)} %get-tuple-element.8, pred[256]{0:T(512)(128)(4,1)S(1)} %get-tuple-element.7, pred[256]{0:T(512)(128)(4,1)S(1)} %get-tuple-element.6, ...), kind=kLoop, calls=%fused_computation.96 | loop fusion | flops 2304 | bytes 4388 | tf_op jit(solution)/shard_map/gather | solution.py:55
  34.6 1.7 gather_fusion.3
  36.3 1.5 convolution_convert_fusion
  37.8 7.2 %all-to-all-start = ((bf16[16,16,2304]{2,1,0:T(8,128)(2,1)}), bf16[16,16,2304]{2,1,0:T(8,128)(2,1)S(1)}, u32[]{:S(2)}, u32[]{:S(2)}) async-start(bf16[16,16,2304]{2,1,0:T(8,128)(2,1)} %bitcast.27), calls=%async_computation | async-start | bytes 2359296 | tf_op jit(solution)/shard_map/all_to_all | solution.py:96
  46.0 18.2 %all-to-all-done = bf16[16,16,2304]{2,1,0:T(8,128)(2,1)S(1)} async-done(((bf16[16,16,2304]{2,1,0:T(8,128)(2,1)}), bf16[16,16,2304]{2,1,0:T(8,128)(2,1)S(1)}, u32[]{:S(2)}, u32[]{:S(2)}) %all-to-all-start) | async-done | bytes 1179680 | tf_op jit(solution)/shard_map/all_to_all | solution.py:96
  65.6 15.4 %all_to_all.33 = bf16[16,6,2304]{2,1,0:T(8,128)(2,1)S(1)} all-to-all(bf16[16,6,2304]{2,1,0:T(8,128)(2,1)S(1)} %bitcast.96), channel_id=1, replica_groups=mesh['zz'=8,'h'=2,'c'=2,'expert'=16] {'expert'}, dimensions={0} | all-to-all | bytes 884736 | tf_op jit(solution)/shard_map/all_to_all | solution.py:128
  81.1 65.4 %all_to_all.34 = bf16[8,12,2304]{2,1,0:T(8,128)(2,1)S(1)} all-to-all(bf16[8,12,2304]{2,1,0:T(8,128)(2,1)S(1)} %reshape.299), channel_id=1, replica_groups=mesh['zz'=8,'h'=2,'c'=2,'expert'=16] {'zz'}, dimensions={0} | all-to-all | bytes 884736 | tf_op jit(solution)/shard_map/all_to_all | solution.py:138
  146.6 1.9 collective-permute-start
  148.6 33.6 %collective-permute-done = bf16[8,12,2304]{2,0,1:T(8,128)(2,1)S(1)} collective-permute-done((bf16[8,12,2304]{2,0,1:T(8,128)(2,1)S(1)}, bf16[8,12,2304]{2,0,1:T(8,128)(2,1)S(1)}, u32[]{:S(2)}, u32[]{:S(2)}) %collective-permute-start) | collective-permute-done | bytes 442400 | tf_op jit(solution)/shard_map/ppermute | solution.py:142
  182.7 1.9 collective-permute-start.1
  184.6 2.4 collective-permute-done.1
  187.1 1.1 reshape_squeeze_stack.3
  188.3 10.2 %all-gather.2.cloned.1.call-done = bf16[3,512,2304]{2,1,0:T(8,128)(2,1)} async-done(((bf16[3,64,2304]{2,1,0:T(8,128)(2,1)}), bf16[3,512,2304]{2,1,0:T(8,128)(2,1)}) %all-gather.2.cloned.1.call-update) | async-done | bytes 7077904 | tf_op jit(solution)/shard_map/all_gather | solution.py:76
  198.4 2.6 slice.86
  201.1 1.7 fusion.55
  203.3 3.3 %convolution_convert_fusion.1 = bf16[192,2304]{1,0:T(8,128)(2,1)} fusion(bf16[3,512,2304]{2,1,0:T(8,128)(2,1)} %all-gather.2.cloned.1.call-done, f32[192,1024]{1,0:T(8,128)S(1)} %fusion.55), kind=kOutput, calls=%fused_computation.7 | convolution fusion | flops 454017024 | bytes 4030464 | tf_op jit(solution)/shard_map/dot_general | solution.py:155
  206.6 1.3 reshape.301
  207.9 1.2 copy.111
  209.1 2.1 collective-permute-start.2
  211.5 3.9 %fusion.56 = f32[96,1024]{1,0:T(8,128)S(1)} fusion(bf16[96,2304]{1,0:T(8,128)(2,1)S(1)} %reshape_squeeze.11, bf16[1024,2304]{1,0:T(8,128)(2,1)} %bitcast.91), kind=kOutput, calls=%fused_computation.120 | convolution fusion | flops 452984832 | bytes 5554176 | tf_op jit(solution)/shard_map/dot_general | solution.py:151
  215.4 3.1 fusion.1
  218.5 1.3 reshape.307
  219.7 1.2 fusion.51
  221.2 8.2 %collective-permute-start.3 = (bf16[8,12,2304]{2,0,1:T(8,128)(2,1)S(1)}, bf16[8,12,2304]{2,0,1:T(8,128)(2,1)}, u32[]{:S(2)}, u32[]{:S(2)}) collective-permute-start(bf16[8,12,2304]{2,0,1:T(8,128)(2,1)S(1)} %copy.114), channel_id=1, source_target_pairs={{0,32},{32,0},{1,33},{33,1},{2,34},{34,2},{3,35},{35,3},{4,36},{36... | collective-permute-start | bytes 1327112 | tf_op jit(solution)/shard_map/ppermute | solution.py:164
  229.4 3.9 %fusion.54 = f32[96,1024]{1,0:T(8,128)S(1)} fusion(bf16[96,2304]{1,0:T(8,128)(2,1)S(1)} %reshape_squeeze.10, bf16[1024,2304]{1,0:T(8,128)(2,1)} %bitcast.92), kind=kOutput, calls=%fused_computation.118 | convolution fusion | flops 452984832 | bytes 5554176 | tf_op jit(solution)/shard_map/dot_general | solution.py:151
  233.3 3.1 fusion
  236.4 1.3 reshape.305
  237.7 2.6 collective-permute-done.3
  240.3 2.0 add_convert_fusion
  242.3 9.2 %all-to-all-start.3 = ((bf16[8,12,2304]{2,1,0:T(8,128)(2,1)}), bf16[8,12,2304]{2,1,0:T(8,128)(2,1)S(1)}, u32[]{:S(2)}, u32[]{:S(2)}) async-start(bf16[8,12,2304]{2,1,0:T(8,128)(2,1)} %add_convert_fusion), calls=%async_computation.3 | async-start | bytes 1179648 | tf_op jit(solution)/shard_map/all_to_all | solution.py:168
  252.1 0.7 gather_fusion.5
  253.0 32.4 %all-to-all-done.3 = bf16[8,12,2304]{2,1,0:T(8,128)(2,1)S(1)} async-done(((bf16[8,12,2304]{2,1,0:T(8,128)(2,1)}), bf16[8,12,2304]{2,1,0:T(8,128)(2,1)S(1)}, u32[]{:S(2)}, u32[]{:S(2)}) %all-to-all-start.3) | async-done | bytes 442400 | tf_op jit(solution)/shard_map/all_to_all | solution.py:168
  285.3 1.0 all_to_all.26
  286.3 6.9 %all-to-all-start.4 = ((bf16[16,6,2304]{2,1,0:T(8,128)(2,1)}), bf16[16,6,2304]{2,1,0:T(8,128)(2,1)S(1)}, u32[]{:S(2)}, u32[]{:S(2)}) async-start(bf16[16,6,2304]{2,1,0:T(8,128)(2,1)} %all_to_all.26), calls=%async_computation.4 | async-start | bytes 1179648 | tf_op jit(solution)/shard_map/all_to_all | solution.py:169
  293.3 12.3 %all-to-all-done.4 = bf16[16,6,2304]{2,1,0:T(8,128)(2,1)S(1)} async-done(((bf16[16,6,2304]{2,1,0:T(8,128)(2,1)}), bf16[16,6,2304]{2,1,0:T(8,128)(2,1)S(1)}, u32[]{:S(2)}, u32[]{:S(2)}) %all-to-all-start.4) | async-done | bytes 442400 | tf_op jit(solution)/shard_map/all_to_all | solution.py:169
  305.8 0.7 gather_fusion.4
  307.2 0.7 multiply_convert_fusion
  (113 shorter events, 8.6 us)
Async XLA Ops:
  7.2 5.6 %copy-start = (bf16[32,128,128]{2,1,0:T(8,128)(2,1)S(1)}, bf16[32,128,128]{2,1,0:T(8,128)(2,1)}, u32[]{:S(2)}) copy-start(bf16[32,128,128]{2,1,0:T(8,128)(2,1)} %param.18) | copy-start | bytes 3145732
  7.2 2.8 copy-start.19
  7.2 3.7 %copy-start.16 = (s32[1,16]{1,0:T(1,128)S(1)}, s32[1,16]{1,0:T(1,128)}, u32[]{:S(2)}) copy-start(s32[1,16]{1,0:T(1,128)} %param.19) | copy-start | bytes 196
  7.2 4.1 %copy-start.2 = (bf16[256,128]{1,0:T(8,128)(2,1)S(1)}, bf16[256,128]{1,0:T(8,128)(2,1)}, u32[]{:S(2)}) copy-start(bf16[256,128]{1,0:T(8,128)(2,1)} %param.16) | copy-start | bytes 196612
  7.2 191.2 %all-gather.2.cloned.1.call-start = ((), (), s32[]{:S(2)}) async-start(), calls=%async_computation.5 | async-start | bytes 7962624 | tf_op jit(solution)/shard_map/all_gather | solution.py:76
  17.4 1.9 copy-start.15
  19.5 3.1 copy-start.3
  23.1 13.2 %copy-start.9 = (bf16[128,2304]{1,0:T(8,128)(2,1)S(1)}, bf16[128,2304]{1,0:T(8,128)(2,1)}, u32[]{:S(2)}) copy-start(bf16[128,2304]{1,0:T(8,128)(2,1)} %param.22) | copy-start | bytes 1769476
  36.3 8.7 %copy-start.13 = (s32[16,2]{0,1:T(2,128)S(1)}, s32[16,2]{0,1:T(2,128)}, u32[]{:S(2)}) copy-start(s32[16,2]{0,1:T(2,128)} %param.28) | copy-start | bytes 388
  37.8 26.6 %copy-start.5 = (bf16[16,2304]{1,0:T(8,128)(2,1)S(1)}, bf16[16,2304]{1,0:T(8,128)(2,1)}, u32[]{:S(2)}) copy-start(bf16[16,2304]{1,0:T(8,128)(2,1)} %param.15) | copy-start | bytes 221188
  37.8 26.7 %copy-start.11 = (f32[2304]{0:T(1024)S(1)}, f32[2304]{0:T(1024)}, u32[]{:S(2)}) copy-start(f32[2304]{0:T(1024)} %param.23) | copy-start | bytes 27652
  37.8 26.4 %all-to-all-start = ((bf16[16,16,2304]{2,1,0:T(8,128)(2,1)}), bf16[16,16,2304]{2,1,0:T(8,128)(2,1)S(1)}, u32[]{:S(2)}, u32[]{:S(2)}) async-start(bf16[16,16,2304]{2,1,0:T(8,128)(2,1)} %bitcast.27), calls=%async_computation | async-start | bytes 2359296 | tf_op jit(solution)/shard_map/all_to_all | solution.py:96
  45.5 0.5 copy-start.17
  64.6 0.6 copy-start.7
  146.6 35.5 %collective-permute-start = (bf16[8,12,2304]{2,0,1:T(8,128)(2,1)S(1)}, bf16[8,12,2304]{2,0,1:T(8,128)(2,1)S(1)}, u32[]{:S(2)}, u32[]{:S(2)}) collective-permute-start(bf16[8,12,2304]{2,0,1:T(8,128)(2,1)S(1)} %copy.107), channel_id=1, source_target_pairs={{0,32},{32,0},{1,33},{33,1},{2,34},{34,2},{3,35},{35,3},{4,36},{36... | collective-permute-start | bytes 1327112 | tf_op jit(solution)/shard_map/ppermute | solution.py:142
  182.7 4.3 %collective-permute-start.1 = (bf16[2,8,12,2304]{3,1,2,0:T(8,128)(2,1)S(1)}, bf16[2,8,12,2304]{3,1,2,0:T(8,128)(2,1)S(1)}, u32[]{:S(2)}, u32[]{:S(2)}) collective-permute-start(bf16[2,8,12,2304]{3,1,2,0:T(8,128)(2,1)S(1)} %copy.109), channel_id=1, source_target_pairs={{0,16},{16,0},{1,17},{17,1},{2,18},{18,2},{3,19},{19,3},{4,20},{20... | collective-permute-start | bytes 2654216 | tf_op jit(solution)/shard_map/ppermute | solution.py:144
  188.3 12.8 %copy-start.4 = (bf16[192,2304]{1,0:T(8,128)(2,1)S(1)}, bf16[192,2304]{1,0:T(8,128)(2,1)}, u32[]{:S(2)}) copy-start(bf16[192,2304]{1,0:T(8,128)(2,1)} %reshape_squeeze_stack.3) | copy-start | bytes 2654212
  201.1 2.2 copy-start.1
  209.1 10.7 %collective-permute-start.2 = (bf16[2,8,12,2304]{3,1,2,0:T(8,128)(2,1)}, bf16[2,8,12,2304]{3,1,2,0:T(8,128)(2,1)}, u32[]{:S(2)}, u32[]{:S(2)}) collective-permute-start(bf16[2,8,12,2304]{3,1,2,0:T(8,128)(2,1)} %copy.111), channel_id=1, source_target_pairs={{0,16},{16,0},{1,17},{17,1},{2,18},{18,2},{3,19},{19,3},{4,20},{20... | collective-permute-start | bytes 2654216 | tf_op jit(solution)/shard_map/ppermute | solution.py:159
  221.2 19.1 %collective-permute-start.3 = (bf16[8,12,2304]{2,0,1:T(8,128)(2,1)S(1)}, bf16[8,12,2304]{2,0,1:T(8,128)(2,1)}, u32[]{:S(2)}, u32[]{:S(2)}) collective-permute-start(bf16[8,12,2304]{2,0,1:T(8,128)(2,1)S(1)} %copy.114), channel_id=1, source_target_pairs={{0,32},{32,0},{1,33},{33,1},{2,34},{34,2},{3,35},{35,3},{4,36},{36... | collective-permute-start | bytes 1327112 | tf_op jit(solution)/shard_map/ppermute | solution.py:164
  237.6 13.9 %copy-start.14 = (s32[16,2]{0,1:T(2,128)S(1)}, s32[16,2]{0,1:T(2,128)}, u32[]{:S(2)}) copy-start(s32[16,2]{0,1:T(2,128)} %param.28) | copy-start | bytes 388
  237.6 14.3 %copy-start.18 = (s32[32]{0:T(128)S(1)}, s32[32]{0:T(128)}, u32[]{:S(2)}) copy-start(s32[32]{0:T(128)} %copy-done.17) | copy-start | bytes 388
  237.7 14.3 %copy-start.8 = (bf16[16,2304]{1,0:T(8,128)(2,1)S(1)}, bf16[16,2304]{1,0:T(8,128)(2,1)}, u32[]{:S(2)}) copy-start(bf16[16,2304]{1,0:T(8,128)(2,1)} %copy-done.7) | copy-start | bytes 221188
  237.7 14.3 %copy-start.10 = (bf16[2304,8]{0,1:T(8,128)(2,1)S(1)}, bf16[2304,8]{0,1:T(8,128)(2,1)}, u32[]{:S(2)}) copy-start(bf16[2304,8]{0,1:T(8,128)(2,1)} %param.24) | copy-start | bytes 110596
  242.3 43.0 %all-to-all-start.3 = ((bf16[8,12,2304]{2,1,0:T(8,128)(2,1)}), bf16[8,12,2304]{2,1,0:T(8,128)(2,1)S(1)}, u32[]{:S(2)}, u32[]{:S(2)}) async-start(bf16[8,12,2304]{2,1,0:T(8,128)(2,1)} %add_convert_fusion), calls=%async_computation.3 | async-start | bytes 1179648 | tf_op jit(solution)/shard_map/all_to_all | solution.py:168
  286.3 19.3 %all-to-all-start.4 = ((bf16[16,6,2304]{2,1,0:T(8,128)(2,1)}), bf16[16,6,2304]{2,1,0:T(8,128)(2,1)S(1)}, u32[]{:S(2)}, u32[]{:S(2)}) async-start(bf16[16,6,2304]{2,1,0:T(8,128)(2,1)} %all_to_all.26), calls=%async_computation.4 | async-start | bytes 1179648 | tf_op jit(solution)/shard_map/all_to_all | solution.py:169
  305.8 1.3 copy-start.6
  305.8 1.5 copy-start.12
Sparse Core Ops, SparseCore 0:
  10.1 188.2 all-gather.1

commit v6 on v1

--- a/solution.py
+++ b/solution.py
@@ -138,14 +138,26 @@
     n_c = lax.axis_size("c")
     slot_total = arrived.shape[0]
     piece = slot_total // n_zz
+    half_cap = capacity // 2
+    column_odd = lax.axis_index("expert") % 2
+    by_piece = arrived.reshape(n_zz, 2, capacity, model_width)
+    mine = lax.dynamic_slice_in_dim(by_piece, column_odd * half_cap, half_cap, axis=2)
     sent = lax.all_to_all(
-        arrived.reshape(n_zz, piece, model_width), "zz", split_axis=0, concat_axis=0, tiled=True
+        mine.reshape(n_zz, piece // 2, model_width), "zz", split_axis=0, concat_axis=0, tiled=True
     )
     swap = [(0, 1), (1, 0)]
     from_h = lax.ppermute(sent, "h", swap)
     both_h = jnp.stack([sent, from_h])
     from_c = lax.ppermute(both_h, "c", swap)
-    rows_here = jnp.stack([both_h, from_c])
+    half_rows = jnp.stack([both_h, from_c]).reshape(n_c, n_h, n_zz, 2, half_cap, model_width)
+    other_half = lax.ppermute(
+        half_rows, "expert", [(i, i ^ 1) for i in range(expert_devs)]
+    )
+    rows_here = jnp.where(
+        column_odd == 0,
+        jnp.concatenate([half_rows, other_half], axis=4),
+        jnp.concatenate([other_half, half_rows], axis=4),
+    ).reshape(n_c, n_h, n_zz, piece, model_width)
     flat_rows = rows_here.reshape(n_c * n_h * n_zz * piece, model_width)
     gate_val = lax.dot_general(
         flat_rows, gate_held, (((1,), (1,)), ((), ())), preferred_element_type=jnp.float32

time: 312 us -> 294 us (0.942)
  blocking collectives: 84.8 us -> 42.1 us
  waiting for transfers between devices: 116 us -> 139 us
    all_to_all x2 -> x1, blocking collectives: 84.8 us -> 42.1 us  [on_device(): lax.all_to_all(mine.reshape(n_zz, piece // 2, model_width), 'zz', split_a...]
    ppermute x0 -> x1, waiting for transfers between devices: none -> 21 us  [on_device(): lax.ppermute(half_rows, 'expert', [(i, i ^ 1) for i in range(expert_devs)])]
    ppermute x1, waiting for transfers between devices: 37.3 us -> 20.1 us  [on_device(): from_h = lax.ppermute(sent, 'h', swap)]
    all_to_all x0 -> x1, waiting for transfers between devices: none -> 11.9 us  [on_device(): lax.all_to_all(outgoing.reshape(expert_devs * capacity, model_width), 'ex...]
    ppermute x1, starting transfers between devices: 7.67 us -> 1.92 us  [on_device(): back_h = lax.ppermute(sum_c[1], 'h', swap)]
    all_gather x1, waiting for transfers between devices: 2.2 us -> 7.93 us  [on_device(): lax.all_gather(jnp.stack([gate_proj[0], up_proj[0], down_proj[0]]), 'zz',...]
    all_to_all x0 -> x1, starting transfers between devices: none -> 3.58 us  [on_device(): lax.all_to_all(outgoing.reshape(expert_devs * capacity, model_width), 'ex...]
  transfers between devices with their start and end apart: 8 -> 10, of which waited for: 8 -> 10; matrix products, arithmetic and copies ran while one was open for 11% -> 12% of each run, Pallas kernels for 0% -> 0%
where the time goes in v6:
time: 294 us; the launch traced here: 293 us
  waiting for transfers between devices  139 us (47%)
  blocking collectives  42.1 us (14%)
  starting transfers between devices  38.3 us (13%)
  other arithmetic  23.2 us (8%)
  local copies, waits for them, and re-layouts  21.2 us (7%)
  matrix products  15.3 us (5%)
  between operations  14.7 us (5%)
    all_to_all x1, blocking collectives, on_device(): lax.all_to_all(mine.reshape(n_zz, piece // 2, model_width), 'zz', split_a...  42.1 us
    all_to_all x1, waiting for transfers between devices, on_device(): lax.all_to_all(summed, 'zz', split_axis=0, concat_axis=0, tiled=True)  32 us
    ppermute x1, waiting for transfers between devices, on_device(): lax.ppermute(half_rows, 'expert', [(i, i ^ 1) for i in range(expert_devs)])  21 us
    ppermute x1, waiting for transfers between devices, on_device(): from_h = lax.ppermute(sent, 'h', swap)  20.1 us
    all_to_all x1, waiting for transfers between devices, on_device(): lax.all_to_all(partial_proj.reshape(expert_count, own_rows, partial_proj....  18.2 us
    all_to_all x1, waiting for transfers between devices, on_device(): lax.all_to_all(own_slots.reshape(slot_total, model_width), 'expert', spli...  12.3 us
    ppermute x1, waiting for transfers between devices, on_device(): back_h = lax.ppermute(sum_c[1], 'h', swap)  12.2 us
    all_to_all x1, waiting for transfers between devices, on_device(): lax.all_to_all(outgoing.reshape(expert_devs * capacity, model_width), 'ex...  11.9 us
  transfers between devices with their start and end apart: 10, of which 10 were waited for; matrix products, arithmetic and copies ran while one was open for 12% of the time, Pallas kernels for 0%

profile of v6, /device:TPU:64, one launch (start us, length us, event | category | flops | bytes accessed | tf_op | source)
XLA Modules:
  0.0 293.5 jit_solution(13484477194570952025)
XLA Ops:
  7.3 2.2 pad_maximum_fusion.1
  9.9 1.3 gather_fusion
  11.9 0.7 reduce.23
  12.8 0.7 gather_fusion.1
  13.6 1.8 reshape.451
  15.4 0.7 gather_fusion.2
  16.2 1.9 reshape.452
  18.3 2.6 fusion.40
  21.4 0.5 fusion.18
  22.3 0.7 fusion.39
  23.2 4.4 %compare_select_fusion.4 = (s32[256,1]{0,1:T(1,128)S(1)}, s32[256,1]{0,1:T(1,128)S(1)}) fusion(s32[]{:T(128)} %bitcast.17, s32[]{:T(128)} %bitcast.18, s32[]{:T(128)} %bitcast.19, s32[]{:T(128)} %bitcast.20, s32[]{:T(128)} %bitcast.21, s32[]{:T(128)} %bitcast.23, s32[]{:T(128)} %bitcast.22, s32[256,1]{0,1:T(1,128)S(1)} %bitcast.106, s32[256,1]{0,1:T(1,128)S(1)} %bitcast.105), kind=kLoop, calls=%fused_computation.75 | loop fusion | flops 3584 | bytes 4124 | tf_op jit(solution)/shard_map/gather | solution.py:55
  27.6 5.8 %select_select_fusion = s32[256]{0:T(256)S(1)} fusion(pred[256]{0:T(512)(128)(4,1)S(1)} %get-tuple-element.10, pred[256]{0:T(512)(128)(4,1)S(1)} %get-tuple-element.9, pred[256]{0:T(512)(128)(4,1)S(1)} %get-tuple-element.8, pred[256]{0:T(512)(128)(4,1)S(1)} %get-tuple-element.7, pred[256]{0:T(512)(128)(4,1)S(1)} %get-tuple-element.6, ...), kind=kLoop, calls=%fused_computation.89 | loop fusion | flops 2304 | bytes 4388 | tf_op jit(solution)/shard_map/gather | solution.py:55
  33.5 1.7 gather_fusion.3
  35.1 1.5 convolution_convert_fusion.1
  36.6 7.2 %all-to-all-start = ((bf16[16,16,2304]{2,1,0:T(8,128)(2,1)}), bf16[16,16,2304]{2,1,0:T(8,128)(2,1)S(1)}, u32[]{:S(2)}, u32[]{:S(2)}) async-start(bf16[16,16,2304]{2,1,0:T(8,128)(2,1)} %bitcast.27), calls=%async_computation | async-start | bytes 2359296 | tf_op jit(solution)/shard_map/all_to_all | solution.py:97
  44.8 18.2 %all-to-all-done = bf16[16,16,2304]{2,1,0:T(8,128)(2,1)S(1)} async-done(((bf16[16,16,2304]{2,1,0:T(8,128)(2,1)}), bf16[16,16,2304]{2,1,0:T(8,128)(2,1)S(1)}, u32[]{:S(2)}, u32[]{:S(2)}) %all-to-all-start) | async-done | bytes 1179680 | tf_op jit(solution)/shard_map/all_to_all | solution.py:97
  64.4 0.8 broadcast_in_dim.25
  65.2 3.6 %all-to-all-start.1 = ((bf16[16,6,2304]{2,1,0:T(8,128)(2,1)}), bf16[16,6,2304]{2,1,0:T(8,128)(2,1)S(1)}, u32[]{:S(2)}, u32[]{:S(2)}) async-start(bf16[16,6,2304]{2,1,0:T(8,128)(2,1)} %bitcast.28), calls=%async_computation.1 | async-start | bytes 1179648 | tf_op jit(solution)/shard_map/all_to_all | solution.py:129
  68.8 11.9 %all-to-all-done.1 = bf16[16,6,2304]{2,1,0:T(8,128)(2,1)S(1)} async-done(((bf16[16,6,2304]{2,1,0:T(8,128)(2,1)}), bf16[16,6,2304]{2,1,0:T(8,128)(2,1)S(1)}, u32[]{:S(2)}, u32[]{:S(2)}) %all-to-all-start.1) | async-done | bytes 442400 | tf_op jit(solution)/shard_map/all_to_all | solution.py:129
  81.1 42.1 %all_to_all.33 = bf16[8,6,2304]{2,1,0:T(8,128)(2,1)S(1)} all-to-all(bf16[8,6,2304]{2,1,0:T(8,128)(2,1)S(1)} %copy.133), channel_id=1, replica_groups=mesh['zz'=8,'h'=2,'c'=2,'expert'=16] {'zz'}, dimensions={0} | all-to-all | bytes 442368 | tf_op jit(solution)/shard_map/all_to_all | solution.py:145
  123.2 2.8 collective-permute-start
  126.1 20.1 %collective-permute-done = bf16[8,6,2304]{2,0,1:T(8,128)(2,1)S(1)} collective-permute-done((bf16[8,6,2304]{2,0,1:T(8,128)(2,1)S(1)}, bf16[8,6,2304]{2,0,1:T(8,128)(2,1)S(1)}, u32[]{:S(2)}, u32[]{:S(2)}) %collective-permute-start) | collective-permute-done | bytes 221216 | tf_op jit(solution)/shard_map/ppermute | solution.py:149
  146.2 1.9 collective-permute-start.1
  148.2 1.8 collective-permute-done.1
  150.0 2.7 collective-permute-start.2
  152.8 21.0 %collective-permute-done.2 = bf16[2,2,8,2,3,2304]{5,2,4,3,1,0:T(8,128)(2,1)} collective-permute-done((bf16[2,2,8,2,3,2304]{5,2,4,3,1,0:T(8,128)(2,1)S(1)}, bf16[2,2,8,2,3,2304]{5,2,4,3,1,0:T(8,128)(2,1)}, u32[]{:S(2)}, u32[]{:S(2)}) %collective-permute-start.2) | collective-permute-done | bytes 884768 | tf_op jit(solution)/shard_map/ppermute | solution.py:153
  173.7 1.6 maximum_select_fusion
  175.7 1.6 select_n.105
  177.4 7.9 %all-gather.2.cloned.1.call-done = bf16[3,512,2304]{2,1,0:T(8,128)(2,1)} async-done(((bf16[3,64,2304]{2,1,0:T(8,128)(2,1)}), bf16[3,512,2304]{2,1,0:T(8,128)(2,1)}) %all-gather.2.cloned.1.call-update) | async-done | bytes 7077904 | tf_op jit(solution)/shard_map/all_gather | solution.py:76
  185.3 4.3 %fusion = f32[384,512]{1,0:T(8,128)} fusion(bf16[384,2304]{1,0:T(8,128)(2,1)} %select_n.105, bf16[3,512,2304]{2,1,0:T(8,128)(2,1)} %all-gather.2.cloned.1.call-done), kind=kOutput, calls=%fused_computation.11 | convolution fusion | flops 905969664 | bytes 4915200 | tf_op jit(solution)/shard_map/dot_general | solution.py:165
  189.6 6.1 %convolution_convert_fusion = bf16[384,2304]{1,0:T(8,128)(2,1)} fusion(bf16[3,512,2304]{2,1,0:T(8,128)(2,1)} %all-gather.2.cloned.1.call-done, f32[384,512]{1,0:T(8,128)} %fusion, bf16[384,2304]{1,0:T(8,128)(2,1)S(1)} %copy-done.3), kind=kOutput, calls=%fused_computation.6 | convolution fusion | flops 1814003712 | bytes 9043968 | tf_op jit(solution)/shard_map/dot_general | solution.py:169
  195.7 2.8 fusion.38
  198.7 1.2 copy.138
  199.9 1.9 collective-permute-start.3
  201.8 1.5 reshape.325
  203.3 1.2 collective-permute-done.3
  204.5 1.4 add_convert_fusion
  206.2 1.9 collective-permute-start.4
  208.1 12.2 %collective-permute-done.4 = bf16[8,12,2304]{2,0,1:T(8,128)(2,1)S(1)} collective-permute-done((bf16[8,12,2304]{2,0,1:T(8,128)(2,1)S(1)}, bf16[8,12,2304]{2,0,1:T(8,128)(2,1)S(1)}, u32[]{:S(2)}, u32[]{:S(2)}) %collective-permute-start.4) | collective-permute-done | bytes 442400 | tf_op jit(solution)/shard_map/ppermute | solution.py:173
  220.3 0.9 fusion.21
  221.2 9.6 %all-to-all-start.3 = ((bf16[8,12,2304]{2,1,0:T(8,128)(2,1)}), bf16[8,12,2304]{2,1,0:T(8,128)(2,1)S(1)}, u32[]{:S(2)}, u32[]{:S(2)}) async-start(bf16[8,12,2304]{2,1,0:T(8,128)(2,1)} %fusion.21), calls=%async_computation.3 | async-start | bytes 1179648 | tf_op jit(solution)/shard_map/all_to_all | solution.py:175
  231.4 0.7 gather_fusion.5
  232.2 32.0 %all-to-all-done.3 = bf16[8,12,2304]{2,1,0:T(8,128)(2,1)S(1)} async-done(((bf16[8,12,2304]{2,1,0:T(8,128)(2,1)}), bf16[8,12,2304]{2,1,0:T(8,128)(2,1)S(1)}, u32[]{:S(2)}, u32[]{:S(2)}) %all-to-all-start.3) | async-done | bytes 442400 | tf_op jit(solution)/shard_map/all_to_all | solution.py:175
  264.3 1.0 all_to_all.26
  265.2 6.6 %all-to-all-start.4 = ((bf16[16,6,2304]{2,1,0:T(8,128)(2,1)}), bf16[16,6,2304]{2,1,0:T(8,128)(2,1)S(1)}, u32[]{:S(2)}, u32[]{:S(2)}) async-start(bf16[16,6,2304]{2,1,0:T(8,128)(2,1)} %all_to_all.26), calls=%async_computation.4 | async-start | bytes 1179648 | tf_op jit(solution)/shard_map/all_to_all | solution.py:176
  272.0 12.3 %all-to-all-done.4 = bf16[16,6,2304]{2,1,0:T(8,128)(2,1)S(1)} async-done(((bf16[16,6,2304]{2,1,0:T(8,128)(2,1)}), bf16[16,6,2304]{2,1,0:T(8,128)(2,1)S(1)}, u32[]{:S(2)}, u32[]{:S(2)}) %all-to-all-start.4) | async-done | bytes 442400 | tf_op jit(solution)/shard_map/all_to_all | solution.py:176
  284.5 0.7 gather_fusion.4
  285.9 0.7 multiply_convert_fusion.2
  (111 shorter events, 7.8 us)
Async XLA Ops:
  7.2 5.6 %copy-start = (bf16[32,128,128]{2,1,0:T(8,128)(2,1)S(1)}, bf16[32,128,128]{2,1,0:T(8,128)(2,1)}, u32[]{:S(2)}) copy-start(bf16[32,128,128]{2,1,0:T(8,128)(2,1)} %param.17) | copy-start | bytes 3145732
  7.2 2.3 copy-start.16
  7.2 2.7 copy-start.1
  7.2 4.7 %copy-start.19 = (s32[1,32]{1,0:T(1,128)S(1)}, s32[1,32]{1,0:T(1,128)}, u32[]{:S(2)}) copy-start(s32[1,32]{1,0:T(1,128)} %param.21) | copy-start | bytes 388
  7.2 178.1 %all-gather.2.cloned.1.call-start = ((), (), s32[]{:S(2)}) async-start(), calls=%async_computation.5 | async-start | bytes 7962624 | tf_op jit(solution)/shard_map/all_gather | solution.py:76
  13.6 1.8 copy-start.4
  16.2 1.9 copy-start.15
  18.3 3.1 %copy-start.2 = (bf16[16,256,2,64]{3,2,1,0:T(2,128)(2,1)S(1)}, bf16[16,256,2,64]{3,2,1,0:T(2,128)(2,1)}, u32[]{:S(2)}) copy-start(bf16[16,256,2,64]{3,2,1,0:T(2,128)(2,1)} %reshape.452) | copy-start | bytes 3145732
  21.9 13.2 %copy-start.9 = (bf16[128,2304]{1,0:T(8,128)(2,1)S(1)}, bf16[128,2304]{1,0:T(8,128)(2,1)}, u32[]{:S(2)}) copy-start(bf16[128,2304]{1,0:T(8,128)(2,1)} %param.22) | copy-start | bytes 1769476
  35.1 8.7 %copy-start.13 = (s32[16,2]{0,1:T(2,128)S(1)}, s32[16,2]{0,1:T(2,128)}, u32[]{:S(2)}) copy-start(s32[16,2]{0,1:T(2,128)} %param.28) | copy-start | bytes 388
  36.6 26.6 %copy-start.5 = (bf16[16,2304]{1,0:T(8,128)(2,1)S(1)}, bf16[16,2304]{1,0:T(8,128)(2,1)}, u32[]{:S(2)}) copy-start(bf16[16,2304]{1,0:T(8,128)(2,1)} %param.15) | copy-start | bytes 221188
  36.6 26.7 %copy-start.11 = (f32[2304]{0:T(1024)S(1)}, f32[2304]{0:T(1024)}, u32[]{:S(2)}) copy-start(f32[2304]{0:T(1024)} %param.23) | copy-start | bytes 27652
  36.6 26.4 %all-to-all-start = ((bf16[16,16,2304]{2,1,0:T(8,128)(2,1)}), bf16[16,16,2304]{2,1,0:T(8,128)(2,1)S(1)}, u32[]{:S(2)}, u32[]{:S(2)}) async-start(bf16[16,16,2304]{2,1,0:T(8,128)(2,1)} %bitcast.27), calls=%async_computation | async-start | bytes 2359296 | tf_op jit(solution)/shard_map/all_to_all | solution.py:97
  44.3 0.5 copy-start.17
  63.4 0.6 copy-start.7
  65.2 15.6 %all-to-all-start.1 = ((bf16[16,6,2304]{2,1,0:T(8,128)(2,1)}), bf16[16,6,2304]{2,1,0:T(8,128)(2,1)S(1)}, u32[]{:S(2)}, u32[]{:S(2)}) async-start(bf16[16,6,2304]{2,1,0:T(8,128)(2,1)} %bitcast.28), calls=%async_computation.1 | async-start | bytes 1179648 | tf_op jit(solution)/shard_map/all_to_all | solution.py:129
  123.2 23.0 %collective-permute-start = (bf16[8,6,2304]{2,0,1:T(8,128)(2,1)S(1)}, bf16[8,6,2304]{2,0,1:T(8,128)(2,1)S(1)}, u32[]{:S(2)}, u32[]{:S(2)}) collective-permute-start(bf16[8,6,2304]{2,0,1:T(8,128)(2,1)S(1)} %copy.134), channel_id=1, source_target_pairs={{0,32},{32,0},{1,33},{33,1},{2,34},{34,2},{3,35},{35,3},{4,36},{36... | collective-permute-start | bytes 663560 | tf_op jit(solution)/shard_map/ppermute | solution.py:149
  146.2 3.7 %collective-permute-start.1 = (bf16[2,8,6,2304]{3,1,2,0:T(8,128)(2,1)S(1)}, bf16[2,8,6,2304]{3,1,2,0:T(8,128)(2,1)S(1)}, u32[]{:S(2)}, u32[]{:S(2)}) collective-permute-start(bf16[2,8,6,2304]{3,1,2,0:T(8,128)(2,1)S(1)} %pad_maximum_fusion.2), channel_id=1, source_target_pairs={{0,16},{16,0},{1,17},{17,1},{2,18},{18,2},{3,19},{19,3},{4,20},{20... | collective-permute-start | bytes 1327112 | tf_op jit(solution)/shard_map/ppermute | solution.py:151
  150.0 23.7 %collective-permute-start.2 = (bf16[2,2,8,2,3,2304]{5,2,4,3,1,0:T(8,128)(2,1)S(1)}, bf16[2,2,8,2,3,2304]{5,2,4,3,1,0:T(8,128)(2,1)}, u32[]{:S(2)}, u32[]{:S(2)}) collective-permute-start(bf16[2,2,8,2,3,2304]{5,2,4,3,1,0:T(8,128)(2,1)S(1)} %pad_maximum_fusion), channel_id=1, source_target_pairs={{0,1},{1,0},{2,3},{3,2},{4,5},{5,4},{6,7},{7,6},{8,9},{9,8},{10,11... | collective-permute-start | bytes 2654216 | tf_op jit(solution)/shard_map/ppermute | solution.py:153
  177.4 12.2 %copy-start.3 = (bf16[384,2304]{1,0:T(8,128)(2,1)S(1)}, bf16[384,2304]{1,0:T(8,128)(2,1)}, u32[]{:S(2)}) copy-start(bf16[384,2304]{1,0:T(8,128)(2,1)} %select_n.105) | copy-start | bytes 5308420
  199.9 4.7 %collective-permute-start.3 = (bf16[2,8,12,2304]{3,1,2,0:T(8,128)(2,1)}, bf16[2,8,12,2304]{3,1,2,0:T(8,128)(2,1)}, u32[]{:S(2)}, u32[]{:S(2)}) collective-permute-start(bf16[2,8,12,2304]{3,1,2,0:T(8,128)(2,1)} %copy.138), channel_id=1, source_target_pairs={{0,16},{16,0},{1,17},{17,1},{2,18},{18,2},{3,19},{19,3},{4,20},{20... | collective-permute-start | bytes 2654216 | tf_op jit(solution)/shard_map/ppermute | solution.py:171
  206.0 24.8 %copy-start.14 = (s32[16,2]{0,1:T(2,128)S(1)}, s32[16,2]{0,1:T(2,128)}, u32[]{:S(2)}) copy-start(s32[16,2]{0,1:T(2,128)} %param.28) | copy-start | bytes 388
  206.0 25.2 %copy-start.18 = (s32[32]{0:T(128)S(1)}, s32[32]{0:T(128)}, u32[]{:S(2)}) copy-start(s32[32]{0:T(128)} %copy-done.17) | copy-start | bytes 388
  206.0 25.2 %copy-start.8 = (bf16[16,2304]{1,0:T(8,128)(2,1)S(1)}, bf16[16,2304]{1,0:T(8,128)(2,1)}, u32[]{:S(2)}) copy-start(bf16[16,2304]{1,0:T(8,128)(2,1)} %copy-done.7) | copy-start | bytes 221188
  206.1 25.2 %copy-start.10 = (bf16[2304,8]{0,1:T(8,128)(2,1)S(1)}, bf16[2304,8]{0,1:T(8,128)(2,1)}, u32[]{:S(2)}) copy-start(bf16[2304,8]{0,1:T(8,128)(2,1)} %param.24) | copy-start | bytes 110596
  206.2 14.1 %collective-permute-start.4 = (bf16[8,12,2304]{2,0,1:T(8,128)(2,1)S(1)}, bf16[8,12,2304]{2,0,1:T(8,128)(2,1)S(1)}, u32[]{:S(2)}, u32[]{:S(2)}) collective-permute-start(bf16[8,12,2304]{2,0,1:T(8,128)(2,1)S(1)} %copy.140), channel_id=1, source_target_pairs={{0,32},{32,0},{1,33},{33,1},{2,34},{34,2},{3,35},{35,3},{4,36},{36... | collective-permute-start | bytes 1327112 | tf_op jit(solution)/shard_map/ppermute | solution.py:173
  221.2 43.0 %all-to-all-start.3 = ((bf16[8,12,2304]{2,1,0:T(8,128)(2,1)}), bf16[8,12,2304]{2,1,0:T(8,128)(2,1)S(1)}, u32[]{:S(2)}, u32[]{:S(2)}) async-start(bf16[8,12,2304]{2,1,0:T(8,128)(2,1)} %fusion.21), calls=%async_computation.3 | async-start | bytes 1179648 | tf_op jit(solution)/shard_map/all_to_all | solution.py:175
  265.2 19.0 %all-to-all-start.4 = ((bf16[16,6,2304]{2,1,0:T(8,128)(2,1)}), bf16[16,6,2304]{2,1,0:T(8,128)(2,1)S(1)}, u32[]{:S(2)}, u32[]{:S(2)}) async-start(bf16[16,6,2304]{2,1,0:T(8,128)(2,1)} %all_to_all.26), calls=%async_computation.4 | async-start | bytes 1179648 | tf_op jit(solution)/shard_map/all_to_all | solution.py:176
  284.4 1.3 copy-start.6
  284.4 1.5 copy-start.12
Sparse Core Ops, SparseCore 0:
  10.1 175.1 all-gather.1

commit v7 on v6

--- a/solution.py
+++ b/solution.py
@@ -172,12 +172,18 @@
     sum_c = (partial[0].astype(jnp.float32) + back_c.astype(jnp.float32)).astype(jnp.bfloat16)
     back_h = lax.ppermute(sum_c[1], "h", swap)
     summed = (sum_c[0].astype(jnp.float32) + back_h.astype(jnp.float32)).astype(jnp.bfloat16)
-    own_slots = lax.all_to_all(summed, "zz", split_axis=0, concat_axis=0, tiled=True)
+    by_half = summed.reshape(n_zz, 2, 2, half_cap, model_width)
+    keep = lax.dynamic_index_in_dim(by_half, column_odd, axis=2, keepdims=False)
+    give = lax.dynamic_index_in_dim(by_half, 1 - column_odd, axis=2, keepdims=False)
+    taken = lax.ppermute(give, "expert", [(i, i ^ 1) for i in range(expert_devs)])
+    both_columns = (keep.astype(jnp.float32) + taken.astype(jnp.float32)).astype(jnp.bfloat16)
+    own_slots = lax.all_to_all(
+        both_columns.reshape(n_zz, piece // 2, model_width), "zz", split_axis=0, concat_axis=0, tiled=True
+    )
     returned = lax.all_to_all(
-        own_slots.reshape(slot_total, model_width), "expert", split_axis=0, concat_axis=0, tiled=True
+        own_slots.reshape(expert_devs, half_cap, model_width), "expert", split_axis=0, concat_axis=0, tiled=True
     ).astype(jnp.float32)
-    arranged = returned.reshape(experts_all, 2, capacity, model_width)
-    expert_result = jnp.sum(arranged, axis=1)
+    expert_result = returned.reshape(experts_all, capacity, model_width)
     per_slot = expert_result.reshape(experts_all * capacity, model_width)[target]
     expert_mix = jnp.sum(per_slot.reshape(own_rows, 2, model_width) * shares[:, :, None], axis=1)
     combined = hidden + expert_mix

time: 294 us -> 289 us (0.983)
  the two profiles are of different devices: /device:TPU:64 before, /device:TPU:2 now
where the time goes in v7:
time: 289 us; the launch traced here: 288 us
  waiting for transfers between devices  118 us (41%)
  blocking collectives  48.4 us (17%)
  starting transfers between devices  44.4 us (15%)
  other arithmetic  24.8 us (9%)
  local copies, waits for them, and re-layouts  22.7 us (8%)
  matrix products  15.3 us (5%)
  between operations  14.6 us (5%)
    all_to_all x1, blocking collectives, on_device(): lax.all_to_all(mine.reshape(n_zz, piece // 2, model_width), 'zz', split_a...  48.4 us
    ppermute x1, waiting for transfers between devices, on_device(): lax.ppermute(half_rows, 'expert', [(i, i ^ 1) for i in range(expert_devs)])  21.1 us
    ppermute x1, waiting for transfers between devices, on_device(): from_h = lax.ppermute(sent, 'h', swap)  21 us
    all_to_all x1, waiting for transfers between devices, on_device(): lax.all_to_all(both_columns.reshape(n_zz, piece // 2, model_width), 'zz',...  20.1 us
    all_to_all x1, waiting for transfers between devices, on_device(): lax.all_to_all(partial_proj.reshape(expert_count, own_rows, partial_proj....  14.9 us
    gather x3, other arithmetic, paged_attention(): offset = row_ids - starts[owning]  10.3 us
    all_to_all x1, starting transfers between devices, on_device(): lax.all_to_all(partial_proj.reshape(expert_count, own_rows, partial_proj....  9.5 us
    ppermute x1, waiting for transfers between devices, on_device(): back_h = lax.ppermute(sum_c[1], 'h', swap)  9.49 us
  transfers between devices with their start and end apart: 11, of which 11 were waited for; matrix products, arithmetic and copies ran while one was open for 13% of the time, Pallas kernels for 0%

profile of v7, /device:TPU:2, one launch (start us, length us, event | category | flops | bytes accessed | tf_op | source)
XLA Modules:
  0.0 287.9 jit_solution(6409612955702778932)
XLA Ops:
  7.3 2.2 pad_maximum_fusion.1
  9.9 1.3 gather_fusion
  12.8 0.7 gather_fusion.1
  13.6 1.8 reshape.454
  15.4 0.7 gather_fusion.2
  16.2 1.9 reshape.455
  18.3 2.6 fusion.42
  22.3 0.7 fusion.41
  23.2 4.4 %compare_select_fusion.4 = (s32[256,1]{0,1:T(1,128)S(1)}, s32[256,1]{0,1:T(1,128)S(1)}) fusion(s32[]{:T(128)} %bitcast.17, s32[]{:T(128)} %bitcast.18, s32[]{:T(128)} %bitcast.19, s32[]{:T(128)} %bitcast.20, s32[]{:T(128)} %bitcast.21, s32[]{:T(128)} %bitcast.23, s32[]{:T(128)} %bitcast.22, s32[256,1]{0,1:T(1,128)S(1)} %bitcast.113, s32[256,1]{0,1:T(1,128)S(1)} %bitcast.112), kind=kLoop, calls=%fused_computation.78 | loop fusion | flops 3584 | bytes 4124 | tf_op jit(solution)/shard_map/gather | solution.py:55
  27.6 5.8 %select_select_fusion = s32[256]{0:T(256)S(1)} fusion(pred[256]{0:T(512)(128)(4,1)S(1)} %get-tuple-element.10, pred[256]{0:T(512)(128)(4,1)S(1)} %get-tuple-element.9, pred[256]{0:T(512)(128)(4,1)S(1)} %get-tuple-element.8, pred[256]{0:T(512)(128)(4,1)S(1)} %get-tuple-element.7, pred[256]{0:T(512)(128)(4,1)S(1)} %get-tuple-element.6, ...), kind=kLoop, calls=%fused_computation.92 | loop fusion | flops 2304 | bytes 4388 | tf_op jit(solution)/shard_map/gather | solution.py:55
  33.5 1.7 gather_fusion.3
  35.1 1.5 convolution_convert_fusion.1
  36.6 9.5 %all-to-all-start = ((bf16[16,16,2304]{2,1,0:T(8,128)(2,1)}), bf16[16,16,2304]{2,1,0:T(8,128)(2,1)S(1)}, u32[]{:S(2)}, u32[]{:S(2)}) async-start(bf16[16,16,2304]{2,1,0:T(8,128)(2,1)} %bitcast.27), calls=%async_computation | async-start | bytes 2359296 | tf_op jit(solution)/shard_map/all_to_all | solution.py:97
  47.1 14.9 %all-to-all-done = bf16[16,16,2304]{2,1,0:T(8,128)(2,1)S(1)} async-done(((bf16[16,16,2304]{2,1,0:T(8,128)(2,1)}), bf16[16,16,2304]{2,1,0:T(8,128)(2,1)S(1)}, u32[]{:S(2)}, u32[]{:S(2)}) %all-to-all-start) | async-done | bytes 1179680 | tf_op jit(solution)/shard_map/all_to_all | solution.py:97
  63.3 0.8 broadcast_in_dim.25
  64.2 4.8 %all-to-all-start.1 = ((bf16[16,6,2304]{2,1,0:T(8,128)(2,1)}), bf16[16,6,2304]{2,1,0:T(8,128)(2,1)S(1)}, u32[]{:S(2)}, u32[]{:S(2)}) async-start(bf16[16,6,2304]{2,1,0:T(8,128)(2,1)} %bitcast.28), calls=%async_computation.1 | async-start | bytes 1179648 | tf_op jit(solution)/shard_map/all_to_all | solution.py:129
  69.0 9.2 %all-to-all-done.1 = bf16[16,6,2304]{2,1,0:T(8,128)(2,1)S(1)} async-done(((bf16[16,6,2304]{2,1,0:T(8,128)(2,1)}), bf16[16,6,2304]{2,1,0:T(8,128)(2,1)S(1)}, u32[]{:S(2)}, u32[]{:S(2)}) %all-to-all-start.1) | async-done | bytes 442400 | tf_op jit(solution)/shard_map/all_to_all | solution.py:129
  78.5 48.4 %all_to_all.29 = bf16[8,6,2304]{2,1,0:T(8,128)(2,1)S(1)} all-to-all(bf16[8,6,2304]{2,1,0:T(8,128)(2,1)S(1)} %copy.141), channel_id=1, replica_groups=mesh['zz'=8,'h'=2,'c'=2,'expert'=16] {'zz'}, dimensions={0} | all-to-all | bytes 442368 | tf_op jit(solution)/shard_map/all_to_all | solution.py:145
  126.9 1.9 collective-permute-start
  128.9 21.0 %collective-permute-done = bf16[8,6,2304]{2,0,1:T(8,128)(2,1)S(1)} collective-permute-done((bf16[8,6,2304]{2,0,1:T(8,128)(2,1)S(1)}, bf16[8,6,2304]{2,0,1:T(8,128)(2,1)S(1)}, u32[]{:S(2)}, u32[]{:S(2)}) %collective-permute-start) | collective-permute-done | bytes 221216 | tf_op jit(solution)/shard_map/ppermute | solution.py:149
  150.0 1.9 collective-permute-start.1
  151.9 1.8 collective-permute-done.1
  153.8 2.6 collective-permute-start.2
  156.4 21.1 %collective-permute-done.2 = bf16[2,2,8,2,3,2304]{5,2,4,3,1,0:T(8,128)(2,1)} collective-permute-done((bf16[2,2,8,2,3,2304]{5,2,4,3,1,0:T(8,128)(2,1)S(1)}, bf16[2,2,8,2,3,2304]{5,2,4,3,1,0:T(8,128)(2,1)}, u32[]{:S(2)}, u32[]{:S(2)}) %collective-permute-start.2) | collective-permute-done | bytes 884768 | tf_op jit(solution)/shard_map/ppermute | solution.py:153
  177.5 1.6 maximum_select_fusion
  179.5 1.6 select_n.112
  181.1 6.3 %all-gather.2.cloned.1.call-done = bf16[3,512,2304]{2,1,0:T(8,128)(2,1)} async-done(((bf16[3,64,2304]{2,1,0:T(8,128)(2,1)}), bf16[3,512,2304]{2,1,0:T(8,128)(2,1)}) %all-gather.2.cloned.1.call-update) | async-done | bytes 7077904 | tf_op jit(solution)/shard_map/all_gather | solution.py:76
  187.4 4.3 %fusion = f32[384,512]{1,0:T(8,128)} fusion(bf16[384,2304]{1,0:T(8,128)(2,1)} %select_n.112, bf16[3,512,2304]{2,1,0:T(8,128)(2,1)} %all-gather.2.cloned.1.call-done), kind=kOutput, calls=%fused_computation.11 | convolution fusion | flops 905969664 | bytes 4915200 | tf_op jit(solution)/shard_map/dot_general | solution.py:165
  191.7 6.1 %convolution_convert_fusion = bf16[384,2304]{1,0:T(8,128)(2,1)} fusion(bf16[3,512,2304]{2,1,0:T(8,128)(2,1)} %all-gather.2.cloned.1.call-done, f32[384,512]{1,0:T(8,128)} %fusion, bf16[384,2304]{1,0:T(8,128)(2,1)S(1)} %copy-done.4), kind=kOutput, calls=%fused_computation.6 | convolution fusion | flops 1814003712 | bytes 9043968 | tf_op jit(solution)/shard_map/dot_general | solution.py:169
  197.8 2.8 fusion.40
  200.8 1.2 copy.146
  202.0 1.9 collective-permute-start.3
  203.9 1.5 reshape.327
  205.5 1.2 collective-permute-done.3
  206.7 2.2 fusion.6
  208.8 0.9 copy-done.2
  209.8 5.6 %collective-permute-start.4 = (bf16[8,12,2304]{2,0,1:T(8,128)(2,1)S(1)}, bf16[8,12,2304]{2,0,1:T(8,128)(2,1)S(1)}, u32[]{:S(2)}, u32[]{:S(2)}) collective-permute-start(bf16[8,12,2304]{2,0,1:T(8,128)(2,1)S(1)} %slice_bitcast_fusion.6), channel_id=1, source_target_pairs={{0,32},{32,0},{1,33},{33,1},{2,34},{34,2},{3,35},{35,3},{4,36},{36... | collective-permute-start | bytes 1327112 | tf_op jit(solution)/shard_map/ppermute | solution.py:173
  216.4 9.5 %collective-permute-done.4 = bf16[8,12,2304]{2,0,1:T(8,128)(2,1)S(1)} collective-permute-done((bf16[8,12,2304]{2,0,1:T(8,128)(2,1)S(1)}, bf16[8,12,2304]{2,0,1:T(8,128)(2,1)S(1)}, u32[]{:S(2)}, u32[]{:S(2)}) %collective-permute-start.4) | collective-permute-done | bytes 442400 | tf_op jit(solution)/shard_map/ppermute | solution.py:173
  225.9 1.1 fusion.24
  227.0 3.4 %collective-permute-start.5 = (bf16[8,2,3,2304]{3,0,2,1:T(8,128)(2,1)S(1)}, bf16[8,2,3,2304]{3,0,2,1:T(8,128)(2,1)S(1)}, u32[]{:S(2)}, u32[]{:S(2)}) collective-permute-start(bf16[8,2,3,2304]{3,0,2,1:T(8,128)(2,1)S(1)} %dynamic-slice_bitcast_fusion), channel_id=1, source_target_pairs={{0,1},{1,0},{2,3},{3,2},{4,5},{5,4},{6,7},{7,6},{8,9},{9,8},{10,11... | collective-permute-start | bytes 663560 | tf_op jit(solution)/shard_map/ppermute | solution.py:178
  230.6 5.3 %collective-permute-done.5 = bf16[8,2,3,2304]{3,0,2,1:T(8,128)(2,1)S(1)} collective-permute-done((bf16[8,2,3,2304]{3,0,2,1:T(8,128)(2,1)S(1)}, bf16[8,2,3,2304]{3,0,2,1:T(8,128)(2,1)S(1)}, u32[]{:S(2)}, u32[]{:S(2)}) %collective-permute-start.5) | collective-permute-done | bytes 221216 | tf_op jit(solution)/shard_map/ppermute | solution.py:178
  235.9 0.8 copy.148
  236.6 5.3 %all-to-all-start.3 = ((bf16[8,6,2304]{2,1,0:T(8,128)(2,1)}), bf16[8,6,2304]{2,1,0:T(8,128)(2,1)S(1)}, u32[]{:S(2)}, u32[]{:S(2)}) async-start(bf16[8,6,2304]{2,1,0:T(8,128)(2,1)} %copy.148), calls=%async_computation.3 | async-start | bytes 589824 | tf_op jit(solution)/shard_map/all_to_all | solution.py:180
  243.0 20.1 %all-to-all-done.3 = bf16[8,6,2304]{2,1,0:T(8,128)(2,1)S(1)} async-done(((bf16[8,6,2304]{2,1,0:T(8,128)(2,1)}), bf16[8,6,2304]{2,1,0:T(8,128)(2,1)S(1)}, u32[]{:S(2)}, u32[]{:S(2)}) %all-to-all-start.3) | async-done | bytes 221216 | tf_op jit(solution)/shard_map/all_to_all | solution.py:180
  263.1 0.9 reshape.324
  264.0 7.3 %all-to-all-start.4 = ((bf16[16,3,2304]{2,1,0:T(4,128)(2,1)}), bf16[16,3,2304]{2,1,0:T(4,128)(2,1)S(1)}, u32[]{:S(2)}, u32[]{:S(2)}) async-start(bf16[16,3,2304]{2,1,0:T(4,128)(2,1)} %reshape.324), calls=%async_computation.4 | async-start | bytes 589824 | tf_op jit(solution)/shard_map/all_to_all | solution.py:183
  271.3 7.4 %all-to-all-done.4 = bf16[16,3,2304]{2,1,0:T(4,128)(2,1)S(1)} async-done(((bf16[16,3,2304]{2,1,0:T(4,128)(2,1)}), bf16[16,3,2304]{2,1,0:T(4,128)(2,1)S(1)}, u32[]{:S(2)}, u32[]{:S(2)}) %all-to-all-start.4) | async-done | bytes 221216 | tf_op jit(solution)/shard_map/all_to_all | solution.py:183
  280.4 0.7 multiply_convert_fusion.2
  (116 shorter events, 10.9 us)
Async XLA Ops:
  7.2 5.6 %copy-start = (bf16[32,128,128]{2,1,0:T(8,128)(2,1)S(1)}, bf16[32,128,128]{2,1,0:T(8,128)(2,1)}, u32[]{:S(2)}) copy-start(bf16[32,128,128]{2,1,0:T(8,128)(2,1)} %param.17) | copy-start | bytes 3145732
  7.2 2.3 copy-start.17
  7.2 2.7 copy-start.1
  7.2 4.7 %copy-start.20 = (s32[1,32]{1,0:T(1,128)S(1)}, s32[1,32]{1,0:T(1,128)}, u32[]{:S(2)}) copy-start(s32[1,32]{1,0:T(1,128)} %param.21) | copy-start | bytes 388
  7.2 180.2 %all-gather.2.cloned.1.call-start = ((), (), s32[]{:S(2)}) async-start(), calls=%async_computation.5 | async-start | bytes 7962624 | tf_op jit(solution)/shard_map/all_gather | solution.py:76
  13.6 1.8 copy-start.5
  16.2 1.9 copy-start.16
  18.3 3.1 %copy-start.3 = (bf16[16,256,2,64]{3,2,1,0:T(2,128)(2,1)S(1)}, bf16[16,256,2,64]{3,2,1,0:T(2,128)(2,1)}, u32[]{:S(2)}) copy-start(bf16[16,256,2,64]{3,2,1,0:T(2,128)(2,1)} %reshape.455) | copy-start | bytes 3145732
  21.9 13.2 %copy-start.10 = (bf16[128,2304]{1,0:T(8,128)(2,1)S(1)}, bf16[128,2304]{1,0:T(8,128)(2,1)}, u32[]{:S(2)}) copy-start(bf16[128,2304]{1,0:T(8,128)(2,1)} %param.22) | copy-start | bytes 1769476
  35.1 11.0 %copy-start.14 = (s32[16,2]{0,1:T(2,128)S(1)}, s32[16,2]{0,1:T(2,128)}, u32[]{:S(2)}) copy-start(s32[16,2]{0,1:T(2,128)} %param.28) | copy-start | bytes 388
  36.6 25.5 %copy-start.6 = (bf16[16,2304]{1,0:T(8,128)(2,1)S(1)}, bf16[16,2304]{1,0:T(8,128)(2,1)}, u32[]{:S(2)}) copy-start(bf16[16,2304]{1,0:T(8,128)(2,1)} %param.15) | copy-start | bytes 221188
  36.6 25.7 %copy-start.12 = (f32[2304]{0:T(1024)S(1)}, f32[2304]{0:T(1024)}, u32[]{:S(2)}) copy-start(f32[2304]{0:T(1024)} %param.23) | copy-start | bytes 27652
  36.6 25.4 %all-to-all-start = ((bf16[16,16,2304]{2,1,0:T(8,128)(2,1)}), bf16[16,16,2304]{2,1,0:T(8,128)(2,1)S(1)}, u32[]{:S(2)}, u32[]{:S(2)}) async-start(bf16[16,16,2304]{2,1,0:T(8,128)(2,1)} %bitcast.27), calls=%async_computation | async-start | bytes 2359296 | tf_op jit(solution)/shard_map/all_to_all | solution.py:97
  46.6 0.5 copy-start.18
  62.4 0.6 copy-start.8
  64.2 14.1 %all-to-all-start.1 = ((bf16[16,6,2304]{2,1,0:T(8,128)(2,1)}), bf16[16,6,2304]{2,1,0:T(8,128)(2,1)S(1)}, u32[]{:S(2)}, u32[]{:S(2)}) async-start(bf16[16,6,2304]{2,1,0:T(8,128)(2,1)} %bitcast.28), calls=%async_computation.1 | async-start | bytes 1179648 | tf_op jit(solution)/shard_map/all_to_all | solution.py:129
  126.9 23.0 %collective-permute-start = (bf16[8,6,2304]{2,0,1:T(8,128)(2,1)S(1)}, bf16[8,6,2304]{2,0,1:T(8,128)(2,1)S(1)}, u32[]{:S(2)}, u32[]{:S(2)}) collective-permute-start(bf16[8,6,2304]{2,0,1:T(8,128)(2,1)S(1)} %copy.142), channel_id=1, source_target_pairs={{0,32},{32,0},{1,33},{33,1},{2,34},{34,2},{3,35},{35,3},{4,36},{36... | collective-permute-start | bytes 663560 | tf_op jit(solution)/shard_map/ppermute | solution.py:149
  150.0 3.7 %collective-permute-start.1 = (bf16[2,8,6,2304]{3,1,2,0:T(8,128)(2,1)S(1)}, bf16[2,8,6,2304]{3,1,2,0:T(8,128)(2,1)S(1)}, u32[]{:S(2)}, u32[]{:S(2)}) collective-permute-start(bf16[2,8,6,2304]{3,1,2,0:T(8,128)(2,1)S(1)} %pad_maximum_fusion.2), channel_id=1, source_target_pairs={{0,16},{16,0},{1,17},{17,1},{2,18},{18,2},{3,19},{19,3},{4,20},{20... | collective-permute-start | bytes 1327112 | tf_op jit(solution)/shard_map/ppermute | solution.py:151
  153.8 23.7 %collective-permute-start.2 = (bf16[2,2,8,2,3,2304]{5,2,4,3,1,0:T(8,128)(2,1)S(1)}, bf16[2,2,8,2,3,2304]{5,2,4,3,1,0:T(8,128)(2,1)}, u32[]{:S(2)}, u32[]{:S(2)}) collective-permute-start(bf16[2,2,8,2,3,2304]{5,2,4,3,1,0:T(8,128)(2,1)S(1)} %pad_maximum_fusion), channel_id=1, source_target_pairs={{0,1},{1,0},{2,3},{3,2},{4,5},{5,4},{6,7},{7,6},{8,9},{9,8},{10,11... | collective-permute-start | bytes 2654216 | tf_op jit(solution)/shard_map/ppermute | solution.py:153
  181.1 10.6 %copy-start.4 = (bf16[384,2304]{1,0:T(8,128)(2,1)S(1)}, bf16[384,2304]{1,0:T(8,128)(2,1)}, u32[]{:S(2)}) copy-start(bf16[384,2304]{1,0:T(8,128)(2,1)} %select_n.112) | copy-start | bytes 5308420
  202.0 4.7 %collective-permute-start.3 = (bf16[2,8,12,2304]{3,1,2,0:T(8,128)(2,1)}, bf16[2,8,12,2304]{3,1,2,0:T(8,128)(2,1)}, u32[]{:S(2)}, u32[]{:S(2)}) collective-permute-start(bf16[2,8,12,2304]{3,1,2,0:T(8,128)(2,1)} %copy.146), channel_id=1, source_target_pairs={{0,16},{16,0},{1,17},{17,1},{2,18},{18,2},{3,19},{19,3},{4,20},{20... | collective-permute-start | bytes 2654216 | tf_op jit(solution)/shard_map/ppermute | solution.py:171
  208.8 0.9 copy-start.2
  209.8 16.1 %collective-permute-start.4 = (bf16[8,12,2304]{2,0,1:T(8,128)(2,1)S(1)}, bf16[8,12,2304]{2,0,1:T(8,128)(2,1)S(1)}, u32[]{:S(2)}, u32[]{:S(2)}) collective-permute-start(bf16[8,12,2304]{2,0,1:T(8,128)(2,1)S(1)} %slice_bitcast_fusion.6), channel_id=1, source_target_pairs={{0,32},{32,0},{1,33},{33,1},{2,34},{34,2},{3,35},{35,3},{4,36},{36... | collective-permute-start | bytes 1327112 | tf_op jit(solution)/shard_map/ppermute | solution.py:173
  216.4 25.6 %copy-start.19 = (s32[32]{0:T(128)S(1)}, s32[32]{0:T(128)}, u32[]{:S(2)}) copy-start(s32[32]{0:T(128)} %copy-done.18) | copy-start | bytes 388
  216.4 25.6 %copy-start.9 = (bf16[16,2304]{1,0:T(8,128)(2,1)S(1)}, bf16[16,2304]{1,0:T(8,128)(2,1)}, u32[]{:S(2)}) copy-start(bf16[16,2304]{1,0:T(8,128)(2,1)} %copy-done.8) | copy-start | bytes 221188
  216.4 25.6 %copy-start.11 = (bf16[2304,8]{0,1:T(8,128)(2,1)S(1)}, bf16[2304,8]{0,1:T(8,128)(2,1)}, u32[]{:S(2)}) copy-start(bf16[2304,8]{0,1:T(8,128)(2,1)} %param.24) | copy-start | bytes 110596
  227.0 8.8 %collective-permute-start.5 = (bf16[8,2,3,2304]{3,0,2,1:T(8,128)(2,1)S(1)}, bf16[8,2,3,2304]{3,0,2,1:T(8,128)(2,1)S(1)}, u32[]{:S(2)}, u32[]{:S(2)}) collective-permute-start(bf16[8,2,3,2304]{3,0,2,1:T(8,128)(2,1)S(1)} %dynamic-slice_bitcast_fusion), channel_id=1, source_target_pairs={{0,1},{1,0},{2,3},{3,2},{4,5},{5,4},{6,7},{7,6},{8,9},{9,8},{10,11... | collective-permute-start | bytes 663560 | tf_op jit(solution)/shard_map/ppermute | solution.py:178
  236.6 26.4 %all-to-all-start.3 = ((bf16[8,6,2304]{2,1,0:T(8,128)(2,1)}), bf16[8,6,2304]{2,1,0:T(8,128)(2,1)S(1)}, u32[]{:S(2)}, u32[]{:S(2)}) async-start(bf16[8,6,2304]{2,1,0:T(8,128)(2,1)} %copy.148), calls=%async_computation.3 | async-start | bytes 589824 | tf_op jit(solution)/shard_map/all_to_all | solution.py:180
  242.1 0.9 copy-start.15
  264.0 14.8 %all-to-all-start.4 = ((bf16[16,3,2304]{2,1,0:T(4,128)(2,1)}), bf16[16,3,2304]{2,1,0:T(4,128)(2,1)S(1)}, u32[]{:S(2)}, u32[]{:S(2)}) async-start(bf16[16,3,2304]{2,1,0:T(4,128)(2,1)} %reshape.324), calls=%async_computation.4 | async-start | bytes 589824 | tf_op jit(solution)/shard_map/all_to_all | solution.py:183
  278.9 1.3 copy-start.7
  278.9 1.5 copy-start.13
Sparse Core Ops, SparseCore 0:
  10.1 177.2 all-gather.1

commit v8 on v7

--- a/solution.py
+++ b/solution.py
@@ -124,10 +124,8 @@
     ).astype(jnp.bfloat16)
     repeated = jnp.repeat(normed, 2, axis=0)
     packed = jnp.dot(placing, repeated, preferred_element_type=jnp.float32).astype(jnp.bfloat16)
-    packed = packed.reshape(experts_all, 1, capacity, model_width)
-    outgoing = jnp.broadcast_to(packed, (experts_all, 2, capacity, model_width))
     arrived = lax.all_to_all(
-        outgoing.reshape(expert_devs * capacity, model_width),
+        packed.reshape(expert_devs * (capacity // 2), model_width),
         "expert",
         split_axis=0,
         concat_axis=0,
@@ -136,12 +134,11 @@
     n_zz = lax.axis_size("zz")
     n_h = lax.axis_size("h")
     n_c = lax.axis_size("c")
-    slot_total = arrived.shape[0]
+    slot_total = 2 * arrived.shape[0]
     piece = slot_total // n_zz
     half_cap = capacity // 2
     column_odd = lax.axis_index("expert") % 2
-    by_piece = arrived.reshape(n_zz, 2, capacity, model_width)
-    mine = lax.dynamic_slice_in_dim(by_piece, column_odd * half_cap, half_cap, axis=2)
+    mine = arrived.reshape(n_zz, 2, half_cap, model_width)
     sent = lax.all_to_all(
         mine.reshape(n_zz, piece // 2, model_width), "zz", split_axis=0, concat_axis=0, tiled=True
     )

time: 289 us -> 295 us (1.021)
  blocking collectives: 48.4 us -> 59.6 us
  waiting for transfers between devices: 118 us -> 114 us
    all_to_all x0 -> x1, blocking collectives: none -> 11.7 us  [on_device(): lax.all_to_all(packed.reshape(expert_devs * (capacity // 2), model_width)...]
    all_to_all x1 -> x0, waiting for transfers between devices: 9.22 us -> none  [on_device(): lax.all_to_all(outgoing.reshape(expert_devs * capacity, model_width), 'ex...]
    all_to_all x1 -> x0, starting transfers between devices: 4.84 us -> none  [on_device(): lax.all_to_all(outgoing.reshape(expert_devs * capacity, model_width), 'ex...]
    ppermute x1, waiting for transfers between devices: 21 us -> 25.7 us  [on_device(): from_h = lax.ppermute(sent, 'h', swap)]
    all_to_all x1, starting transfers between devices: 7.26 us -> 11.5 us  [on_device(): lax.all_to_all(own_slots.reshape(expert_devs, half_cap, model_width), 'ex...]
  transfers between devices with their start and end apart: 11 -> 10, of which waited for: 11 -> 10; matrix products, arithmetic and copies ran while one was open for 13% -> 12% of each run, Pallas kernels for 0% -> 0%
where the time goes in v8:
time: 295 us; the launch traced here: 294 us
  waiting for transfers between devices  114 us (39%)
  blocking collectives  59.6 us (20%)
  starting transfers between devices  43.1 us (15%)
  other arithmetic  24.9 us (8%)
  local copies, waits for them, and re-layouts  22 us (7%)
  matrix products  15.4 us (5%)
  between operations  14.6 us (5%)
    all_to_all x1, blocking collectives, on_device(): lax.all_to_all(mine.reshape(n_zz, piece // 2, model_width), 'zz', split_a...  47.9 us
    ppermute x1, waiting for transfers between devices, on_device(): from_h = lax.ppermute(sent, 'h', swap)  25.7 us
    ppermute x1, waiting for transfers between devices, on_device(): lax.ppermute(half_rows, 'expert', [(i, i ^ 1) for i in range(expert_devs)])  21.6 us
    all_to_all x1, waiting for transfers between devices, on_device(): lax.all_to_all(both_columns.reshape(n_zz, piece // 2, model_width), 'zz',...  19.9 us
    all_to_all x1, waiting for transfers between devices, on_device(): lax.all_to_all(partial_proj.reshape(expert_count, own_rows, partial_proj....  14.9 us
    all_to_all x1, blocking collectives, on_device(): lax.all_to_all(packed.reshape(expert_devs * (capacity // 2), model_width)...  11.7 us
    all_to_all x1, starting transfers between devices, on_device(): lax.all_to_all(own_slots.reshape(expert_devs, half_cap, model_width), 'ex...  11.5 us
    gather x3, other arithmetic, paged_attention(): offset = row_ids - starts[owning]  10.3 us
  transfers between devices with their start and end apart: 10, of which 10 were waited for; matrix products, arithmetic and copies ran while one was open for 12% of the time, Pallas kernels for 0%

profile of v8, /device:TPU:2, one launch (start us, length us, event | category | flops | bytes accessed | tf_op | source)
XLA Modules:
  0.0 293.7 jit_solution(17748593964976126970)
XLA Ops:
  7.3 2.2 pad_maximum_fusion.1
  9.9 1.3 gather_fusion
  12.8 0.7 gather_fusion.1
  13.6 1.8 reshape.442
  15.4 0.7 gather_fusion.2
  16.2 1.9 reshape.443
  18.3 2.6 fusion.42
  22.3 0.7 fusion.41
  23.2 4.4 %compare_select_fusion.4 = (s32[256,1]{0,1:T(1,128)S(1)}, s32[256,1]{0,1:T(1,128)S(1)}) fusion(s32[]{:T(128)} %bitcast.17, s32[]{:T(128)} %bitcast.18, s32[]{:T(128)} %bitcast.19, s32[]{:T(128)} %bitcast.20, s32[]{:T(128)} %bitcast.21, s32[]{:T(128)} %bitcast.23, s32[]{:T(128)} %bitcast.22, s32[256,1]{0,1:T(1,128)S(1)} %bitcast.106, s32[256,1]{0,1:T(1,128)S(1)} %bitcast.105), kind=kLoop, calls=%fused_computation.78 | loop fusion | flops 3584 | bytes 4124 | tf_op jit(solution)/shard_map/gather | solution.py:55
  27.6 5.8 %select_select_fusion = s32[256]{0:T(256)S(1)} fusion(pred[256]{0:T(512)(128)(4,1)S(1)} %get-tuple-element.10, pred[256]{0:T(512)(128)(4,1)S(1)} %get-tuple-element.9, pred[256]{0:T(512)(128)(4,1)S(1)} %get-tuple-element.8, pred[256]{0:T(512)(128)(4,1)S(1)} %get-tuple-element.7, pred[256]{0:T(512)(128)(4,1)S(1)} %get-tuple-element.6, ...), kind=kLoop, calls=%fused_computation.92 | loop fusion | flops 2304 | bytes 4388 | tf_op jit(solution)/shard_map/gather | solution.py:55
  33.5 1.7 gather_fusion.3
  35.1 1.5 convolution_convert_fusion.1
  36.6 9.5 %all-to-all-start = ((bf16[16,16,2304]{2,1,0:T(8,128)(2,1)}), bf16[16,16,2304]{2,1,0:T(8,128)(2,1)S(1)}, u32[]{:S(2)}, u32[]{:S(2)}) async-start(bf16[16,16,2304]{2,1,0:T(8,128)(2,1)} %bitcast.27), calls=%async_computation | async-start | bytes 2359296 | tf_op jit(solution)/shard_map/all_to_all | solution.py:97
  47.1 14.9 %all-to-all-done = bf16[16,16,2304]{2,1,0:T(8,128)(2,1)S(1)} async-done(((bf16[16,16,2304]{2,1,0:T(8,128)(2,1)}), bf16[16,16,2304]{2,1,0:T(8,128)(2,1)S(1)}, u32[]{:S(2)}, u32[]{:S(2)}) %all-to-all-start) | async-done | bytes 1179680 | tf_op jit(solution)/shard_map/all_to_all | solution.py:97
  63.4 11.7 %all_to_all.29 = bf16[16,3,2304]{2,1,0:T(4,128)(2,1)S(1)} all-to-all(bf16[16,3,2304]{2,1,0:T(4,128)(2,1)S(1)} %all_to_all.19), channel_id=1, replica_groups=mesh['zz'=8,'h'=2,'c'=2,'expert'=16] {'expert'}, dimensions={0} | all-to-all | bytes 442368 | tf_op jit(solution)/shard_map/all_to_all | solution.py:127
  75.3 47.9 %all_to_all.30 = bf16[8,6,2304]{2,1,0:T(8,128)(2,1)S(1)} all-to-all(bf16[8,6,2304]{2,1,0:T(8,128)(2,1)S(1)} %reshape_reshape.10), channel_id=1, replica_groups=mesh['zz'=8,'h'=2,'c'=2,'expert'=16] {'zz'}, dimensions={0} | all-to-all | bytes 442368 | tf_op jit(solution)/shard_map/all_to_all | solution.py:142
  123.1 2.8 collective-permute-start
  126.0 25.7 %collective-permute-done = bf16[8,6,2304]{2,1,0:T(8,128)(2,1)S(1)} collective-permute-done((bf16[8,6,2304]{2,1,0:T(8,128)(2,1)S(1)}, bf16[8,6,2304]{2,1,0:T(8,128)(2,1)S(1)}, u32[]{:S(2)}, u32[]{:S(2)}) %collective-permute-start) | collective-permute-done | bytes 221216 | tf_op jit(solution)/shard_map/ppermute | solution.py:146
  151.9 2.0 collective-permute-start.1
  154.0 1.6 collective-permute-done.1
  155.7 2.1 collective-permute-start.2
  157.8 21.6 %collective-permute-done.2 = bf16[2,2,8,2,3,2304]{5,2,4,3,1,0:T(8,128)(2,1)} collective-permute-done((bf16[2,2,8,2,3,2304]{5,2,4,3,1,0:T(8,128)(2,1)S(1)}, bf16[2,2,8,2,3,2304]{5,2,4,3,1,0:T(8,128)(2,1)}, u32[]{:S(2)}, u32[]{:S(2)}) %collective-permute-start.2) | collective-permute-done | bytes 884768 | tf_op jit(solution)/shard_map/ppermute | solution.py:150
  179.3 1.6 maximum_select_fusion
  181.4 1.6 select_n.108
  183.0 5.9 %all-gather.2.cloned.1.call-done = bf16[3,512,2304]{2,1,0:T(8,128)(2,1)} async-done(((bf16[3,64,2304]{2,1,0:T(8,128)(2,1)}), bf16[3,512,2304]{2,1,0:T(8,128)(2,1)}) %all-gather.2.cloned.1.call-update) | async-done | bytes 7077904 | tf_op jit(solution)/shard_map/all_gather | solution.py:76
  188.9 4.3 %fusion = f32[384,512]{1,0:T(8,128)} fusion(bf16[384,2304]{1,0:T(8,128)(2,1)} %select_n.108, bf16[3,512,2304]{2,1,0:T(8,128)(2,1)} %all-gather.2.cloned.1.call-done), kind=kOutput, calls=%fused_computation.11 | convolution fusion | flops 905969664 | bytes 4915200 | tf_op jit(solution)/shard_map/dot_general | solution.py:162
  193.2 6.1 %convolution_convert_fusion = bf16[384,2304]{1,0:T(8,128)(2,1)} fusion(bf16[3,512,2304]{2,1,0:T(8,128)(2,1)} %all-gather.2.cloned.1.call-done, f32[384,512]{1,0:T(8,128)} %fusion, bf16[384,2304]{1,0:T(8,128)(2,1)S(1)} %copy-done.4), kind=kOutput, calls=%fused_computation.6 | convolution fusion | flops 1814003712 | bytes 9043968 | tf_op jit(solution)/shard_map/dot_general | solution.py:166
  199.3 2.8 fusion.40
  202.3 1.2 copy.119
  203.5 1.9 collective-permute-start.3
  205.4 1.5 reshape.315
  206.9 1.2 collective-permute-done.3
  208.1 2.2 fusion.6
  210.3 0.9 copy-done.2
  211.3 5.7 %collective-permute-start.4 = (bf16[8,12,2304]{2,0,1:T(8,128)(2,1)S(1)}, bf16[8,12,2304]{2,0,1:T(8,128)(2,1)S(1)}, u32[]{:S(2)}, u32[]{:S(2)}) collective-permute-start(bf16[8,12,2304]{2,0,1:T(8,128)(2,1)S(1)} %slice_bitcast_fusion.6), channel_id=1, source_target_pairs={{0,32},{32,0},{1,33},{33,1},{2,34},{34,2},{3,35},{35,3},{4,36},{36... | collective-permute-start | bytes 1327112 | tf_op jit(solution)/shard_map/ppermute | solution.py:170
  216.9 0.7 shift-left_bitcast_fusion
  217.9 9.5 %collective-permute-done.4 = bf16[8,12,2304]{2,0,1:T(8,128)(2,1)S(1)} collective-permute-done((bf16[8,12,2304]{2,0,1:T(8,128)(2,1)S(1)}, bf16[8,12,2304]{2,0,1:T(8,128)(2,1)S(1)}, u32[]{:S(2)}, u32[]{:S(2)}) %collective-permute-start.4) | collective-permute-done | bytes 442400 | tf_op jit(solution)/shard_map/ppermute | solution.py:170
  227.4 1.1 fusion.24
  228.5 2.1 collective-permute-start.5
  230.8 6.6 %collective-permute-done.5 = bf16[8,2,3,2304]{3,0,2,1:T(8,128)(2,1)S(1)} collective-permute-done((bf16[8,2,3,2304]{3,0,2,1:T(8,128)(2,1)S(1)}, bf16[8,2,3,2304]{3,0,2,1:T(8,128)(2,1)S(1)}, u32[]{:S(2)}, u32[]{:S(2)}) %collective-permute-start.5) | collective-permute-done | bytes 221216 | tf_op jit(solution)/shard_map/ppermute | solution.py:175
  237.4 0.8 copy.121
  238.1 5.5 %all-to-all-start.3 = ((bf16[8,6,2304]{2,1,0:T(8,128)(2,1)}), bf16[8,6,2304]{2,1,0:T(8,128)(2,1)S(1)}, u32[]{:S(2)}, u32[]{:S(2)}) async-start(bf16[8,6,2304]{2,1,0:T(8,128)(2,1)} %copy.121), calls=%async_computation.3 | async-start | bytes 589824 | tf_op jit(solution)/shard_map/all_to_all | solution.py:177
  243.8 0.7 gather_fusion.5
  244.6 19.9 %all-to-all-done.3 = bf16[8,6,2304]{2,1,0:T(8,128)(2,1)S(1)} async-done(((bf16[8,6,2304]{2,1,0:T(8,128)(2,1)}), bf16[8,6,2304]{2,1,0:T(8,128)(2,1)S(1)}, u32[]{:S(2)}, u32[]{:S(2)}) %all-to-all-start.3) | async-done | bytes 221216 | tf_op jit(solution)/shard_map/all_to_all | solution.py:177
  264.6 0.9 reshape.312
  265.4 11.5 %all-to-all-start.4 = ((bf16[16,3,2304]{2,1,0:T(4,128)(2,1)}), bf16[16,3,2304]{2,1,0:T(4,128)(2,1)S(1)}, u32[]{:S(2)}, u32[]{:S(2)}) async-start(bf16[16,3,2304]{2,1,0:T(4,128)(2,1)} %reshape.312), calls=%async_computation.4 | async-start | bytes 589824 | tf_op jit(solution)/shard_map/all_to_all | solution.py:180
  277.0 7.4 %all-to-all-done.4 = bf16[16,3,2304]{2,1,0:T(4,128)(2,1)S(1)} async-done(((bf16[16,3,2304]{2,1,0:T(4,128)(2,1)}), bf16[16,3,2304]{2,1,0:T(4,128)(2,1)S(1)}, u32[]{:S(2)}, u32[]{:S(2)}) %all-to-all-start.4) | async-done | bytes 221216 | tf_op jit(solution)/shard_map/all_to_all | solution.py:180
  286.1 0.7 multiply_convert_fusion.2
  (113 shorter events, 9.7 us)
Async XLA Ops:
  7.2 5.6 %copy-start = (bf16[32,128,128]{2,1,0:T(8,128)(2,1)S(1)}, bf16[32,128,128]{2,1,0:T(8,128)(2,1)}, u32[]{:S(2)}) copy-start(bf16[32,128,128]{2,1,0:T(8,128)(2,1)} %param.17) | copy-start | bytes 3145732
  7.2 2.3 copy-start.17
  7.2 2.7 copy-start.1
  7.2 4.7 %copy-start.20 = (s32[1,32]{1,0:T(1,128)S(1)}, s32[1,32]{1,0:T(1,128)}, u32[]{:S(2)}) copy-start(s32[1,32]{1,0:T(1,128)} %param.21) | copy-start | bytes 388
  7.2 181.7 %all-gather.2.cloned.1.call-start = ((), (), s32[]{:S(2)}) async-start(), calls=%async_computation.5 | async-start | bytes 7962624 | tf_op jit(solution)/shard_map/all_gather | solution.py:76
  13.6 1.8 copy-start.5
  16.2 1.9 copy-start.16
  18.3 3.1 %copy-start.3 = (bf16[16,256,2,64]{3,2,1,0:T(2,128)(2,1)S(1)}, bf16[16,256,2,64]{3,2,1,0:T(2,128)(2,1)}, u32[]{:S(2)}) copy-start(bf16[16,256,2,64]{3,2,1,0:T(2,128)(2,1)} %reshape.443) | copy-start | bytes 3145732
  21.9 13.2 %copy-start.10 = (bf16[128,2304]{1,0:T(8,128)(2,1)S(1)}, bf16[128,2304]{1,0:T(8,128)(2,1)}, u32[]{:S(2)}) copy-start(bf16[128,2304]{1,0:T(8,128)(2,1)} %param.22) | copy-start | bytes 1769476
  35.1 11.0 %copy-start.14 = (s32[16,2]{0,1:T(2,128)S(1)}, s32[16,2]{0,1:T(2,128)}, u32[]{:S(2)}) copy-start(s32[16,2]{0,1:T(2,128)} %param.28) | copy-start | bytes 388
  36.6 25.5 %copy-start.6 = (bf16[16,2304]{1,0:T(8,128)(2,1)S(1)}, bf16[16,2304]{1,0:T(8,128)(2,1)}, u32[]{:S(2)}) copy-start(bf16[16,2304]{1,0:T(8,128)(2,1)} %param.15) | copy-start | bytes 221188
  36.6 25.7 %copy-start.12 = (f32[2304]{0:T(1024)S(1)}, f32[2304]{0:T(1024)}, u32[]{:S(2)}) copy-start(f32[2304]{0:T(1024)} %param.23) | copy-start | bytes 27652
  36.6 25.4 %all-to-all-start = ((bf16[16,16,2304]{2,1,0:T(8,128)(2,1)}), bf16[16,16,2304]{2,1,0:T(8,128)(2,1)S(1)}, u32[]{:S(2)}, u32[]{:S(2)}) async-start(bf16[16,16,2304]{2,1,0:T(8,128)(2,1)} %bitcast.27), calls=%async_computation | async-start | bytes 2359296 | tf_op jit(solution)/shard_map/all_to_all | solution.py:97
  46.6 0.5 copy-start.18
  62.4 0.6 copy-start.8
  123.1 28.5 %collective-permute-start = (bf16[8,6,2304]{2,1,0:T(8,128)(2,1)S(1)}, bf16[8,6,2304]{2,1,0:T(8,128)(2,1)S(1)}, u32[]{:S(2)}, u32[]{:S(2)}) collective-permute-start(bf16[8,6,2304]{2,1,0:T(8,128)(2,1)S(1)} %all_to_all.30), channel_id=1, source_target_pairs={{0,32},{32,0},{1,33},{33,1},{2,34},{34,2},{3,35},{35,3},{4,36},{36... | collective-permute-start | bytes 663560 | tf_op jit(solution)/shard_map/ppermute | solution.py:146
  151.9 3.7 %collective-permute-start.1 = (bf16[2,8,6,2304]{3,1,2,0:T(8,128)(2,1)S(1)}, bf16[2,8,6,2304]{3,1,2,0:T(8,128)(2,1)S(1)}, u32[]{:S(2)}, u32[]{:S(2)}) collective-permute-start(bf16[2,8,6,2304]{3,1,2,0:T(8,128)(2,1)S(1)} %copy.117), channel_id=1, source_target_pairs={{0,16},{16,0},{1,17},{17,1},{2,18},{18,2},{3,19},{19,3},{4,20},{20... | collective-permute-start | bytes 1327112 | tf_op jit(solution)/shard_map/ppermute | solution.py:148
  155.7 23.7 %collective-permute-start.2 = (bf16[2,2,8,2,3,2304]{5,2,4,3,1,0:T(8,128)(2,1)S(1)}, bf16[2,2,8,2,3,2304]{5,2,4,3,1,0:T(8,128)(2,1)}, u32[]{:S(2)}, u32[]{:S(2)}) collective-permute-start(bf16[2,2,8,2,3,2304]{5,2,4,3,1,0:T(8,128)(2,1)S(1)} %pad_maximum_fusion), channel_id=1, source_target_pairs={{0,1},{1,0},{2,3},{3,2},{4,5},{5,4},{6,7},{7,6},{8,9},{9,8},{10,11... | collective-permute-start | bytes 2654216 | tf_op jit(solution)/shard_map/ppermute | solution.py:150
  183.0 10.2 %copy-start.4 = (bf16[384,2304]{1,0:T(8,128)(2,1)S(1)}, bf16[384,2304]{1,0:T(8,128)(2,1)}, u32[]{:S(2)}) copy-start(bf16[384,2304]{1,0:T(8,128)(2,1)} %select_n.108) | copy-start | bytes 5308420
  203.5 4.7 %collective-permute-start.3 = (bf16[2,8,12,2304]{3,1,2,0:T(8,128)(2,1)}, bf16[2,8,12,2304]{3,1,2,0:T(8,128)(2,1)}, u32[]{:S(2)}, u32[]{:S(2)}) collective-permute-start(bf16[2,8,12,2304]{3,1,2,0:T(8,128)(2,1)} %copy.119), channel_id=1, source_target_pairs={{0,16},{16,0},{1,17},{17,1},{2,18},{18,2},{3,19},{19,3},{4,20},{20... | collective-permute-start | bytes 2654216 | tf_op jit(solution)/shard_map/ppermute | solution.py:168
  210.3 0.9 copy-start.2
  211.3 16.1 %collective-permute-start.4 = (bf16[8,12,2304]{2,0,1:T(8,128)(2,1)S(1)}, bf16[8,12,2304]{2,0,1:T(8,128)(2,1)S(1)}, u32[]{:S(2)}, u32[]{:S(2)}) collective-permute-start(bf16[8,12,2304]{2,0,1:T(8,128)(2,1)S(1)} %slice_bitcast_fusion.6), channel_id=1, source_target_pairs={{0,32},{32,0},{1,33},{33,1},{2,34},{34,2},{3,35},{35,3},{4,36},{36... | collective-permute-start | bytes 1327112 | tf_op jit(solution)/shard_map/ppermute | solution.py:170
  217.9 25.7 %copy-start.19 = (s32[32]{0:T(128)S(1)}, s32[32]{0:T(128)}, u32[]{:S(2)}) copy-start(s32[32]{0:T(128)} %copy-done.18) | copy-start | bytes 388
  217.9 25.7 %copy-start.9 = (bf16[16,2304]{1,0:T(8,128)(2,1)S(1)}, bf16[16,2304]{1,0:T(8,128)(2,1)}, u32[]{:S(2)}) copy-start(bf16[16,2304]{1,0:T(8,128)(2,1)} %copy-done.8) | copy-start | bytes 221188
  217.9 25.8 %copy-start.11 = (bf16[2304,8]{0,1:T(8,128)(2,1)S(1)}, bf16[2304,8]{0,1:T(8,128)(2,1)}, u32[]{:S(2)}) copy-start(bf16[2304,8]{0,1:T(8,128)(2,1)} %param.24) | copy-start | bytes 110596
  228.5 8.8 %collective-permute-start.5 = (bf16[8,2,3,2304]{3,0,2,1:T(8,128)(2,1)S(1)}, bf16[8,2,3,2304]{3,0,2,1:T(8,128)(2,1)S(1)}, u32[]{:S(2)}, u32[]{:S(2)}) collective-permute-start(bf16[8,2,3,2304]{3,0,2,1:T(8,128)(2,1)S(1)} %dynamic-slice_bitcast_fusion), channel_id=1, source_target_pairs={{0,1},{1,0},{2,3},{3,2},{4,5},{5,4},{6,7},{7,6},{8,9},{9,8},{10,11... | collective-permute-start | bytes 663560 | tf_op jit(solution)/shard_map/ppermute | solution.py:175
  238.1 26.4 %all-to-all-start.3 = ((bf16[8,6,2304]{2,1,0:T(8,128)(2,1)}), bf16[8,6,2304]{2,1,0:T(8,128)(2,1)S(1)}, u32[]{:S(2)}, u32[]{:S(2)}) async-start(bf16[8,6,2304]{2,1,0:T(8,128)(2,1)} %copy.121), calls=%async_computation.3 | async-start | bytes 589824 | tf_op jit(solution)/shard_map/all_to_all | solution.py:177
  243.8 0.9 copy-start.15
  265.4 19.0 %all-to-all-start.4 = ((bf16[16,3,2304]{2,1,0:T(4,128)(2,1)}), bf16[16,3,2304]{2,1,0:T(4,128)(2,1)S(1)}, u32[]{:S(2)}, u32[]{:S(2)}) async-start(bf16[16,3,2304]{2,1,0:T(4,128)(2,1)} %reshape.312), calls=%async_computation.4 | async-start | bytes 589824 | tf_op jit(solution)/shard_map/all_to_all | solution.py:180
  284.6 1.3 copy-start.7
  284.6 1.5 copy-start.13
Sparse Core Ops, SparseCore 0:
  10.1 178.7 all-gather.1
